TPU v7x, 512 devices: a whole 4x4x16 slice. The times are simulated.
512 devices in a mesh: sec: 2 (over core), seq: 32 (over z, y_lo), rep: 8 (over x, y_hi).
Axes of the slice: x: 4, y: 4 (y_hi: 2, y_lo: 2; y = y_hi * 2 + y_lo), z: 16, core: 2. Of those that a mesh axis runs over, the one named last changes fastest.
Arguments:
- head_query: bfloat16 [64, 24, 1536, 128], P(('sec', 'rep'), None, 'seq'), may hold values from -4.5 to 4.5
- head_keys: bfloat16 [64, 24, 1536, 128], P(('sec', 'rep'), None, 'seq'), may hold values from -4.5 to 4.5
- head_values: bfloat16 [64, 24, 1536, 128], P(('sec', 'rep'), None, 'seq'), may hold values from -6 to 6
- mod_shift: float32 [64, 3072], P(('sec', 'rep')), may hold values from -3 to 3
- mod_scale: float32 [64, 3072], P(('sec', 'rep')), may hold values from -0.9 to 0.9
- final_weight: bfloat16 [3072, 64], replicated, may hold values from -0.109375 to 0.109375
- final_bias: float32 [64], replicated, may hold values from -3 to 3
- noisy_latent: float32 [64, 3, 64, 512], P(('sec', 'rep'), None, 'seq'), may hold values from -7.2 to 7.2
- step_index: int32 [64], P(('sec', 'rep')), may hold values from 46 to 49
- clip_order: int32 [64], replicated, may hold values from 0 to 63, each once
- conv_weight: bfloat16 [3, 3, 3, 16, 512], replicated, may hold values from -0.3125 to 0.3125
- conv_bias: float32 [512], replicated, may hold values from -3 to 3
- group_gain: float32 [512], replicated, may hold values from 0.1 to 1.9
- group_shift: float32 [512], replicated, may hold values from -3 to 3
Outputs:
- denoised: float32 [64, 3, 64, 512], P(('sec', 'rep'), None, 'seq')
- features: bfloat16 [64, 3, 64, 16384], P(('sec', 'rep'), None, 'seq')
All inputs are finite; a program needn't handle non-finite values.
Results may differ from a plain program's by a relative error of at most 0.005.
Values may be sent and summed in bfloat16 or wider, within the bound.
No kernel may reach another device: no remote copies, remote signals or barrier semaphores. Data moves between devices by JAX's collectives and lax.ppermute only.
A program may use at most 128 MiB of HBM per device.

v0:
```python
import math

import jax
import jax.numpy as jnp
from jax import lax
from jax.sharding import PartitionSpec as P

HEADS = 24
HEAD_DIM = 128
LAT_CH = 16
VAE_CH = 512
GROUPS = 32
FRAMES = 3
PATCH_W = 16
NSTEPS = 50
PATCH_OUT = 64
LAT_W = 32


eps_norm = 1e-06
shift_factor = 7.0


def extended(cells, sides, width):
    for axis, dim in sides:
        count = lax.axis_size(axis)
        ends = count - 1
        head = lax.slice_in_dim(cells, 0, width, axis=dim)
        tail = lax.slice_in_dim(cells, cells.shape[dim] - width, cells.shape[dim], axis=dim)
        cells = jnp.concatenate(
            [
                lax.ppermute(tail, axis, [(i, (i + 1) % count) for i in range(ends)]),
                cells,
                lax.ppermute(head, axis, [((i + 1) % count, i) for i in range(ends)]),
            ],
            axis=dim,
        )
    return cells


def attend_unit(operands):
    query_rows, key_rows, value_rows = operands
    length = query_rows.shape[0]
    block = math.gcd(length, 512)
    scale = 1.0 / math.sqrt(query_rows.shape[1])
    blocks = query_rows.reshape(length // block, block, query_rows.shape[1])

    def one_block(rows):
        scores = jnp.dot(rows, key_rows.T, preferred_element_type=jnp.float32) * scale
        top = jnp.max(scores, axis=1, keepdims=True)
        expd = jnp.exp(scores - top)
        weights = (expd / jnp.sum(expd, axis=1, keepdims=True)).astype(jnp.bfloat16)
        return jnp.dot(weights, value_rows, preferred_element_type=jnp.float32).astype(jnp.bfloat16)

    return lax.map(one_block, blocks).reshape(length, query_rows.shape[1])


def sigma_level(index):
    level = 1.0 - index.astype(jnp.float32) / NSTEPS
    return shift_factor * level / (1.0 + (shift_factor - 1.0) * level)


def causal_columns(rimmed):
    clips, frames, rows_rim, wide = rimmed.shape
    width = wide // LAT_CH
    grid = rimmed.reshape(clips, frames, rows_rim, width, LAT_CH)
    first = grid[:, :1]
    grid = jnp.concatenate([first, first, grid], axis=1)
    grid = jnp.pad(grid, ((0, 0), (0, 0), (0, 0), (1, 1), (0, 0)), mode="edge")
    taps = []
    for tap_time in range(3):
        for tap_row in range(3):
            for tap_col in range(3):
                taps.append(
                    grid[
                        :,
                        tap_time : tap_time + frames,
                        tap_row : tap_row + rows_rim - 2,
                        tap_col : tap_col + width,
                        :,
                    ]
                )
    return jnp.stack(taps, axis=4).reshape(clips, frames, rows_rim - 2, width, 27 * LAT_CH)


def edge_rows(rimmed):
    position = lax.axis_index("seq")
    last_index = lax.axis_size("seq") - 1
    upper = jnp.where(position == 0, rimmed[:, :, 1:2], rimmed[:, :, 0:1])
    lower = jnp.where(position == last_index, rimmed[:, :, -2:-1], rimmed[:, :, -1:])
    return jnp.concatenate([upper, rimmed[:, :, 1:-1], lower], axis=2)


def shards(
    head_query,
    head_keys,
    head_values,
    mod_shift,
    mod_scale,
    final_weight,
    final_bias,
    noisy_latent,
    step_index,
    clip_order,
    conv_weight,
    conv_bias,
    group_gain,
    group_shift,
):
    n_seq = lax.axis_size("seq")
    clips = head_query.shape[0]
    tok_dev = head_query.shape[2]
    units_local = clips * HEADS // n_seq
    query_four = head_query.reshape(n_seq, units_local, tok_dev, HEAD_DIM)
    keys_four = head_keys.reshape(n_seq, units_local, tok_dev, HEAD_DIM)
    values_four = head_values.reshape(n_seq, units_local, tok_dev, HEAD_DIM)
    query_part = lax.all_to_all(query_four, "seq", split_axis=0, concat_axis=2, tiled=True)
    keys_part = lax.all_to_all(keys_four, "seq", split_axis=0, concat_axis=2, tiled=True)
    values_part = lax.all_to_all(values_four, "seq", split_axis=0, concat_axis=2, tiled=True)
    outputs = lax.map(attend_unit, (query_part[0], keys_part[0], values_part[0]))[None]
    mixed = lax.all_to_all(outputs, "seq", split_axis=2, concat_axis=0, tiled=True)
    weights3 = final_weight.astype(jnp.float32).reshape(HEADS, HEAD_DIM, PATCH_OUT)
    scale3 = mod_scale.reshape(clips, HEADS, HEAD_DIM)
    shift3 = mod_shift.reshape(clips, HEADS, HEAD_DIM)
    heads = mixed.reshape(clips, HEADS, tok_dev, HEAD_DIM).astype(jnp.float32)
    mean = jnp.mean(heads, axis=(1, 3), keepdims=True)
    spread = jnp.mean(jnp.square(heads - mean), axis=(1, 3), keepdims=True)
    normed = (heads - mean) * lax.rsqrt(spread + eps_norm)
    modulated = normed * (1.0 + scale3[:, :, None, :]) + shift3[:, :, None, :]
    velocity = (
        jnp.einsum("chtd,hdo->cto", modulated, weights3, precision=lax.Precision.HIGHEST)
        + final_bias
    )
    rows_dev = noisy_latent.shape[2]
    velocity = velocity.reshape(clips, rows_dev // 2, FRAMES, PATCH_W, 2, 2, LAT_CH)
    velocity = jnp.transpose(velocity, (0, 2, 1, 4, 3, 5, 6)).reshape(noisy_latent.shape)
    step = sigma_level(step_index + 1) - sigma_level(step_index)
    denoised = noisy_latent + step[:, None, None, None] * velocity
    decoder_in = denoised.astype(jnp.bfloat16)
    group_index = lax.axis_index(("sec", "rep"))
    wanted = lax.dynamic_slice_in_dim(clip_order, group_index * clips, clips)
    everyone = lax.all_gather(decoder_in, ("sec", "rep"), axis=0, tiled=True)
    picked = jnp.take(everyone, wanted, axis=0)
    rimmed = edge_rows(extended(picked, (("seq", 2),), 1))
    columns = causal_columns(rimmed)
    flat_weight = conv_weight.reshape(27 * LAT_CH, VAE_CH)
    conv_out = (
        jnp.dot(columns.reshape(-1, 27 * LAT_CH), flat_weight, preferred_element_type=jnp.float32)
        + conv_bias
    )
    conv_out = conv_out.reshape(clips, -1, GROUPS, VAE_CH // GROUPS)
    cells = conv_out.shape[1] * n_seq * (VAE_CH // GROUPS)
    local_sum = jnp.sum(conv_out, axis=(1, 3))
    mean = lax.psum(local_sum, "seq") / cells
    centered = conv_out - mean[:, None, :, None]
    spread = lax.psum(jnp.sum(jnp.square(centered), axis=(1, 3)), "seq") / cells
    normed = (centered * lax.rsqrt(spread + eps_norm)[:, None, :, None]).reshape(clips, -1, VAE_CH)
    features = jax.nn.silu(normed * group_gain + group_shift).astype(jnp.bfloat16)
    features = features.reshape(clips, FRAMES, rows_dev, LAT_W * VAE_CH)
    return (denoised, features)


def solution(mesh):
    placed = (
        P(("sec", "rep"), None, "seq", None),
        P(("sec", "rep"), None, "seq", None),
        P(("sec", "rep"), None, "seq", None),
        P(("sec", "rep"), None),
        P(("sec", "rep"), None),
        P(),
        P(),
        P(("sec", "rep"), None, "seq", None),
        P(("sec", "rep")),
        P(),
        P(),
        P(),
        P(),
        P(),
    )
    return jax.shard_map(
        shards,
        mesh=mesh,
        in_specs=placed,
        out_specs=(P(("sec", "rep"), None, "seq", None), P(("sec", "rep"), None, "seq", None)),
        check_vma=False,
    )
```

profile of v0, /device:TPU:14, one launch (start us, length us, event | category | flops | bytes accessed | tf_op | source)
XLA Modules:
  0.0 569.2 jit_solution(6883211467850710125)
XLA Ops:
  0.7 77.9 %all_to_all.54 = bf16[32,3,48,128]{3,2,1,0:T(8,128)(2,1)} all-to-all(bf16[32,3,48,128]{3,2,1,0:T(8,128)(2,1)} %bitcast.227), channel_id=1, replica_groups=mesh['sec'=2,'seq'=32,'rep'=8] {'seq'}, dimensions={0} | all-to-all | bytes 2359296 | tf_op jit(solution)/shard_map/all_to_all | solution.py:117
  78.5 64.2 %all_to_all.55 = bf16[32,3,48,128]{3,2,1,0:T(8,128)(2,1)} all-to-all(bf16[32,3,48,128]{3,2,1,0:T(8,128)(2,1)S(1)} %bitcast.228), channel_id=1, replica_groups=mesh['sec'=2,'seq'=32,'rep'=8] {'seq'}, dimensions={0} | all-to-all | bytes 2359296 | tf_op jit(solution)/shard_map/all_to_all | solution.py:118
  142.7 4.2 all-to-all-start.2
  146.9 1.4 copy.116
  148.5 1.1 copy.117
  149.6 55.0 %all-to-all-done.2 = bf16[32,3,48,128]{3,2,1,0:T(8,128)(2,1)S(1)} async-done(((bf16[32,3,48,128]{3,2,1,0:T(8,128)(2,1)}), bf16[32,3,48,128]{3,2,1,0:T(8,128)(2,1)S(1)}, u32[]{:S(2)}, u32[]{:S(2)}) %all-to-all-start.2) | async-done | bytes 1179680 | tf_op jit(solution)/shard_map/all_to_all | solution.py:119
  204.6 1.1 copy.118
  205.8 24.2 %while.21 = (s32[]{:T(128)}, bf16[3,1536,128]{2,1,0:T(8,128)(2,1)}, bf16[3,1536,128]{2,1,0:T(8,128)(2,1)S(1)}, bf16[3,1536,128]{2,1,0:T(8,128)(2,1)}, bf16[3,153...) while((s32[]{:T(128)}, bf16[3,1536,128]{2,1,0:T(8,128)(2,1)}, ...), condition=%wide.region_5.6_spmd, body=%wide.region_0.5_spmd.sunk | while | flops 408222720 | bytes 13641974 | solution.py:120
  205.8 1.2 dynamic-slice_bitcast_fusion.3
  207.0 6.1 %while.22 = (s32[]{:T(128)}, bf16[3,512,128]{2,1,0:T(8,128)(2,1)S(1)}, bf16[3,512,128]{2,1,0:T(8,128)(2,1)S(1)}, bf16[1536,128]{1,0:T(8,128)(2,1)S(1)}, bf16[1536,128]{1,0:T(8,128)(2,1)S(1)}, /*index=5*/s32[]{:T(128)}) while((s32[]{:T(128)}, bf16[3,512,128]{2,1,0:T(8,128)(2,1)S(1)}, bf16[3,512,128]{2,1,0:T(8,128)(2,1)S(1)}, ...), condition=%wide.region_4.4_spmd, body=%wide.region_1.3_spmd.sunk | while | flops 408222720 | bytes 10496085 | solution.py:55
  208.2 0.8 fusion.89
  210.2 0.8 fusion.89
  212.2 0.8 fusion.89
  213.0 0.8 bitcast_dynamic-update-slice_fusion.2
  213.8 1.2 dynamic-slice_bitcast_fusion.3
  215.0 6.1 %while.22 = (s32[]{:T(128)}, bf16[3,512,128]{2,1,0:T(8,128)(2,1)S(1)}, bf16[3,512,128]{2,1,0:T(8,128)(2,1)S(1)}, bf16[1536,128]{1,0:T(8,128)(2,1)S(1)}, bf16[1536,128]{1,0:T(8,128)(2,1)S(1)}, /*index=5*/s32[]{:T(128)}) while((s32[]{:T(128)}, bf16[3,512,128]{2,1,0:T(8,128)(2,1)S(1)}, bf16[3,512,128]{2,1,0:T(8,128)(2,1)S(1)}, ...), condition=%wide.region_4.4_spmd, body=%wide.region_1.3_spmd.sunk | while | flops 408222720 | bytes 10496085 | solution.py:55
  216.2 0.8 fusion.89
  218.3 0.8 fusion.89
  220.3 0.8 fusion.89
  221.1 0.8 bitcast_dynamic-update-slice_fusion.2
  221.9 1.2 dynamic-slice_bitcast_fusion.3
  223.1 6.1 %while.22 = (s32[]{:T(128)}, bf16[3,512,128]{2,1,0:T(8,128)(2,1)S(1)}, bf16[3,512,128]{2,1,0:T(8,128)(2,1)S(1)}, bf16[1536,128]{1,0:T(8,128)(2,1)S(1)}, bf16[1536,128]{1,0:T(8,128)(2,1)S(1)}, /*index=5*/s32[]{:T(128)}) while((s32[]{:T(128)}, bf16[3,512,128]{2,1,0:T(8,128)(2,1)S(1)}, bf16[3,512,128]{2,1,0:T(8,128)(2,1)S(1)}, ...), condition=%wide.region_4.4_spmd, body=%wide.region_1.3_spmd.sunk | while | flops 408222720 | bytes 10496085 | solution.py:55
  224.3 0.8 fusion.89
  226.3 0.8 fusion.89
  228.3 0.8 fusion.89
  229.1 0.8 bitcast_dynamic-update-slice_fusion.2
  229.9 8.1 %copy.141 = bf16[3,1536,128]{2,0,1:T(4,128)(2,1)} copy(bf16[3,1536,128]{2,1,0:T(8,128)(2,1)} %get-tuple-element.56) | data formatting | bytes 2359296 | tf_op jit(solution)/shard_map/while | solution.py:120
  238.1 5.7 all-to-all-start.3
  243.9 76.1 %all-to-all-done.3 = bf16[1,3,1536,128]{3,1,0,2:T(4,128)(2,1)S(1)} async-done(((bf16[1,3,1536,128]{3,1,0,2:T(4,128)(2,1)}), bf16[1,3,1536,128]{3,1,0,2:T(4,128)(2,1)S(1)}, u32[]{:S(2)}, u32[]{:S(2)}) %all-to-all-start.3) | async-done | bytes 1179680 | tf_op jit(solution)/shard_map/all_to_all | solution.py:121
  320.4 3.1 fusion.19
  323.7 22.0 %multiply_reduce_fusion = f32[32,48]{1,0:T(8,128)S(1)} fusion(bf16[1,3,32,48,128]{4,1,3,2,0:T(4,128)(2,1)S(1)} %bitcast.219, f32[32,48]{1,0:T(8,128)S(1)} %broadcast_bitcast_fusion.2), kind=kLoop, calls=%fused_computation.17 | loop fusion | flops 2357760 | bytes 1191936 | tf_op jit(solution)/shard_map/reduce_sum | solution.py:127
  345.8 1.6 fusion.28
  348.4 0.7 fusion.72
  349.2 37.0 %all_gather.3 = bf16[64,3,2,512]{3,2,1,0:T(2,128)(2,1)S(1)} all-gather(bf16[4,3,2,512]{3,2,1,0:T(2,128)(2,1)S(1)} %get-tuple-element.79), channel_id=1, replica_groups=mesh['sec'=2,'seq'=32,'rep'=8] {'sec','rep'}, dimensions={0}, use_global_device_ids=true | all-gather | bytes 417792 | tf_op jit(solution)/shard_map/all_gather | solution.py:142
  386.9 2.7 collective-permute-start
  389.6 3.4 collective-permute-start.1
  393.1 3.1 collective-permute-done.1
  398.5 0.7 fusion.69
  400.0 0.7 fusion.67
  400.7 0.7 fusion.66
  402.1 0.7 fusion.40
  402.8 0.7 fusion.64
  404.2 0.7 fusion.48
  404.9 0.7 fusion.62
  406.4 0.7 fusion.45
  407.1 0.7 fusion.60
  407.8 0.7 fusion.59
  408.5 0.7 fusion.42
  409.3 0.7 fusion.58
  411.4 0.7 fusion.55
  413.5 0.7 fusion.52
  415.6 0.7 fusion.49
  416.3 7.9 %copy.123 = bf16[4,3,2,32,27,16]{3,2,1,0,5,4:T(2,128)(2,1)S(1)} copy(bf16[4,3,2,32,27,16]{5,3,2,1,0,4:T(8,128)(2,1)} %fusion.49) | data formatting | bytes 1327104 | tf_op jit(solution)/shard_map/stack | solution.py:83
  424.3 2.5 reshape_reshape.3
  426.8 1.7 convolution_add_fusion
  428.5 1.6 copy.124
  430.1 2.5 reshape.109
  432.6 2.7 reshape.110
  435.8 60.3 %psum.14 = f32[4,32]{1,0:T(4,128)S(1)} all-reduce(f32[4,32]{1,0:T(4,128)S(1)} %copy.125), channel_id=1, replica_groups=mesh['sec'=2,'seq'=32,'rep'=8] {'seq'}, use_global_device_ids=true, to_apply=%region_11.12 | all-reduce | flops 128 | bytes 1024 | tf_op jit(solution)/shard_map/psum | solution.py:154
  496.2 0.8 multiply_reduce_fusion.1
  497.0 61.9 %psum.15 = f32[4,32]{1,0:T(4,128)S(1)} all-reduce(f32[4,32]{1,0:T(4,128)S(1)} %copy.127), channel_id=1, replica_groups=mesh['sec'=2,'seq'=32,'rep'=8] {'seq'}, use_global_device_ids=true, to_apply=%region_13.14 | all-reduce | flops 128 | bytes 1024 | tf_op jit(solution)/shard_map/psum | solution.py:156
  559.3 2.5 mul.94
  562.2 2.5 sub.70
  564.7 4.5 fusion.20
  (104 shorter events, 24.5 us)
Async XLA Ops:
  0.6 426.1 %copy-start = (bf16[3,3,3,16,512]{4,3,2,1,0:T(8,128)(2,1)S(1)}, bf16[3,3,3,16,512]{4,3,2,1,0:T(8,128)(2,1)}, u32[]{:S(2)}) copy-start(bf16[3,3,3,16,512]{4,3,2,1,0:T(8,128)(2,1)} %param.28) | copy-start | bytes 1327108
  0.6 77.9 %copy-start.2 = (bf16[4,24,48,128]{3,2,1,0:T(8,128)(2,1)S(1)}, bf16[4,24,48,128]{3,2,1,0:T(8,128)(2,1)}, u32[]{:S(2)}) copy-start(bf16[4,24,48,128]{3,2,1,0:T(8,128)(2,1)} %param.19) | copy-start | bytes 3538948
  142.7 61.9 %all-to-all-start.2 = ((bf16[32,3,48,128]{3,2,1,0:T(8,128)(2,1)}), bf16[32,3,48,128]{3,2,1,0:T(8,128)(2,1)S(1)}, u32[]{:S(2)}, u32[]{:S(2)}) async-start(bf16[32,3,48,128]{3,2,1,0:T(8,128)(2,1)} %bitcast.14), calls=%async_computation.2 | async-start | bytes 2359296 | tf_op jit(solution)/shard_map/all_to_all | solution.py:119
  146.9 1.6 copy-start.1
  229.9 13.8 %copy-start.8 = (s32[64]{0:T(128)S(1)}, s32[64]{0:T(128)}, u32[]{:S(2)}) copy-start(s32[64]{0:T(128)} %param.27) | copy-start | bytes 772
  229.9 13.9 %copy-start.11 = (s32[4]{0:T(128)S(1)}, s32[4]{0:T(128)}, u32[]{:S(2)}) copy-start(s32[4]{0:T(128)} %param.26) | copy-start | bytes 52
  229.9 13.9 %copy-start.6 = (f32[512]{0:T(512)S(1)}, f32[512]{0:T(512)}, u32[]{:S(2)}) copy-start(f32[512]{0:T(512)} %param.31) | copy-start | bytes 6148
  229.9 14.0 %copy-start.3 = (f32[4,3072]{1,0:T(4,128)S(1)}, f32[4,3072]{1,0:T(4,128)}, u32[]{:S(2)}) copy-start(f32[4,3072]{1,0:T(4,128)} %param.22) | copy-start | bytes 147460
  229.9 14.0 %copy-start.4 = (f32[4,3072]{1,0:T(4,128)S(1)}, f32[4,3072]{1,0:T(4,128)}, u32[]{:S(2)}) copy-start(f32[4,3072]{1,0:T(4,128)} %param.21) | copy-start | bytes 147460
  238.1 82.0 %all-to-all-start.3 = ((bf16[1,3,1536,128]{3,1,0,2:T(4,128)(2,1)}), bf16[1,3,1536,128]{3,1,0,2:T(4,128)(2,1)S(1)}, u32[]{:S(2)}, u32[]{:S(2)}) async-start(bf16[1,3,1536,128]{3,1,0,2:T(4,128)(2,1)} %bitcast.224), calls=%async_computation.3 | async-start | bytes 3145728 | tf_op jit(solution)/shard_map/all_to_all | solution.py:121
  323.5 22.3 %copy-start.9 = (bf16[3072,64]{0,1:T(8,128)(2,1)S(1)}, bf16[3072,64]{0,1:T(8,128)(2,1)}, u32[]{:S(2)}) copy-start(bf16[3072,64]{0,1:T(8,128)(2,1)} %param.23) | copy-start | bytes 1179652
  323.5 22.3 %copy-start.12 = (f32[64]{0:T(128)S(1)}, f32[64]{0:T(128)}, u32[]{:S(2)}) copy-start(f32[64]{0:T(128)} %param.24) | copy-start | bytes 772
  323.7 24.7 %copy-start.5 = (f32[4,3,2,512]{3,2,1,0:T(2,128)S(1)}, f32[4,3,2,512]{3,2,1,0:T(2,128)}, u32[]{:S(2)}) copy-start(f32[4,3,2,512]{3,2,1,0:T(2,128)} %param.25) | copy-start | bytes 147460
  345.8 47.2 %copy-start.7 = (f32[512]{0:T(512)S(1)}, f32[512]{0:T(512)}, u32[]{:S(2)}) copy-start(f32[512]{0:T(512)} %param.30) | copy-start | bytes 6148
  386.9 6.2 %collective-permute-start = (bf16[4,3,1,512]{3,2,1,0:T(2,128)(2,1)S(1)}, bf16[4,3,1,512]{3,2,1,0:T(2,128)(2,1)S(1)}, u32[]{:S(2)}, u32[]{:S(2)}) collective-permute-start(bf16[4,3,1,512]{3,2,1,0:T(2,128)(2,1)S(1)} %get-tuple-element.89), channel_id=1, source_target_pairs={{0,8},{8,16},{16,24},{24,32},{32,40},{40,48},{48,56},{56,64},{64,7... | collective-permute-start | bytes 36872 | tf_op jit(solution)/shard_map/ppermute | solution.py:32
  389.6 6.6 %collective-permute-start.1 = (bf16[4,3,1,512]{3,2,1,0:T(2,128)(2,1)S(1)}, bf16[4,3,1,512]{3,2,1,0:T(2,128)(2,1)S(1)}, u32[]{:S(2)}, u32[]{:S(2)}) collective-permute-start(bf16[4,3,1,512]{3,2,1,0:T(2,128)(2,1)S(1)} %get-tuple-element.90), channel_id=1, source_target_pairs={{8,0},{16,8},{24,16},{32,24},{40,32},{48,40},{56,48},{64,56},{72,6... | collective-permute-start | bytes 36872 | tf_op jit(solution)/shard_map/ppermute | solution.py:34
  424.3 2.5 copy-start.10
where the time goes:
time: 570 us; the launch traced here: 569 us
  blocking collectives  301 us (53%)
  waiting for transfers between devices  134 us (24%)
  local copies, waits for them, and re-layouts  58.9 us (10%)
  other arithmetic  41.5 us (7%)
  matrix products  16.1 us (3%)
  starting transfers between devices  15.9 us (3%)
    all_to_all x1, blocking collectives, shards(): lax.all_to_all(query_four, 'seq', split_axis=0, concat_axis=2, tiled=True)  77.9 us
    all_to_all x1, waiting for transfers between devices, shards(): lax.all_to_all(outputs, 'seq', split_axis=2, concat_axis=0, tiled=True)  76.1 us
    all_to_all x1, blocking collectives, shards(): lax.all_to_all(keys_four, 'seq', split_axis=0, concat_axis=2, tiled=True)  64.2 us
    psum x1, blocking collectives, shards(): spread = lax.psum(jnp.sum(jnp.square(centered), axis=(1, 3)), 'seq') / cells  61.9 us
    psum x1, blocking collectives, shards(): mean = lax.psum(local_sum, 'seq') / cells  60.3 us
    all_to_all x1, waiting for transfers between devices, shards(): lax.all_to_all(values_four, 'seq', split_axis=0, concat_axis=2, tiled=True)  55 us
    all_gather x1, blocking collectives, shards(): everyone = lax.all_gather(decoder_in, ('sec', 'rep'), axis=0, tiled=True)  37 us
    reduce_sum x2, other arithmetic, shards(): spread = jnp.mean(jnp.square(heads - mean), axis=(1, 3), keepdims=True)  22 us
  transfers between devices with their start and end apart: 4, of which 3 were waited for; matrix products, arithmetic and copies ran while one was open for 0% of the time, Pallas kernels for 0%

commit v1 on v0

--- a/solution.py
+++ b/solution.py
@@ -36,6 +36,36 @@
             axis=dim,
         )
     return cells
+
+
+def butterfly_gather(block, axis):
+    count = lax.axis_size(axis)
+    me = lax.axis_index(axis)
+    held = block[None]
+    step = 1
+    while step < count:
+        other = lax.ppermute(held, axis, [(i, i ^ step) for i in range(count)])
+        low = (me // step) % 2 == 0
+        held = jnp.where(
+            low,
+            jnp.concatenate([held, other], axis=0),
+            jnp.concatenate([other, held], axis=0),
+        )
+        step *= 2
+    return held.reshape((count * block.shape[0],) + block.shape[1:])
+
+
+def butterfly_moments(mean, m2, count, axis):
+    size = lax.axis_size(axis)
+    step = 1
+    while step < size:
+        pair = lax.ppermute(jnp.stack([mean, m2]), axis, [(i, i ^ step) for i in range(size)])
+        other_mean, other_m2 = pair[0], pair[1]
+        gap = mean - other_mean
+        m2 = (m2 + other_m2) + jnp.square(gap) * (0.5 * count * step)
+        mean = (mean + other_mean) * 0.5
+        step *= 2
+    return mean, m2
 
 
 def attend_unit(operands):
@@ -111,24 +141,30 @@
     clips = head_query.shape[0]
     tok_dev = head_query.shape[2]
     units_local = clips * HEADS // n_seq
-    query_four = head_query.reshape(n_seq, units_local, tok_dev, HEAD_DIM)
-    keys_four = head_keys.reshape(n_seq, units_local, tok_dev, HEAD_DIM)
-    values_four = head_values.reshape(n_seq, units_local, tok_dev, HEAD_DIM)
-    query_part = lax.all_to_all(query_four, "seq", split_axis=0, concat_axis=2, tiled=True)
-    keys_part = lax.all_to_all(keys_four, "seq", split_axis=0, concat_axis=2, tiled=True)
-    values_part = lax.all_to_all(values_four, "seq", split_axis=0, concat_axis=2, tiled=True)
-    outputs = lax.map(attend_unit, (query_part[0], keys_part[0], values_part[0]))[None]
+    stacked = jnp.stack(
+        [
+            head_query.reshape(n_seq, units_local, tok_dev, HEAD_DIM),
+            head_keys.reshape(n_seq, units_local, tok_dev, HEAD_DIM),
+            head_values.reshape(n_seq, units_local, tok_dev, HEAD_DIM),
+        ],
+        axis=1,
+    )
+    parts = lax.all_to_all(stacked, "seq", split_axis=0, concat_axis=3, tiled=True)
+    outputs = lax.map(attend_unit, (parts[0, 0], parts[0, 1], parts[0, 2]))[None]
     mixed = lax.all_to_all(outputs, "seq", split_axis=2, concat_axis=0, tiled=True)
-    weights3 = final_weight.astype(jnp.float32).reshape(HEADS, HEAD_DIM, PATCH_OUT)
-    scale3 = mod_scale.reshape(clips, HEADS, HEAD_DIM)
-    shift3 = mod_shift.reshape(clips, HEADS, HEAD_DIM)
     heads = mixed.reshape(clips, HEADS, tok_dev, HEAD_DIM).astype(jnp.float32)
-    mean = jnp.mean(heads, axis=(1, 3), keepdims=True)
-    spread = jnp.mean(jnp.square(heads - mean), axis=(1, 3), keepdims=True)
-    normed = (heads - mean) * lax.rsqrt(spread + eps_norm)
-    modulated = normed * (1.0 + scale3[:, :, None, :]) + shift3[:, :, None, :]
+    tokens = jnp.transpose(heads, (0, 2, 1, 3)).reshape(clips, tok_dev, HEADS * HEAD_DIM)
+    mean = jnp.mean(tokens, axis=2, keepdims=True)
+    spread = jnp.mean(jnp.square(tokens - mean), axis=2, keepdims=True)
+    normed = (tokens - mean) * lax.rsqrt(spread + eps_norm)
+    modulated = normed * (1.0 + mod_scale[:, None, :]) + mod_shift[:, None, :]
     velocity = (
-        jnp.einsum("chtd,hdo->cto", modulated, weights3, precision=lax.Precision.HIGHEST)
+        jnp.einsum(
+            "ctk,ko->cto",
+            modulated,
+            final_weight.astype(jnp.float32),
+            precision=lax.Precision.HIGHEST,
+        )
         + final_bias
     )
     rows_dev = noisy_latent.shape[2]
@@ -139,7 +175,7 @@
     decoder_in = denoised.astype(jnp.bfloat16)
     group_index = lax.axis_index(("sec", "rep"))
     wanted = lax.dynamic_slice_in_dim(clip_order, group_index * clips, clips)
-    everyone = lax.all_gather(decoder_in, ("sec", "rep"), axis=0, tiled=True)
+    everyone = butterfly_gather(decoder_in, ("sec", "rep"))
     picked = jnp.take(everyone, wanted, axis=0)
     rimmed = edge_rows(extended(picked, (("seq", 2),), 1))
     columns = causal_columns(rimmed)
@@ -149,11 +185,13 @@
         + conv_bias
     )
     conv_out = conv_out.reshape(clips, -1, GROUPS, VAE_CH // GROUPS)
-    cells = conv_out.shape[1] * n_seq * (VAE_CH // GROUPS)
-    local_sum = jnp.sum(conv_out, axis=(1, 3))
-    mean = lax.psum(local_sum, "seq") / cells
+    count = conv_out.shape[1] * (VAE_CH // GROUPS)
+    local_mean = jnp.sum(conv_out, axis=(1, 3)) / count
+    centered_local = conv_out - local_mean[:, None, :, None]
+    local_m2 = jnp.sum(jnp.square(centered_local), axis=(1, 3))
+    mean, m2 = butterfly_moments(local_mean, local_m2, count, "seq")
     centered = conv_out - mean[:, None, :, None]
-    spread = lax.psum(jnp.sum(jnp.square(centered), axis=(1, 3)), "seq") / cells
+    spread = m2 / (count * n_seq)
     normed = (centered * lax.rsqrt(spread + eps_norm)[:, None, :, None]).reshape(clips, -1, VAE_CH)
     features = jax.nn.silu(normed * group_gain + group_shift).astype(jnp.bfloat16)
     features = features.reshape(clips, FRAMES, rows_dev, LAT_W * VAE_CH)

time: 570 us -> 435 us (0.76)
  the two profiles are of different devices: /device:TPU:14 before, /device:TPU:28 now
where the time goes in v1:
time: 435 us; the launch traced here: 434 us
  waiting for transfers between devices  277 us (64%)
  local copies, waits for them, and re-layouts  64.8 us (15%)
  starting transfers between devices  52.6 us (12%)
  other arithmetic  21.9 us (5%)
  matrix products  16.1 us (4%)
    all_to_all x1, waiting for transfers between devices, shards(): lax.all_to_all(stacked, 'seq', split_axis=0, concat_axis=3, tiled=True)  162 us
    all_to_all x1, waiting for transfers between devices, shards(): lax.all_to_all(outputs, 'seq', split_axis=2, concat_axis=0, tiled=True)  75.9 us
    ppermute x5, waiting for transfers between devices, butterfly_moments(): lax.ppermute(jnp.stack([mean, m2]), axis, [(i, i ^ step) for i in range(s...  22 us
    all_to_all x1, starting transfers between devices, shards(): lax.all_to_all(stacked, 'seq', split_axis=0, concat_axis=3, tiled=True)  16.8 us
    unnamed x49, local copies, waits for them, and re-layouts  16.5 us
    ppermute x5, starting transfers between devices, butterfly_moments(): lax.ppermute(jnp.stack([mean, m2]), axis, [(i, i ^ step) for i in range(s...  15.5 us
    ppermute x4, waiting for transfers between devices, butterfly_gather(): other = lax.ppermute(held, axis, [(i, i ^ step) for i in range(count)])  13.5 us
    ppermute x4, starting transfers between devices, butterfly_gather(): other = lax.ppermute(held, axis, [(i, i ^ step) for i in range(count)])  10.8 us
  transfers between devices with their start and end apart: 13, of which 12 were waited for; matrix products, arithmetic and copies ran while one was open for 1% of the time, Pallas kernels for 0%

profile of v1, /device:TPU:28, one launch (start us, length us, event | category | flops | bytes accessed | tf_op | source)
XLA Modules:
  0.0 434.3 jit_solution(8863734314999805236)
XLA Ops:
  0.6 3.5 pad_maximum_fusion
  4.1 16.8 %all-to-all-start = ((bf16[32,3,3,48,128]{4,3,2,1,0:T(8,128)(2,1)}), bf16[32,3,3,48,128]{4,3,2,1,0:T(8,128)(2,1)}, u32[]{:S(2)}, u32[]{:S(2)}) async-start(bf16[32,3,3,48,128]{4,3,2,1,0:T(8,128)(2,1)} %pad_maximum_fusion), calls=%async_computation | async-start | bytes 7077888 | tf_op jit(solution)/shard_map/all_to_all | solution.py:152
  20.9 162.2 %all-to-all-done = bf16[32,3,3,48,128]{4,3,2,1,0:T(8,128)(2,1)} async-done(((bf16[32,3,3,48,128]{4,3,2,1,0:T(8,128)(2,1)}), bf16[32,3,3,48,128]{4,3,2,1,0:T(8,128)(2,1)}, u32[]{:S(2)}, u32[]{:S(2)}) %all-to-all-start) | async-done | bytes 3538976 | tf_op jit(solution)/shard_map/all_to_all | solution.py:152
  183.0 2.7 copy.160
  185.7 1.7 slice_bitcast_fusion
  187.4 26.8 %while.21 = (s32[]{:T(128)}, bf16[3,1536,128]{2,1,0:T(8,128)(2,1)}, bf16[3,1536,128]{2,1,0:T(8,128)(2,1)}, bf16[3,1536,128]{2,1,0:T(8,128)(2,1)}, bf16[3,1536,12...) while((s32[]{:T(128)}, bf16[3,1536,128]{2,1,0:T(8,128)(2,1)}, bf16[3,1536,128]{2,1,0:T(8,128)(2,1)}, ...), condition=%wide.region_5.6_spmd, body=%wide.region_0.5_spmd.sunk | while | flops 408222720 | bytes 13641974 | solution.py:153
  187.4 1.0 constant_dynamic-slice_fusion.2
  188.4 1.1 dynamic-slice_bitcast_fusion.3
  189.5 6.1 %while.22 = (s32[]{:T(128)}, bf16[3,512,128]{2,1,0:T(8,128)(2,1)S(1)}, bf16[3,512,128]{2,1,0:T(8,128)(2,1)S(1)}, bf16[1536,128]{1,0:T(8,128)(2,1)S(1)}, bf16[1536,128]{1,0:T(8,128)(2,1)S(1)}, /*index=5*/s32[]{:T(128)}) while((s32[]{:T(128)}, bf16[3,512,128]{2,1,0:T(8,128)(2,1)S(1)}, bf16[3,512,128]{2,1,0:T(8,128)(2,1)S(1)}, ...), condition=%wide.region_4.4_spmd, body=%wide.region_1.3_spmd.sunk | while | flops 408222720 | bytes 10496085 | solution.py:85
  190.7 0.8 fusion.106
  192.8 0.8 fusion.106
  194.8 0.8 fusion.106
  195.6 0.8 bitcast_dynamic-update-slice_fusion.2
  196.3 1.0 constant_dynamic-slice_fusion.2
  197.4 1.1 dynamic-slice_bitcast_fusion.3
  198.4 6.1 %while.22 = (s32[]{:T(128)}, bf16[3,512,128]{2,1,0:T(8,128)(2,1)S(1)}, bf16[3,512,128]{2,1,0:T(8,128)(2,1)S(1)}, bf16[1536,128]{1,0:T(8,128)(2,1)S(1)}, bf16[1536,128]{1,0:T(8,128)(2,1)S(1)}, /*index=5*/s32[]{:T(128)}) while((s32[]{:T(128)}, bf16[3,512,128]{2,1,0:T(8,128)(2,1)S(1)}, bf16[3,512,128]{2,1,0:T(8,128)(2,1)S(1)}, ...), condition=%wide.region_4.4_spmd, body=%wide.region_1.3_spmd.sunk | while | flops 408222720 | bytes 10496085 | solution.py:85
  199.7 0.8 fusion.106
  201.7 0.8 fusion.106
  203.7 0.8 fusion.106
  204.5 0.8 bitcast_dynamic-update-slice_fusion.2
  205.3 1.0 constant_dynamic-slice_fusion.2
  206.3 1.1 dynamic-slice_bitcast_fusion.3
  207.3 6.1 %while.22 = (s32[]{:T(128)}, bf16[3,512,128]{2,1,0:T(8,128)(2,1)S(1)}, bf16[3,512,128]{2,1,0:T(8,128)(2,1)S(1)}, bf16[1536,128]{1,0:T(8,128)(2,1)S(1)}, bf16[1536,128]{1,0:T(8,128)(2,1)S(1)}, /*index=5*/s32[]{:T(128)}) while((s32[]{:T(128)}, bf16[3,512,128]{2,1,0:T(8,128)(2,1)S(1)}, bf16[3,512,128]{2,1,0:T(8,128)(2,1)S(1)}, ...), condition=%wide.region_4.4_spmd, body=%wide.region_1.3_spmd.sunk | while | flops 408222720 | bytes 10496085 | solution.py:85
  208.6 0.8 fusion.106
  210.6 0.8 fusion.106
  212.6 0.8 fusion.106
  213.4 0.8 bitcast_dynamic-update-slice_fusion.2
  214.2 8.1 %copy.182 = bf16[3,1536,128]{2,0,1:T(4,128)(2,1)} copy(bf16[3,1536,128]{2,1,0:T(8,128)(2,1)} %get-tuple-element.56) | data formatting | bytes 2359296 | tf_op jit(solution)/shard_map/while | solution.py:153
  222.4 3.8 all-to-all-start.1
  226.2 75.9 %all-to-all-done.1 = bf16[1,3,1536,128]{3,1,0,2:T(4,128)(2,1)S(1)} async-done(((bf16[1,3,1536,128]{3,1,0,2:T(4,128)(2,1)}), bf16[1,3,1536,128]{3,1,0,2:T(4,128)(2,1)S(1)}, u32[]{:S(2)}, u32[]{:S(2)}) %all-to-all-start.1) | async-done | bytes 1179680 | tf_op jit(solution)/shard_map/all_to_all | solution.py:154
  303.6 1.6 fusion.25
  306.9 3.1 collective-permute-start
  310.1 4.1 collective-permute-done
  314.2 3.1 collective-permute-start.1
  317.4 2.8 collective-permute-done.1
  320.4 2.4 collective-permute-start.2
  322.9 5.5 %collective-permute-done.2 = bf16[4,4,3,2,512]{4,3,2,1,0:T(2,128)(2,1)S(1)} collective-permute-done((bf16[4,4,3,2,512]{4,3,2,1,0:T(2,128)(2,1)S(1)}, bf16[4,4,3,2,512]{4,3,2,1,0:T(2,128)(2,1)S(1)}, u32[]{:S(2)}, u32[]{:S(2)}) %collective-permute-start.2) | collective-permute-done | bytes 98336 | tf_op jit(solution)/shard_map/ppermute | solution.py:47
  328.9 2.1 collective-permute-start.3
  331.1 1.1 collective-permute-done.3
  332.2 0.9 broadcast_select_fusion
  333.8 3.1 collective-permute-start.4
  336.9 2.7 collective-permute-start.5
  339.7 3.8 collective-permute-done.5
  363.8 7.9 %copy.166 = bf16[4,3,2,32,27,16]{3,2,1,0,5,4:T(2,128)(2,1)S(1)} copy(bf16[4,3,2,32,27,16]{5,3,2,1,0,4:T(8,128)(2,1)} %fusion.46) | data formatting | bytes 1327104 | tf_op jit(solution)/shard_map/stack | solution.py:113
  371.7 2.5 reshape_reshape.3
  374.2 1.7 convolution_add_fusion
  375.9 1.2 copy-done.1
  377.1 1.6 copy.167
  378.7 2.7 reshape.222
  382.1 0.8 multiply_reduce_fusion.1
  382.9 1.9 collective-permute-start.6
  384.8 3.6 collective-permute-done.6
  388.4 1.9 collective-permute-start.7
  390.3 3.6 collective-permute-done.7
  393.9 3.8 collective-permute-start.8
  397.8 2.5 collective-permute-done.8
  400.3 3.1 collective-permute-start.9
  403.4 6.3 %collective-permute-done.9 = f32[2,4,32]{2,1,0:T(4,128)S(1)} collective-permute-done((f32[2,4,32]{2,1,0:T(4,128)S(1)}, f32[2,4,32]{2,1,0:T(4,128)S(1)}, u32[]{:S(2)}, u32[]{:S(2)}) %collective-permute-start.9) | collective-permute-done | bytes 1056 | tf_op jit(solution)/shard_map/ppermute | solution.py:62
  409.8 4.8 %collective-permute-start.10 = (f32[2,4,32]{2,1,0:T(4,128)S(1)}, f32[2,4,32]{2,1,0:T(4,128)S(1)}, u32[]{:S(2)}, u32[]{:S(2)}) collective-permute-start(f32[2,4,32]{2,1,0:T(4,128)S(1)} %pad_maximum_fusion.13), channel_id=1, source_target_pairs={{0,128},{8,136},{16,144},{24,152},{32,160},{40,168},{48,176},{56,1... | collective-permute-start | bytes 3080 | tf_op jit(solution)/shard_map/ppermute | solution.py:62
  414.6 3.4 reshape.221
  418.0 6.0 %collective-permute-done.10 = f32[2,4,32]{2,1,0:T(4,128)S(1)} collective-permute-done((f32[2,4,32]{2,1,0:T(4,128)S(1)}, f32[2,4,32]{2,1,0:T(4,128)S(1)}, u32[]{:S(2)}, u32[]{:S(2)}) %collective-permute-start.10) | collective-permute-done | bytes 1056 | tf_op jit(solution)/shard_map/ppermute | solution.py:62
  424.4 2.5 mul.262
  427.3 2.5 sub.141
  429.8 4.5 %fusion.20 = bf16[4,3,2,16384]{3,2,1,0:T(2,128)(2,1)} fusion(f32[4,3,2,16384]{3,2,1,0:T(2,128)} %mul.262, f32[4,3,2,16384]{3,2,1,0:T(2,128)} %reshape.221, f32[4,3,2,16384]{3,2,1,0:T(2,128)} %sub.141, f32[16384]{0:T(1024)S(1)} %bitcast.321, f32[16384]{0:T(1024)S(1)} %bitcast.322), kind=kLoop, calls=%fused_computation.36 | loop fusion | flops 3538944 | bytes 5636096 | tf_op jit(solution)/shard_map/convert_element_type | solution.py:196
  (125 shorter events, 37.6 us)
Async XLA Ops:
  0.6 373.6 %copy-start = (bf16[3,3,3,16,512]{4,3,2,1,0:T(8,128)(2,1)S(1)}, bf16[3,3,3,16,512]{4,3,2,1,0:T(8,128)(2,1)}, u32[]{:S(2)}) copy-start(bf16[3,3,3,16,512]{4,3,2,1,0:T(8,128)(2,1)} %param.28) | copy-start | bytes 1327108
  4.1 178.9 %all-to-all-start = ((bf16[32,3,3,48,128]{4,3,2,1,0:T(8,128)(2,1)}), bf16[32,3,3,48,128]{4,3,2,1,0:T(8,128)(2,1)}, u32[]{:S(2)}, u32[]{:S(2)}) async-start(bf16[32,3,3,48,128]{4,3,2,1,0:T(8,128)(2,1)} %pad_maximum_fusion), calls=%async_computation | async-start | bytes 7077888 | tf_op jit(solution)/shard_map/all_to_all | solution.py:152
  214.2 11.9 %copy-start.10 = (s32[4]{0:T(128)S(1)}, s32[4]{0:T(128)}, u32[]{:S(2)}) copy-start(s32[4]{0:T(128)} %param.26) | copy-start | bytes 52
  214.2 11.9 %copy-start.2 = (f32[4,3072]{1,0:T(4,128)S(1)}, f32[4,3072]{1,0:T(4,128)}, u32[]{:S(2)}) copy-start(f32[4,3072]{1,0:T(4,128)} %param.22) | copy-start | bytes 147460
  222.4 79.7 %all-to-all-start.1 = ((bf16[1,3,1536,128]{3,1,0,2:T(4,128)(2,1)}), bf16[1,3,1536,128]{3,1,0,2:T(4,128)(2,1)S(1)}, u32[]{:S(2)}, u32[]{:S(2)}) async-start(bf16[1,3,1536,128]{3,1,0,2:T(4,128)(2,1)} %bitcast.314), calls=%async_computation.1 | async-start | bytes 3145728 | tf_op jit(solution)/shard_map/all_to_all | solution.py:154
  302.6 1.0 copy-start.7
  302.6 1.0 copy-start.8
  302.6 1.0 copy-start.11
  303.2 3.0 copy-start.3
  303.6 27.4 %copy-start.6 = (s32[64]{0:T(128)S(1)}, s32[64]{0:T(128)}, u32[]{:S(2)}) copy-start(s32[64]{0:T(128)} %param.27) | copy-start | bytes 772
  306.9 7.2 %collective-permute-start = (bf16[1,4,3,2,512]{4,3,2,1,0:T(2,128)(2,1)S(1)}, bf16[1,4,3,2,512]{4,3,2,1,0:T(2,128)(2,1)S(1)}, u32[]{:S(2)}, u32[]{:S(2)}) collective-permute-start(bf16[1,4,3,2,512]{4,3,2,1,0:T(2,128)(2,1)S(1)} %get-tuple-element.79), channel_id=1, source_target_pairs={{0,1},{1,0},{2,3},{3,2},{4,5},{5,4},{6,7},{7,6},{256,257},{257,256... | collective-permute-start | bytes 73736 | tf_op jit(solution)/shard_map/ppermute | solution.py:47
  314.2 6.0 %collective-permute-start.1 = (bf16[2,4,3,2,512]{4,3,2,1,0:T(2,128)(2,1)S(1)}, bf16[2,4,3,2,512]{4,3,2,1,0:T(2,128)(2,1)S(1)}, u32[]{:S(2)}, u32[]{:S(2)}) collective-permute-start(bf16[2,4,3,2,512]{4,3,2,1,0:T(2,128)(2,1)S(1)} %broadcast_select_fusion.3), channel_id=1, source_target_pairs={{0,2},{1,3},{2,0},{3,1},{4,6},{5,7},{6,4},{7,5},{256,258},{257,259... | collective-permute-start | bytes 147464 | tf_op jit(solution)/shard_map/ppermute | solution.py:47
  320.4 8.0 %collective-permute-start.2 = (bf16[4,4,3,2,512]{4,3,2,1,0:T(2,128)(2,1)S(1)}, bf16[4,4,3,2,512]{4,3,2,1,0:T(2,128)(2,1)S(1)}, u32[]{:S(2)}, u32[]{:S(2)}) collective-permute-start(bf16[4,4,3,2,512]{4,3,2,1,0:T(2,128)(2,1)S(1)} %broadcast_select_fusion.2), channel_id=1, source_target_pairs={{0,4},{1,5},{2,6},{3,7},{4,0},{5,1},{6,2},{7,3},{256,260},{257,261... | collective-permute-start | bytes 294920 | tf_op jit(solution)/shard_map/ppermute | solution.py:47
  328.9 3.3 collective-permute-start.3
  333.8 5.9 %collective-permute-start.4 = (bf16[4,3,1,512]{3,2,1,0:T(2,128)(2,1)S(1)}, bf16[4,3,1,512]{3,2,1,0:T(2,128)(2,1)S(1)}, u32[]{:S(2)}, u32[]{:S(2)}) collective-permute-start(bf16[4,3,1,512]{3,2,1,0:T(2,128)(2,1)S(1)} %get-tuple-element.92), channel_id=1, source_target_pairs={{0,8},{8,16},{16,24},{24,32},{32,40},{40,48},{48,56},{56,64},{64,7... | collective-permute-start | bytes 36872 | tf_op jit(solution)/shard_map/ppermute | solution.py:32
  336.9 6.6 %collective-permute-start.5 = (bf16[4,3,1,512]{3,2,1,0:T(2,128)(2,1)S(1)}, bf16[4,3,1,512]{3,2,1,0:T(2,128)(2,1)S(1)}, u32[]{:S(2)}, u32[]{:S(2)}) collective-permute-start(bf16[4,3,1,512]{3,2,1,0:T(2,128)(2,1)S(1)} %get-tuple-element.93), channel_id=1, source_target_pairs={{8,0},{16,8},{24,16},{32,24},{40,32},{48,40},{56,48},{64,56},{72,6... | collective-permute-start | bytes 36872 | tf_op jit(solution)/shard_map/ppermute | solution.py:34
  371.7 2.5 copy-start.9
  375.9 1.2 copy-start.1
  378.7 24.7 %copy-start.4 = (f32[512]{0:T(512)S(1)}, f32[512]{0:T(512)}, u32[]{:S(2)}) copy-start(f32[512]{0:T(512)} %param.31) | copy-start | bytes 6148
  381.4 33.1 %copy-start.5 = (f32[512]{0:T(512)S(1)}, f32[512]{0:T(512)}, u32[]{:S(2)}) copy-start(f32[512]{0:T(512)} %param.30) | copy-start | bytes 6148
  382.9 5.5 %collective-permute-start.6 = (f32[2,4,32]{2,1,0:T(4,128)S(1)}, f32[2,4,32]{2,1,0:T(4,128)S(1)}, u32[]{:S(2)}, u32[]{:S(2)}) collective-permute-start(f32[2,4,32]{2,1,0:T(4,128)S(1)} %pad_maximum_fusion.9), channel_id=1, source_target_pairs={{0,8},{8,0},{16,24},{24,16},{32,40},{40,32},{48,56},{56,48},{64,72... | collective-permute-start | bytes 3080 | tf_op jit(solution)/shard_map/ppermute | solution.py:62
  388.4 5.5 %collective-permute-start.7 = (f32[2,4,32]{2,1,0:T(4,128)S(1)}, f32[2,4,32]{2,1,0:T(4,128)S(1)}, u32[]{:S(2)}, u32[]{:S(2)}) collective-permute-start(f32[2,4,32]{2,1,0:T(4,128)S(1)} %pad_maximum_fusion.10), channel_id=1, source_target_pairs={{0,16},{8,24},{16,0},{24,8},{32,48},{40,56},{48,32},{56,40},{64,80... | collective-permute-start | bytes 3080 | tf_op jit(solution)/shard_map/ppermute | solution.py:62
  393.9 6.4 %collective-permute-start.8 = (f32[2,4,32]{2,1,0:T(4,128)S(1)}, f32[2,4,32]{2,1,0:T(4,128)S(1)}, u32[]{:S(2)}, u32[]{:S(2)}) collective-permute-start(f32[2,4,32]{2,1,0:T(4,128)S(1)} %pad_maximum_fusion.11), channel_id=1, source_target_pairs={{0,32},{8,40},{16,48},{24,56},{32,0},{40,8},{48,16},{56,24},{64,96... | collective-permute-start | bytes 3080 | tf_op jit(solution)/shard_map/ppermute | solution.py:62
  400.3 9.4 %collective-permute-start.9 = (f32[2,4,32]{2,1,0:T(4,128)S(1)}, f32[2,4,32]{2,1,0:T(4,128)S(1)}, u32[]{:S(2)}, u32[]{:S(2)}) collective-permute-start(f32[2,4,32]{2,1,0:T(4,128)S(1)} %pad_maximum_fusion.12), channel_id=1, source_target_pairs={{0,64},{8,72},{16,80},{24,88},{32,96},{40,104},{48,112},{56,120},{... | collective-permute-start | bytes 3080 | tf_op jit(solution)/shard_map/ppermute | solution.py:62
  409.8 14.3 %collective-permute-start.10 = (f32[2,4,32]{2,1,0:T(4,128)S(1)}, f32[2,4,32]{2,1,0:T(4,128)S(1)}, u32[]{:S(2)}, u32[]{:S(2)}) collective-permute-start(f32[2,4,32]{2,1,0:T(4,128)S(1)} %pad_maximum_fusion.13), channel_id=1, source_target_pairs={{0,128},{8,136},{16,144},{24,152},{32,160},{40,168},{48,176},{56,1... | collective-permute-start | bytes 3080 | tf_op jit(solution)/shard_map/ppermute | solution.py:62

commit v2 on v1

--- a/solution.py
+++ b/solution.py
@@ -150,23 +150,46 @@
         axis=1,
     )
     parts = lax.all_to_all(stacked, "seq", split_axis=0, concat_axis=3, tiled=True)
-    outputs = lax.map(attend_unit, (parts[0, 0], parts[0, 1], parts[0, 2]))[None]
-    mixed = lax.all_to_all(outputs, "seq", split_axis=2, concat_axis=0, tiled=True)
-    heads = mixed.reshape(clips, HEADS, tok_dev, HEAD_DIM).astype(jnp.float32)
-    tokens = jnp.transpose(heads, (0, 2, 1, 3)).reshape(clips, tok_dev, HEADS * HEAD_DIM)
-    mean = jnp.mean(tokens, axis=2, keepdims=True)
-    spread = jnp.mean(jnp.square(tokens - mean), axis=2, keepdims=True)
-    normed = (tokens - mean) * lax.rsqrt(spread + eps_norm)
-    modulated = normed * (1.0 + mod_scale[:, None, :]) + mod_shift[:, None, :]
-    velocity = (
-        jnp.einsum(
-            "ctk,ko->cto",
-            modulated,
-            final_weight.astype(jnp.float32),
-            precision=lax.Precision.HIGHEST,
-        )
-        + final_bias
-    )
+    outputs = lax.map(attend_unit, (parts[0, 0], parts[0, 1], parts[0, 2]))
+    seq_len = outputs.shape[1]
+    chunks = HEADS // units_local
+    width = units_local * HEAD_DIM
+    me = lax.axis_index("seq")
+    own_clip = me // chunks
+    own_chunk = me % chunks
+    weight = final_weight.astype(jnp.float32)
+    x = jnp.transpose(outputs.astype(jnp.float32), (1, 0, 2)).reshape(seq_len, width)
+    part_mean = jnp.mean(x, axis=1, keepdims=True)
+    part_dev = x - part_mean
+    part_m2 = jnp.sum(jnp.square(part_dev), axis=1, keepdims=True)
+    scale_row = lax.dynamic_slice_in_dim(mod_scale, own_clip, 1, axis=0)[0]
+    scale_part = lax.dynamic_slice_in_dim(scale_row, own_chunk * width, width)
+    weight_part = lax.dynamic_slice_in_dim(weight, own_chunk * width, width, axis=0)
+    folded = (1.0 + scale_part)[:, None] * weight_part
+    partial = jnp.dot(part_dev, folded, precision=lax.Precision.HIGHEST)
+    packed = jnp.concatenate([partial, part_mean, part_m2], axis=1)
+    fields = packed.shape[1]
+    packed = packed.reshape(n_seq, tok_dev * fields)
+    recv = lax.all_to_all(packed, "seq", split_axis=0, concat_axis=0, tiled=True)
+    recv = recv.reshape(clips, chunks, tok_dev, fields)
+    partials = recv[..., :PATCH_OUT]
+    means = recv[..., PATCH_OUT]
+    m2s = recv[..., PATCH_OUT + 1]
+    mean = jnp.mean(means, axis=1)
+    gaps = means - mean[:, None, :]
+    m2 = jnp.sum(m2s, axis=1) + width * jnp.sum(jnp.square(gaps), axis=1)
+    rstd = lax.rsqrt(m2 / (HEADS * HEAD_DIM) + eps_norm)
+    folded_all = jnp.einsum(
+        "cjk,jko->cjo",
+        (1.0 + mod_scale).reshape(clips, chunks, width),
+        weight.reshape(chunks, width, PATCH_OUT),
+        precision=lax.Precision.HIGHEST,
+    )
+    core = jnp.sum(partials, axis=1) + jnp.einsum(
+        "cjt,cjo->cto", gaps, folded_all, precision=lax.Precision.HIGHEST
+    )
+    shift_proj = jnp.dot(mod_shift, weight, precision=lax.Precision.HIGHEST)
+    velocity = rstd[..., None] * core + shift_proj[:, None, :] + final_bias
     rows_dev = noisy_latent.shape[2]
     velocity = velocity.reshape(clips, rows_dev // 2, FRAMES, PATCH_W, 2, 2, LAT_CH)
     velocity = jnp.transpose(velocity, (0, 2, 1, 4, 3, 5, 6)).reshape(noisy_latent.shape)

time: 435 us -> 382 us (0.88)
  the two profiles are of different devices: /device:TPU:28 before, /device:TPU:4 now
where the time goes in v2:
time: 382 us; the launch traced here: 381 us
  waiting for transfers between devices  220 us (58%)
  starting transfers between devices  58.6 us (15%)
  local copies, waits for them, and re-layouts  57.7 us (15%)
  other arithmetic  25.2 us (7%)
  matrix products  17.4 us (5%)
    all_to_all x1, waiting for transfers between devices, shards(): lax.all_to_all(stacked, 'seq', split_axis=0, concat_axis=3, tiled=True)  155 us
    all_to_all x1, waiting for transfers between devices, shards(): lax.all_to_all(packed, 'seq', split_axis=0, concat_axis=0, tiled=True)  26.7 us
    ppermute x5, waiting for transfers between devices, butterfly_moments(): lax.ppermute(jnp.stack([mean, m2]), axis, [(i, i ^ step) for i in range(s...  21.9 us
    all_to_all x1, starting transfers between devices, shards(): lax.all_to_all(stacked, 'seq', split_axis=0, concat_axis=3, tiled=True)  16.6 us
    unnamed x51, local copies, waits for them, and re-layouts  16.3 us
    ppermute x5, starting transfers between devices, butterfly_moments(): lax.ppermute(jnp.stack([mean, m2]), axis, [(i, i ^ step) for i in range(s...  15.6 us
    ppermute x4, starting transfers between devices, butterfly_gather(): other = lax.ppermute(held, axis, [(i, i ^ step) for i in range(count)])  12.4 us
    ppermute x4, waiting for transfers between devices, butterfly_gather(): other = lax.ppermute(held, axis, [(i, i ^ step) for i in range(count)])  11.9 us
  transfers between devices with their start and end apart: 13, of which 13 were waited for; matrix products, arithmetic and copies ran while one was open for 2% of the time, Pallas kernels for 0%

profile of v2, /device:TPU:4, one launch (start us, length us, event | category | flops | bytes accessed | tf_op | source)
XLA Modules:
  0.0 380.6 jit_solution(6046944974565535720)
XLA Ops:
  0.6 3.5 pad_maximum_fusion
  4.1 16.6 %all-to-all-start = ((bf16[32,3,3,48,128]{4,3,2,1,0:T(8,128)(2,1)}), bf16[32,3,3,48,128]{4,3,2,1,0:T(8,128)(2,1)}, u32[]{:S(2)}, u32[]{:S(2)}) async-start(bf16[32,3,3,48,128]{4,3,2,1,0:T(8,128)(2,1)} %pad_maximum_fusion), calls=%async_computation | async-start | bytes 7077888 | tf_op jit(solution)/shard_map/all_to_all | solution.py:152
  20.8 1.4 add_reduce_fusion
  22.1 155.1 %all-to-all-done = bf16[32,3,3,48,128]{4,3,2,1,0:T(8,128)(2,1)} async-done(((bf16[32,3,3,48,128]{4,3,2,1,0:T(8,128)(2,1)}), bf16[32,3,3,48,128]{4,3,2,1,0:T(8,128)(2,1)}, u32[]{:S(2)}, u32[]{:S(2)}) %all-to-all-start) | async-done | bytes 3538976 | tf_op jit(solution)/shard_map/all_to_all | solution.py:152
  177.3 2.7 copy.171
  180.0 1.9 slice_bitcast_fusion
  181.8 25.6 %while.21 = (s32[]{:T(128)}, bf16[3,1536,128]{1,2,0:T(8,128)(2,1)S(1)}, bf16[3,1536,128]{2,1,0:T(8,128)(2,1)}, bf16[3,1536,128]{2,1,0:T(8,128)(2,1)}, bf16[3,153...) while((s32[]{:T(128)}, bf16[3,1536,128]{1,2,0:T(8,128)(2,1)S(1)}, ...), condition=%wide.region_5.6_spmd, body=%wide.region_0.5_spmd.sunk | while | flops 408222720 | bytes 14428406 | solution.py:153
  181.8 1.0 constant_dynamic-slice_fusion.2
  182.9 1.2 dynamic-slice_bitcast_fusion.3
  184.0 6.1 %while.22 = (s32[]{:T(128)}, bf16[3,512,128]{2,1,0:T(8,128)(2,1)S(1)}, bf16[3,512,128]{2,1,0:T(8,128)(2,1)S(1)}, bf16[1536,128]{1,0:T(8,128)(2,1)S(1)}, bf16[1536,128]{1,0:T(8,128)(2,1)S(1)}, /*index=5*/s32[]{:T(128)}) while((s32[]{:T(128)}, bf16[3,512,128]{2,1,0:T(8,128)(2,1)S(1)}, bf16[3,512,128]{2,1,0:T(8,128)(2,1)S(1)}, ...), condition=%wide.region_4.4_spmd, body=%wide.region_1.3_spmd.sunk | while | flops 408222720 | bytes 10496085 | solution.py:85
  185.3 0.8 fusion.113
  187.3 0.8 fusion.113
  189.3 0.8 fusion.113
  190.4 1.0 constant_dynamic-slice_fusion.2
  191.4 1.2 dynamic-slice_bitcast_fusion.3
  192.6 6.1 %while.22 = (s32[]{:T(128)}, bf16[3,512,128]{2,1,0:T(8,128)(2,1)S(1)}, bf16[3,512,128]{2,1,0:T(8,128)(2,1)S(1)}, bf16[1536,128]{1,0:T(8,128)(2,1)S(1)}, bf16[1536,128]{1,0:T(8,128)(2,1)S(1)}, /*index=5*/s32[]{:T(128)}) while((s32[]{:T(128)}, bf16[3,512,128]{2,1,0:T(8,128)(2,1)S(1)}, bf16[3,512,128]{2,1,0:T(8,128)(2,1)S(1)}, ...), condition=%wide.region_4.4_spmd, body=%wide.region_1.3_spmd.sunk | while | flops 408222720 | bytes 10496085 | solution.py:85
  193.8 0.8 fusion.113
  195.8 0.8 fusion.113
  197.9 0.8 fusion.113
  198.9 1.0 constant_dynamic-slice_fusion.2
  199.9 1.2 dynamic-slice_bitcast_fusion.3
  201.1 6.1 %while.22 = (s32[]{:T(128)}, bf16[3,512,128]{2,1,0:T(8,128)(2,1)S(1)}, bf16[3,512,128]{2,1,0:T(8,128)(2,1)S(1)}, bf16[1536,128]{1,0:T(8,128)(2,1)S(1)}, bf16[1536,128]{1,0:T(8,128)(2,1)S(1)}, /*index=5*/s32[]{:T(128)}) while((s32[]{:T(128)}, bf16[3,512,128]{2,1,0:T(8,128)(2,1)S(1)}, bf16[3,512,128]{2,1,0:T(8,128)(2,1)S(1)}, ...), condition=%wide.region_4.4_spmd, body=%wide.region_1.3_spmd.sunk | while | flops 408222720 | bytes 10496085 | solution.py:85
  202.3 0.8 fusion.113
  204.4 0.8 fusion.113
  206.4 0.8 fusion.113
  208.4 1.6 fusion.62
  210.4 1.8 all_to_all.25
  212.1 9.2 %all-to-all-start.1 = ((f32[32,1,3168]{2,1,0:T(1,128)}), f32[32,1,3168]{2,1,0:T(1,128)S(1)}, u32[]{:S(2)}, u32[]{:S(2)}) async-start(f32[32,1,3168]{2,1,0:T(1,128)} %all_to_all.25), calls=%async_computation.1 | async-start | bytes 819200 | tf_op jit(solution)/shard_map/all_to_all | solution.py:173
  222.3 26.7 %all-to-all-done.1 = f32[32,1,3168]{2,1,0:T(1,128)S(1)} async-done(((f32[32,1,3168]{2,1,0:T(1,128)}), f32[32,1,3168]{2,1,0:T(1,128)S(1)}, u32[]{:S(2)}, u32[]{:S(2)}) %all-to-all-start.1) | async-done | bytes 405536 | tf_op jit(solution)/shard_map/all_to_all | solution.py:173
  249.1 1.0 reduce.6
  250.7 0.8 slice_reduce_fusion.2
  253.7 4.8 %collective-permute-start = (bf16[1,4,3,2,512]{4,3,2,1,0:T(2,128)(2,1)S(1)}, bf16[1,4,3,2,512]{4,3,2,1,0:T(2,128)(2,1)S(1)}, u32[]{:S(2)}, u32[]{:S(2)}) collective-permute-start(bf16[1,4,3,2,512]{4,3,2,1,0:T(2,128)(2,1)S(1)} %get-tuple-element.82), channel_id=1, source_target_pairs={{0,1},{1,0},{2,3},{3,2},{4,5},{5,4},{6,7},{7,6},{256,257},{257,256... | collective-permute-start | bytes 73736 | tf_op jit(solution)/shard_map/ppermute | solution.py:47
  258.5 2.4 collective-permute-done
  261.0 3.3 collective-permute-start.1
  264.3 2.7 collective-permute-done.1
  267.2 2.4 collective-permute-start.2
  269.7 5.5 %collective-permute-done.2 = bf16[4,4,3,2,512]{4,3,2,1,0:T(2,128)(2,1)S(1)} collective-permute-done((bf16[4,4,3,2,512]{4,3,2,1,0:T(2,128)(2,1)S(1)}, bf16[4,4,3,2,512]{4,3,2,1,0:T(2,128)(2,1)S(1)}, u32[]{:S(2)}, u32[]{:S(2)}) %collective-permute-start.2) | collective-permute-done | bytes 98336 | tf_op jit(solution)/shard_map/ppermute | solution.py:47
  275.6 1.9 collective-permute-start.3
  277.7 1.3 collective-permute-done.3
  279.0 0.9 broadcast_select_fusion
  280.6 3.5 collective-permute-start.4
  284.1 1.3 collective-permute-start.5
  285.6 4.2 %collective-permute-done.5 = bf16[4,3,1,512]{3,2,1,0:T(2,128)(2,1)S(1)} collective-permute-done((bf16[4,3,1,512]{3,2,1,0:T(2,128)(2,1)S(1)}, bf16[4,3,1,512]{3,2,1,0:T(2,128)(2,1)S(1)}, u32[]{:S(2)}, u32[]{:S(2)}) %collective-permute-start.5) | collective-permute-done | bytes 12320 | tf_op jit(solution)/shard_map/ppermute | solution.py:34
  310.1 7.9 %copy.179 = bf16[4,3,2,32,27,16]{3,2,1,0,5,4:T(2,128)(2,1)S(1)} copy(bf16[4,3,2,32,27,16]{5,3,2,1,0,4:T(8,128)(2,1)} %fusion.39) | data formatting | bytes 1327104 | tf_op jit(solution)/shard_map/stack | solution.py:113
  318.1 2.5 reshape_reshape.3
  320.6 1.7 convolution_add_fusion
  322.3 1.1 copy-done.1
  323.4 1.6 copy.180
  325.1 2.7 reshape.254
  328.4 0.8 multiply_reduce_fusion
  329.3 2.8 collective-permute-start.6
  332.1 2.7 collective-permute-done.6
  334.8 2.2 collective-permute-start.7
  337.0 3.3 collective-permute-done.7
  340.3 2.7 collective-permute-start.8
  343.0 3.7 collective-permute-done.8
  346.7 3.8 %collective-permute-start.9 = (f32[2,4,32]{2,1,0:T(4,128)S(1)}, f32[2,4,32]{2,1,0:T(4,128)S(1)}, u32[]{:S(2)}, u32[]{:S(2)}) collective-permute-start(f32[2,4,32]{2,1,0:T(4,128)S(1)} %pad_maximum_fusion.13), channel_id=1, source_target_pairs={{0,64},{8,72},{16,80},{24,88},{32,96},{40,104},{48,112},{56,120},{... | collective-permute-start | bytes 3080 | tf_op jit(solution)/shard_map/ppermute | solution.py:62
  350.6 5.5 %collective-permute-done.9 = f32[2,4,32]{2,1,0:T(4,128)S(1)} collective-permute-done((f32[2,4,32]{2,1,0:T(4,128)S(1)}, f32[2,4,32]{2,1,0:T(4,128)S(1)}, u32[]{:S(2)}, u32[]{:S(2)}) %collective-permute-start.9) | collective-permute-done | bytes 1056 | tf_op jit(solution)/shard_map/ppermute | solution.py:62
  356.1 4.1 %collective-permute-start.10 = (f32[2,4,32]{2,1,0:T(4,128)S(1)}, f32[2,4,32]{2,1,0:T(4,128)S(1)}, u32[]{:S(2)}, u32[]{:S(2)}) collective-permute-start(f32[2,4,32]{2,1,0:T(4,128)S(1)} %pad_maximum_fusion.14), channel_id=1, source_target_pairs={{0,128},{8,136},{16,144},{24,152},{32,160},{40,168},{48,176},{56,1... | collective-permute-start | bytes 3080 | tf_op jit(solution)/shard_map/ppermute | solution.py:62
  360.3 3.4 reshape.253
  363.7 6.7 %collective-permute-done.10 = f32[2,4,32]{2,1,0:T(4,128)S(1)} collective-permute-done((f32[2,4,32]{2,1,0:T(4,128)S(1)}, f32[2,4,32]{2,1,0:T(4,128)S(1)}, u32[]{:S(2)}, u32[]{:S(2)}) %collective-permute-start.10) | collective-permute-done | bytes 1056 | tf_op jit(solution)/shard_map/ppermute | solution.py:62
  370.8 2.5 mul.279
  373.6 2.5 sub.151
  376.1 4.5 %fusion.16 = bf16[4,3,2,16384]{3,2,1,0:T(2,128)(2,1)} fusion(f32[4,3,2,16384]{3,2,1,0:T(2,128)} %mul.279, f32[4,3,2,16384]{3,2,1,0:T(2,128)} %reshape.253, f32[4,3,2,16384]{3,2,1,0:T(2,128)} %sub.151, f32[16384]{0:T(1024)S(1)} %bitcast.310, f32[16384]{0:T(1024)S(1)} %bitcast.311), kind=kLoop, calls=%fused_computation.31 | loop fusion | flops 3538944 | bytes 5636096 | tf_op jit(solution)/shard_map/convert_element_type | solution.py:219
  (142 shorter events, 40.3 us)
Async XLA Ops:
  0.6 319.9 %copy-start = (bf16[3,3,3,16,512]{4,3,2,1,0:T(8,128)(2,1)S(1)}, bf16[3,3,3,16,512]{4,3,2,1,0:T(8,128)(2,1)}, u32[]{:S(2)}) copy-start(bf16[3,3,3,16,512]{4,3,2,1,0:T(8,128)(2,1)} %param.28) | copy-start | bytes 1327108
  4.1 173.1 %all-to-all-start = ((bf16[32,3,3,48,128]{4,3,2,1,0:T(8,128)(2,1)}), bf16[32,3,3,48,128]{4,3,2,1,0:T(8,128)(2,1)}, u32[]{:S(2)}, u32[]{:S(2)}) async-start(bf16[32,3,3,48,128]{4,3,2,1,0:T(8,128)(2,1)} %pad_maximum_fusion), calls=%async_computation | async-start | bytes 7077888 | tf_op jit(solution)/shard_map/all_to_all | solution.py:152
  207.4 1.0 copy-start.2
  207.4 1.0 copy-start.6
  208.4 12.9 %copy-start.12 = (s32[4]{0:T(128)S(1)}, s32[4]{0:T(128)}, u32[]{:S(2)}) copy-start(s32[4]{0:T(128)} %param.26) | copy-start | bytes 52
  208.4 13.0 %copy-start.4 = (f32[4,3072]{1,0:T(4,128)S(1)}, f32[4,3072]{1,0:T(4,128)}, u32[]{:S(2)}) copy-start(f32[4,3072]{1,0:T(4,128)} %param.21) | copy-start | bytes 147460
  208.4 13.4 %copy-start.3 = (f32[4,3072]{1,0:T(4,128)S(1)}, f32[4,3072]{1,0:T(4,128)}, u32[]{:S(2)}) copy-start(f32[4,3072]{1,0:T(4,128)} %param.22) | copy-start | bytes 147460
  212.1 39.4 %copy-start.9 = (f32[64]{0:T(128)S(1)}, f32[64]{0:T(128)}, u32[]{:S(2)}) copy-start(f32[64]{0:T(128)} %param.24) | copy-start | bytes 772
  212.1 36.9 %all-to-all-start.1 = ((f32[32,1,3168]{2,1,0:T(1,128)}), f32[32,1,3168]{2,1,0:T(1,128)S(1)}, u32[]{:S(2)}, u32[]{:S(2)}) async-start(f32[32,1,3168]{2,1,0:T(1,128)} %all_to_all.25), calls=%async_computation.1 | async-start | bytes 819200 | tf_op jit(solution)/shard_map/all_to_all | solution.py:173
  222.3 30.6 %copy-start.5 = (f32[4,3,2,512]{3,2,1,0:T(2,128)S(1)}, f32[4,3,2,512]{3,2,1,0:T(2,128)}, u32[]{:S(2)}) copy-start(f32[4,3,2,512]{3,2,1,0:T(2,128)} %param.25) | copy-start | bytes 147460
  250.0 27.5 %copy-start.10 = (s32[64]{0:T(128)S(1)}, s32[64]{0:T(128)}, u32[]{:S(2)}) copy-start(s32[64]{0:T(128)} %param.27) | copy-start | bytes 772
  253.7 7.2 %collective-permute-start = (bf16[1,4,3,2,512]{4,3,2,1,0:T(2,128)(2,1)S(1)}, bf16[1,4,3,2,512]{4,3,2,1,0:T(2,128)(2,1)S(1)}, u32[]{:S(2)}, u32[]{:S(2)}) collective-permute-start(bf16[1,4,3,2,512]{4,3,2,1,0:T(2,128)(2,1)S(1)} %get-tuple-element.82), channel_id=1, source_target_pairs={{0,1},{1,0},{2,3},{3,2},{4,5},{5,4},{6,7},{7,6},{256,257},{257,256... | collective-permute-start | bytes 73736 | tf_op jit(solution)/shard_map/ppermute | solution.py:47
  261.0 6.0 %collective-permute-start.1 = (bf16[2,4,3,2,512]{4,3,2,1,0:T(2,128)(2,1)S(1)}, bf16[2,4,3,2,512]{4,3,2,1,0:T(2,128)(2,1)S(1)}, u32[]{:S(2)}, u32[]{:S(2)}) collective-permute-start(bf16[2,4,3,2,512]{4,3,2,1,0:T(2,128)(2,1)S(1)} %broadcast_select_fusion.3), channel_id=1, source_target_pairs={{0,2},{1,3},{2,0},{3,1},{4,6},{5,7},{6,4},{7,5},{256,258},{257,259... | collective-permute-start | bytes 147464 | tf_op jit(solution)/shard_map/ppermute | solution.py:47
  267.2 8.0 %collective-permute-start.2 = (bf16[4,4,3,2,512]{4,3,2,1,0:T(2,128)(2,1)S(1)}, bf16[4,4,3,2,512]{4,3,2,1,0:T(2,128)(2,1)S(1)}, u32[]{:S(2)}, u32[]{:S(2)}) collective-permute-start(bf16[4,4,3,2,512]{4,3,2,1,0:T(2,128)(2,1)S(1)} %broadcast_select_fusion.2), channel_id=1, source_target_pairs={{0,4},{1,5},{2,6},{3,7},{4,0},{5,1},{6,2},{7,3},{256,260},{257,261... | collective-permute-start | bytes 294920 | tf_op jit(solution)/shard_map/ppermute | solution.py:47
  275.6 3.3 collective-permute-start.3
  280.6 5.0 %collective-permute-start.4 = (bf16[4,3,1,512]{3,2,1,0:T(2,128)(2,1)S(1)}, bf16[4,3,1,512]{3,2,1,0:T(2,128)(2,1)S(1)}, u32[]{:S(2)}, u32[]{:S(2)}) collective-permute-start(bf16[4,3,1,512]{3,2,1,0:T(2,128)(2,1)S(1)} %get-tuple-element.95), channel_id=1, source_target_pairs={{0,8},{8,16},{16,24},{24,32},{32,40},{40,48},{48,56},{56,64},{64,7... | collective-permute-start | bytes 36872 | tf_op jit(solution)/shard_map/ppermute | solution.py:32
  284.1 5.7 %collective-permute-start.5 = (bf16[4,3,1,512]{3,2,1,0:T(2,128)(2,1)S(1)}, bf16[4,3,1,512]{3,2,1,0:T(2,128)(2,1)S(1)}, u32[]{:S(2)}, u32[]{:S(2)}) collective-permute-start(bf16[4,3,1,512]{3,2,1,0:T(2,128)(2,1)S(1)} %get-tuple-element.96), channel_id=1, source_target_pairs={{8,0},{16,8},{24,16},{32,24},{40,32},{48,40},{56,48},{64,56},{72,6... | collective-permute-start | bytes 36872 | tf_op jit(solution)/shard_map/ppermute | solution.py:34
  318.1 2.5 copy-start.11
  322.3 1.2 copy-start.1
  325.1 25.5 %copy-start.7 = (f32[512]{0:T(512)S(1)}, f32[512]{0:T(512)}, u32[]{:S(2)}) copy-start(f32[512]{0:T(512)} %param.31) | copy-start | bytes 6148
  327.8 32.4 %copy-start.8 = (f32[512]{0:T(512)S(1)}, f32[512]{0:T(512)}, u32[]{:S(2)}) copy-start(f32[512]{0:T(512)} %param.30) | copy-start | bytes 6148
  329.3 5.5 %collective-permute-start.6 = (f32[2,4,32]{2,1,0:T(4,128)S(1)}, f32[2,4,32]{2,1,0:T(4,128)S(1)}, u32[]{:S(2)}, u32[]{:S(2)}) collective-permute-start(f32[2,4,32]{2,1,0:T(4,128)S(1)} %pad_maximum_fusion.10), channel_id=1, source_target_pairs={{0,8},{8,0},{16,24},{24,16},{32,40},{40,32},{48,56},{56,48},{64,72... | collective-permute-start | bytes 3080 | tf_op jit(solution)/shard_map/ppermute | solution.py:62
  334.8 5.5 %collective-permute-start.7 = (f32[2,4,32]{2,1,0:T(4,128)S(1)}, f32[2,4,32]{2,1,0:T(4,128)S(1)}, u32[]{:S(2)}, u32[]{:S(2)}) collective-permute-start(f32[2,4,32]{2,1,0:T(4,128)S(1)} %pad_maximum_fusion.11), channel_id=1, source_target_pairs={{0,16},{8,24},{16,0},{24,8},{32,48},{40,56},{48,32},{56,40},{64,80... | collective-permute-start | bytes 3080 | tf_op jit(solution)/shard_map/ppermute | solution.py:62
  340.3 6.4 %collective-permute-start.8 = (f32[2,4,32]{2,1,0:T(4,128)S(1)}, f32[2,4,32]{2,1,0:T(4,128)S(1)}, u32[]{:S(2)}, u32[]{:S(2)}) collective-permute-start(f32[2,4,32]{2,1,0:T(4,128)S(1)} %pad_maximum_fusion.12), channel_id=1, source_target_pairs={{0,32},{8,40},{16,48},{24,56},{32,0},{40,8},{48,16},{56,24},{64,96... | collective-permute-start | bytes 3080 | tf_op jit(solution)/shard_map/ppermute | solution.py:62
  346.7 9.4 %collective-permute-start.9 = (f32[2,4,32]{2,1,0:T(4,128)S(1)}, f32[2,4,32]{2,1,0:T(4,128)S(1)}, u32[]{:S(2)}, u32[]{:S(2)}) collective-permute-start(f32[2,4,32]{2,1,0:T(4,128)S(1)} %pad_maximum_fusion.13), channel_id=1, source_target_pairs={{0,64},{8,72},{16,80},{24,88},{32,96},{40,104},{48,112},{56,120},{... | collective-permute-start | bytes 3080 | tf_op jit(solution)/shard_map/ppermute | solution.py:62
  356.1 14.2 %collective-permute-start.10 = (f32[2,4,32]{2,1,0:T(4,128)S(1)}, f32[2,4,32]{2,1,0:T(4,128)S(1)}, u32[]{:S(2)}, u32[]{:S(2)}) collective-permute-start(f32[2,4,32]{2,1,0:T(4,128)S(1)} %pad_maximum_fusion.14), channel_id=1, source_target_pairs={{0,128},{8,136},{16,144},{24,152},{32,160},{40,168},{48,176},{56,1... | collective-permute-start | bytes 3080 | tf_op jit(solution)/shard_map/ppermute | solution.py:62

commit v3 on v2

--- a/solution.py
+++ b/solution.py
@@ -36,6 +36,12 @@
             axis=dim,
         )
     return cells
+
+
+def gather_all(block, axis):
+    count = lax.axis_size(axis)
+    copies = jnp.broadcast_to(block[None], (count,) + block.shape)
+    return lax.all_to_all(copies, axis, 0, 0, tiled=True)
 
 
 def butterfly_gather(block, axis):
@@ -198,21 +204,32 @@
     decoder_in = denoised.astype(jnp.bfloat16)
     group_index = lax.axis_index(("sec", "rep"))
     wanted = lax.dynamic_slice_in_dim(clip_order, group_index * clips, clips)
-    everyone = butterfly_gather(decoder_in, ("sec", "rep"))
+    everyone = gather_all(decoder_in, ("sec", "rep"))
+    everyone = everyone.reshape((-1,) + decoder_in.shape[1:])
     picked = jnp.take(everyone, wanted, axis=0)
     rimmed = edge_rows(extended(picked, (("seq", 2),), 1))
-    columns = causal_columns(rimmed)
-    flat_weight = conv_weight.reshape(27 * LAT_CH, VAE_CH)
-    conv_out = (
-        jnp.dot(columns.reshape(-1, 27 * LAT_CH), flat_weight, preferred_element_type=jnp.float32)
-        + conv_bias
-    )
+    grid = rimmed.reshape(clips, FRAMES, rimmed.shape[2], LAT_W, LAT_CH)
+    first = grid[:, :1]
+    grid = jnp.concatenate([first, first, grid], axis=1)
+    grid = jnp.pad(grid, ((0, 0), (0, 0), (0, 0), (1, 1), (0, 0)), mode="edge")
+    conv_out = lax.conv_general_dilated(
+        grid,
+        conv_weight,
+        (1, 1, 1),
+        "VALID",
+        dimension_numbers=("NDHWC", "DHWIO", "NDHWC"),
+        preferred_element_type=jnp.float32,
+    )
+    conv_out = conv_out.reshape(clips, -1, VAE_CH) + conv_bias
     conv_out = conv_out.reshape(clips, -1, GROUPS, VAE_CH // GROUPS)
     count = conv_out.shape[1] * (VAE_CH // GROUPS)
     local_mean = jnp.sum(conv_out, axis=(1, 3)) / count
     centered_local = conv_out - local_mean[:, None, :, None]
     local_m2 = jnp.sum(jnp.square(centered_local), axis=(1, 3))
-    mean, m2 = butterfly_moments(local_mean, local_m2, count, "seq")
+    moments = gather_all(jnp.stack([local_mean, local_m2]), "seq")
+    means, m2s = moments[:, 0], moments[:, 1]
+    mean = jnp.mean(means, axis=0)
+    m2 = jnp.sum(m2s, axis=0) + count * jnp.sum(jnp.square(means - mean), axis=0)
     centered = conv_out - mean[:, None, :, None]
     spread = m2 / (count * n_seq)
     normed = (centered * lax.rsqrt(spread + eps_norm)[:, None, :, None]).reshape(clips, -1, VAE_CH)

time: 382 us -> 327 us (0.86)
  the two profiles are of different devices: /device:TPU:4 before, /device:TPU:8 now
where the time goes in v3:
time: 327 us
  waiting for transfers between devices  208 us (64%)
  starting transfers between devices  39.7 us (12%)
  local copies, waits for them, and re-layouts  36.9 us (11%)
  other arithmetic  21.7 us (7%)
  matrix products  18.3 us (6%)
    all_to_all x1, waiting for transfers between devices, shards(): lax.all_to_all(stacked, 'seq', split_axis=0, concat_axis=3, tiled=True)  161 us
    all_to_all x1, waiting for transfers between devices, shards(): lax.all_to_all(packed, 'seq', split_axis=0, concat_axis=0, tiled=True)  26.2 us
    all_to_all x2, waiting for transfers between devices, gather_all(): return lax.all_to_all(copies, axis, 0, 0, tiled=True)  18.4 us
    all_to_all x1, starting transfers between devices, shards(): lax.all_to_all(stacked, 'seq', split_axis=0, concat_axis=3, tiled=True)  16.8 us
    all_to_all x2, starting transfers between devices, gather_all(): return lax.all_to_all(copies, axis, 0, 0, tiled=True)  13.4 us
    dot_general x9, matrix products, one_block(): jnp.dot(weights, value_rows, preferred_element_type=jnp.float32)  6.97 us
  transfers between devices with their start and end apart: 6, of which 5 were waited for; matrix products, arithmetic and copies ran while one was open for 2% of the time, Pallas kernels for 0%

profile of v3, /device:TPU:8, one launch (start us, length us, event | category | flops | bytes accessed | tf_op | source)
XLA Modules:
  0.0 326.7 jit_solution(8435700189595449701)
XLA Ops:
  0.6 3.5 %pad_maximum_fusion = bf16[32,3,3,48,128]{4,3,2,1,0:T(8,128)(2,1)} fusion(bf16[32,1,3,48,128]{4,3,2,1,0:T(8,128)(2,1)} %bitcast.115, bf16[32,1,3,48,128]{4,3,2,1,0:T(8,128)(2,1)} %bitcast.116, bf16[32,1,3,48,128]{4,3,2,1,0:T(8,128)(2,1)} %bitcast.117), kind=kLoop, calls=%fused_computation.16 | loop fusion | flops 3538944 | bytes 7077888 | tf_op jit(solution)/shard_map/stack | solution.py:150
  4.1 16.8 %all-to-all-start = ((bf16[32,3,3,48,128]{4,3,2,1,0:T(8,128)(2,1)}), bf16[32,3,3,48,128]{4,3,2,1,0:T(8,128)(2,1)}, u32[]{:S(2)}, u32[]{:S(2)}) async-start(bf16[32,3,3,48,128]{4,3,2,1,0:T(8,128)(2,1)} %pad_maximum_fusion), calls=%async_computation | async-start | bytes 7077888 | tf_op jit(solution)/shard_map/all_to_all | solution.py:158
  20.9 1.4 add_reduce_fusion
  22.3 160.8 %all-to-all-done = bf16[32,3,3,48,128]{4,3,2,1,0:T(8,128)(2,1)} async-done(((bf16[32,3,3,48,128]{4,3,2,1,0:T(8,128)(2,1)}), bf16[32,3,3,48,128]{4,3,2,1,0:T(8,128)(2,1)}, u32[]{:S(2)}, u32[]{:S(2)}) %all-to-all-start) | async-done | bytes 3538976 | tf_op jit(solution)/shard_map/all_to_all | solution.py:158
  183.1 2.7 copy.101
  185.8 1.8 slice_bitcast_fusion.1
  187.6 25.6 %while.21 = (s32[]{:T(128)}, bf16[3,1536,128]{1,2,0:T(8,128)(2,1)S(1)}, bf16[3,1536,128]{2,1,0:T(8,128)(2,1)}, bf16[3,1536,128]{2,1,0:T(8,128)(2,1)}, bf16[3,153...) while((s32[]{:T(128)}, bf16[3,1536,128]{1,2,0:T(8,128)(2,1)S(1)}, ...), condition=%wide.region_5.6_spmd, body=%wide.region_0.5_spmd.sunk | while | flops 408222720 | bytes 14428406 | solution.py:159
  187.6 1.0 constant_dynamic-slice_fusion.2
  188.7 1.2 dynamic-slice_bitcast_fusion.3
  189.8 6.1 %while.22 = (s32[]{:T(128)}, bf16[3,512,128]{2,1,0:T(8,128)(2,1)S(1)}, bf16[3,512,128]{2,1,0:T(8,128)(2,1)S(1)}, bf16[1536,128]{1,0:T(8,128)(2,1)S(1)}, bf16[1536,128]{1,0:T(8,128)(2,1)S(1)}, /*index=5*/s32[]{:T(128)}) while((s32[]{:T(128)}, bf16[3,512,128]{2,1,0:T(8,128)(2,1)S(1)}, bf16[3,512,128]{2,1,0:T(8,128)(2,1)S(1)}, ...), condition=%wide.region_4.4_spmd, body=%wide.region_1.3_spmd.sunk | while | flops 408222720 | bytes 10496085 | solution.py:91
  189.8 0.7 fusion.52
  191.1 0.8 fusion.54
  191.9 0.7 fusion.52
  193.1 0.8 fusion.54
  193.9 0.7 fusion.52
  195.1 0.8 fusion.54
  196.1 1.0 constant_dynamic-slice_fusion.2
  197.2 1.2 dynamic-slice_bitcast_fusion.3
  198.4 6.1 %while.22 = (s32[]{:T(128)}, bf16[3,512,128]{2,1,0:T(8,128)(2,1)S(1)}, bf16[3,512,128]{2,1,0:T(8,128)(2,1)S(1)}, bf16[1536,128]{1,0:T(8,128)(2,1)S(1)}, bf16[1536,128]{1,0:T(8,128)(2,1)S(1)}, /*index=5*/s32[]{:T(128)}) while((s32[]{:T(128)}, bf16[3,512,128]{2,1,0:T(8,128)(2,1)S(1)}, bf16[3,512,128]{2,1,0:T(8,128)(2,1)S(1)}, ...), condition=%wide.region_4.4_spmd, body=%wide.region_1.3_spmd.sunk | while | flops 408222720 | bytes 10496085 | solution.py:91
  198.4 0.7 fusion.52
  199.6 0.8 fusion.54
  200.4 0.7 fusion.52
  201.6 0.8 fusion.54
  202.4 0.7 fusion.52
  203.6 0.8 fusion.54
  204.7 1.0 constant_dynamic-slice_fusion.2
  205.7 1.2 dynamic-slice_bitcast_fusion.3
  206.9 6.1 %while.22 = (s32[]{:T(128)}, bf16[3,512,128]{2,1,0:T(8,128)(2,1)S(1)}, bf16[3,512,128]{2,1,0:T(8,128)(2,1)S(1)}, bf16[1536,128]{1,0:T(8,128)(2,1)S(1)}, bf16[1536,128]{1,0:T(8,128)(2,1)S(1)}, /*index=5*/s32[]{:T(128)}) while((s32[]{:T(128)}, bf16[3,512,128]{2,1,0:T(8,128)(2,1)S(1)}, bf16[3,512,128]{2,1,0:T(8,128)(2,1)S(1)}, ...), condition=%wide.region_4.4_spmd, body=%wide.region_1.3_spmd.sunk | while | flops 408222720 | bytes 10496085 | solution.py:91
  206.9 0.7 fusion.52
  208.1 0.8 fusion.54
  208.9 0.7 fusion.52
  210.1 0.8 fusion.54
  210.9 0.7 fusion.52
  212.2 0.8 fusion.54
  214.1 0.7 copy-done.2
  214.7 1.6 fusion.21
  216.7 1.8 all_to_all.33
  218.5 3.7 %all-to-all-start.1 = ((f32[32,1,3168]{2,1,0:T(1,128)}), f32[32,1,3168]{2,1,0:T(1,128)S(1)}, u32[]{:S(2)}, u32[]{:S(2)}) async-start(f32[32,1,3168]{2,1,0:T(1,128)} %all_to_all.33), calls=%async_computation.1 | async-start | bytes 819200 | tf_op jit(solution)/shard_map/all_to_all | solution.py:179
  223.2 26.2 %all-to-all-done.1 = f32[32,1,3168]{2,1,0:T(1,128)S(1)} async-done(((f32[32,1,3168]{2,1,0:T(1,128)}), f32[32,1,3168]{2,1,0:T(1,128)S(1)}, u32[]{:S(2)}, u32[]{:S(2)}) %all-to-all-start.1) | async-done | bytes 405536 | tf_op jit(solution)/shard_map/all_to_all | solution.py:179
  249.4 1.0 reduce.14
  251.0 0.8 slice_reduce_fusion.4
  253.3 0.7 fusion.33
  254.1 0.9 broadcast_in_dim.33
  255.0 6.1 %all-to-all-start.2 = ((bf16[16,4,3,2,512]{4,3,2,1,0:T(2,128)(2,1)}), bf16[16,4,3,2,512]{4,3,2,1,0:T(2,128)(2,1)S(1)}, u32[]{:S(2)}, u32[]{:S(2)}) async-start(bf16[16,4,3,2,512]{4,3,2,1,0:T(2,128)(2,1)} %broadcast_in_dim.33), calls=%async_computation.2 | async-start | bytes 786432 | tf_op jit(solution)/shard_map/all_to_all | solution.py:44
  261.3 10.8 %all-to-all-done.2 = bf16[16,4,3,2,512]{4,3,2,1,0:T(2,128)(2,1)S(1)} async-done(((bf16[16,4,3,2,512]{4,3,2,1,0:T(2,128)(2,1)}), bf16[16,4,3,2,512]{4,3,2,1,0:T(2,128)(2,1)S(1)}, u32[]{:S(2)}, u32[]{:S(2)}) %all-to-all-start.2) | async-done | bytes 393248 | tf_op jit(solution)/shard_map/all_to_all | solution.py:44
  272.1 0.6 gather_fusion
  272.8 2.4 collective-permute-start
  275.3 3.4 %collective-permute-start.1 = (bf16[4,3,1,512]{3,2,1,0:T(2,128)(2,1)S(1)}, bf16[4,3,1,512]{3,2,1,0:T(2,128)(2,1)S(1)}, u32[]{:S(2)}, u32[]{:S(2)}) collective-permute-start(bf16[4,3,1,512]{3,2,1,0:T(2,128)(2,1)S(1)} %get-tuple-element.98), channel_id=1, source_target_pairs={{8,0},{16,8},{24,16},{32,24},{40,32},{48,40},{56,48},{64,56},{72,6... | collective-permute-start | bytes 36872 | tf_op jit(solution)/shard_map/ppermute | solution.py:34
  278.8 3.1 collective-permute-done.1
  284.4 0.7 copy.129
  285.6 0.6 fusion.13
  286.3 2.6 broadcast_add_fusion
  288.9 1.5 copy.116
  292.2 1.5 copy.118
  294.3 0.8 reshape.184
  295.0 7.3 %all-to-all-start.3 = ((f32[32,1,256]{2,1,0:T(1,128)}), f32[32,1,256]{2,1,0:T(1,128)S(1)}, u32[]{:S(2)}, u32[]{:S(2)}) async-start(f32[32,1,256]{2,1,0:T(1,128)} %reshape.184), calls=%async_computation.3 | async-start | bytes 65536 | tf_op jit(solution)/shard_map/all_to_all | solution.py:44
  302.3 1.5 copy.114
  303.9 0.6 slice_bitcast_fusion
  304.8 2.5 reshape.154
  307.2 7.6 %all-to-all-done.3 = f32[32,1,256]{2,1,0:T(1,128)S(1)} async-done(((f32[32,1,256]{2,1,0:T(1,128)}), f32[32,1,256]{2,1,0:T(1,128)S(1)}, u32[]{:S(2)}, u32[]{:S(2)}) %all-to-all-start.3) | async-done | bytes 32800 | tf_op jit(solution)/shard_map/all_to_all | solution.py:44
  315.3 0.7 reduce.18
  316.7 2.5 mul.119
  319.6 2.5 sub.96
  322.0 4.6 %fusion.12 = bf16[4,3,2,16384]{3,2,1,0:T(2,128)(2,1)} fusion(f32[4,3,2,16384]{3,2,1,0:T(2,128)} %mul.119, f32[4,3,2,16384]{3,2,1,0:T(2,128)} %sub.96, f32[4,3,2,16384]{3,2,1,0:T(2,128)} %reshape.154, f32[16384]{0:T(1024)S(1)} %bitcast.119, f32[16384]{0:T(1024)S(1)} %bitcast.120, f32[16384]{0:T(1024)S(1)} %bitcast.121), kind=kLoop, calls=%fused_computation.29 | loop fusion | flops 3932160 | bytes 5701632 | tf_op jit(solution)/shard_map/convert_element_type | solution.py:236
  (116 shorter events, 17.3 us)
Async XLA Ops:
  0.6 285.6 %copy-start = (bf16[3,3,3,16,512]{4,3,2,1,0:T(8,128)(2,1)S(1)}, bf16[3,3,3,16,512]{4,3,2,1,0:T(8,128)(2,1)}, u32[]{:S(2)}) copy-start(bf16[3,3,3,16,512]{4,3,2,1,0:T(8,128)(2,1)} %param.28) | copy-start | bytes 1327108
  4.1 178.9 %all-to-all-start = ((bf16[32,3,3,48,128]{4,3,2,1,0:T(8,128)(2,1)}), bf16[32,3,3,48,128]{4,3,2,1,0:T(8,128)(2,1)}, u32[]{:S(2)}, u32[]{:S(2)}) async-start(bf16[32,3,3,48,128]{4,3,2,1,0:T(8,128)(2,1)} %pad_maximum_fusion), calls=%async_computation | async-start | bytes 7077888 | tf_op jit(solution)/shard_map/all_to_all | solution.py:158
  213.7 1.0 copy-start.2
  213.7 1.0 copy-start.6
  216.4 5.8 %copy-start.12 = (s32[4]{0:T(128)S(1)}, s32[4]{0:T(128)}, u32[]{:S(2)}) copy-start(s32[4]{0:T(128)} %param.26) | copy-start | bytes 52
  216.4 5.8 %copy-start.7 = (f32[512]{0:T(512)S(1)}, f32[512]{0:T(512)}, u32[]{:S(2)}) copy-start(f32[512]{0:T(512)} %param.31) | copy-start | bytes 6148
  216.4 5.8 %copy-start.4 = (f32[4,3072]{1,0:T(4,128)S(1)}, f32[4,3072]{1,0:T(4,128)}, u32[]{:S(2)}) copy-start(f32[4,3072]{1,0:T(4,128)} %param.21) | copy-start | bytes 147460
  216.4 6.2 %copy-start.3 = (f32[4,3072]{1,0:T(4,128)S(1)}, f32[4,3072]{1,0:T(4,128)}, u32[]{:S(2)}) copy-start(f32[4,3072]{1,0:T(4,128)} %param.22) | copy-start | bytes 147460
  218.5 30.9 %all-to-all-start.1 = ((f32[32,1,3168]{2,1,0:T(1,128)}), f32[32,1,3168]{2,1,0:T(1,128)S(1)}, u32[]{:S(2)}, u32[]{:S(2)}) async-start(f32[32,1,3168]{2,1,0:T(1,128)} %all_to_all.33), calls=%async_computation.1 | async-start | bytes 819200 | tf_op jit(solution)/shard_map/all_to_all | solution.py:179
  250.3 1.5 copy-start.10
  251.0 2.3 copy-start.5
  252.2 8.9 %copy-start.11 = (s32[64]{0:T(128)S(1)}, s32[64]{0:T(128)}, u32[]{:S(2)}) copy-start(s32[64]{0:T(128)} %param.27) | copy-start | bytes 772
  252.3 9.0 %copy-start.8 = (f32[512]{0:T(512)S(1)}, f32[512]{0:T(512)}, u32[]{:S(2)}) copy-start(f32[512]{0:T(512)} %param.30) | copy-start | bytes 6148
  252.3 26.4 %copy-start.9 = (f32[512]{0:T(512)S(1)}, f32[512]{0:T(512)}, u32[]{:S(2)}) copy-start(f32[512]{0:T(512)} %param.29) | copy-start | bytes 6148
  255.0 17.1 %all-to-all-start.2 = ((bf16[16,4,3,2,512]{4,3,2,1,0:T(2,128)(2,1)}), bf16[16,4,3,2,512]{4,3,2,1,0:T(2,128)(2,1)S(1)}, u32[]{:S(2)}, u32[]{:S(2)}) async-start(bf16[16,4,3,2,512]{4,3,2,1,0:T(2,128)(2,1)} %broadcast_in_dim.33), calls=%async_computation.2 | async-start | bytes 786432 | tf_op jit(solution)/shard_map/all_to_all | solution.py:44
  272.8 6.0 %collective-permute-start = (bf16[4,3,1,512]{3,2,1,0:T(2,128)(2,1)S(1)}, bf16[4,3,1,512]{3,2,1,0:T(2,128)(2,1)S(1)}, u32[]{:S(2)}, u32[]{:S(2)}) collective-permute-start(bf16[4,3,1,512]{3,2,1,0:T(2,128)(2,1)S(1)} %get-tuple-element.97), channel_id=1, source_target_pairs={{0,8},{8,16},{16,24},{24,32},{32,40},{40,48},{48,56},{56,64},{64,7... | collective-permute-start | bytes 36872 | tf_op jit(solution)/shard_map/ppermute | solution.py:32
  275.3 6.6 %collective-permute-start.1 = (bf16[4,3,1,512]{3,2,1,0:T(2,128)(2,1)S(1)}, bf16[4,3,1,512]{3,2,1,0:T(2,128)(2,1)S(1)}, u32[]{:S(2)}, u32[]{:S(2)}) collective-permute-start(bf16[4,3,1,512]{3,2,1,0:T(2,128)(2,1)S(1)} %get-tuple-element.98), channel_id=1, source_target_pairs={{8,0},{16,8},{24,16},{32,24},{40,32},{48,40},{56,48},{64,56},{72,6... | collective-permute-start | bytes 36872 | tf_op jit(solution)/shard_map/ppermute | solution.py:34
  285.5 0.7 copy-start.13
  293.7 8.6 %copy-start.1 = (f32[3,2,32,5,512]{4,2,3,1,0:T(8,128)S(1)}, f32[3,2,32,5,512]{4,2,3,1,0:T(8,128)}, u32[]{:S(2)}) copy-start(f32[3,2,32,5,512]{4,2,3,1,0:T(8,128)} %get-tuple-element.102) | copy-start | bytes 5898244
  295.0 19.8 %all-to-all-start.3 = ((f32[32,1,256]{2,1,0:T(1,128)}), f32[32,1,256]{2,1,0:T(1,128)S(1)}, u32[]{:S(2)}, u32[]{:S(2)}) async-start(f32[32,1,256]{2,1,0:T(1,128)} %reshape.184), calls=%async_computation.3 | async-start | bytes 65536 | tf_op jit(solution)/shard_map/all_to_all | solution.py:44

commit v4 on v3

--- a/solution.py
+++ b/solution.py
@@ -147,16 +147,17 @@
     clips = head_query.shape[0]
     tok_dev = head_query.shape[2]
     units_local = clips * HEADS // n_seq
-    stacked = jnp.stack(
-        [
-            head_query.reshape(n_seq, units_local, tok_dev, HEAD_DIM),
-            head_keys.reshape(n_seq, units_local, tok_dev, HEAD_DIM),
-            head_values.reshape(n_seq, units_local, tok_dev, HEAD_DIM),
-        ],
-        axis=1,
-    )
-    parts = lax.all_to_all(stacked, "seq", split_axis=0, concat_axis=3, tiled=True)
-    outputs = lax.map(attend_unit, (parts[0, 0], parts[0, 1], parts[0, 2]))
+    query_four = head_query.reshape(n_seq, units_local, tok_dev, HEAD_DIM)
+    keys_four = head_keys.reshape(n_seq, units_local, tok_dev, HEAD_DIM)
+    values_four = head_values.reshape(n_seq, units_local, tok_dev, HEAD_DIM)
+    attended = []
+    for unit in range(units_local):
+        stacked = jnp.stack(
+            [query_four[:, unit], keys_four[:, unit], values_four[:, unit]], axis=1
+        )
+        part = lax.all_to_all(stacked, "seq", split_axis=0, concat_axis=2, tiled=True)
+        attended.append(attend_unit((part[0, 0], part[0, 1], part[0, 2])))
+    outputs = jnp.stack(attended)
     seq_len = outputs.shape[1]
     chunks = HEADS // units_local
     width = units_local * HEAD_DIM

time: 327 us -> 353 us (1.080)
  starting transfers between devices: 39.7 us -> 63 us
  other arithmetic: 21.7 us -> 25.9 us
  local copies, waits for them, and re-layouts: 36.9 us -> 32.7 us
    all_to_all x1, starting transfers between devices: 3.67 us -> 15.5 us  [shards(): lax.all_to_all(packed, 'seq', split_axis=0, concat_axis=0, tiled=True)]
    all_to_all x1 -> x3, starting transfers between devices: 16.8 us -> 28.2 us  [shards(): lax.all_to_all(stacked, 'seq', split_axis=0, concat_axis=2, tiled=True)]
    squeeze x4 -> x3, local copies, waits for them, and re-layouts: 5.37 us -> 0.24 us  [shards(): attended.append(attend_unit((part[0, 0], part[0, 1], part[0, 2])))]
    all_to_all x1 -> x3, waiting for transfers between devices: 161 us -> 160 us  [shards(): lax.all_to_all(stacked, 'seq', split_axis=0, concat_axis=2, tiled=True)]
  transfers between devices with their start and end apart: 6 -> 8, of which waited for: 5 -> 7; matrix products, arithmetic and copies ran while one was open for 2% -> 7% of each run, Pallas kernels for 0% -> 0%
where the time goes in v4:
time: 353 us; the launch traced here: 349 us
  waiting for transfers between devices  208 us (59%)
  starting transfers between devices  63 us (18%)
  local copies, waits for them, and re-layouts  32.7 us (9%)
  other arithmetic  25.9 us (7%)
  matrix products  18.3 us (5%)
    all_to_all x3, waiting for transfers between devices, shards(): lax.all_to_all(stacked, 'seq', split_axis=0, concat_axis=2, tiled=True)  160 us
    all_to_all x3, starting transfers between devices, shards(): lax.all_to_all(stacked, 'seq', split_axis=0, concat_axis=2, tiled=True)  28.2 us
    all_to_all x1, waiting for transfers between devices, shards(): lax.all_to_all(packed, 'seq', split_axis=0, concat_axis=0, tiled=True)  26.5 us
    all_to_all x2, waiting for transfers between devices, gather_all(): return lax.all_to_all(copies, axis, 0, 0, tiled=True)  18.4 us
    all_to_all x1, starting transfers between devices, shards(): lax.all_to_all(packed, 'seq', split_axis=0, concat_axis=0, tiled=True)  15.5 us
    all_to_all x2, starting transfers between devices, gather_all(): return lax.all_to_all(copies, axis, 0, 0, tiled=True)  13.5 us
  transfers between devices with their start and end apart: 8, of which 7 were waited for; matrix products, arithmetic and copies ran while one was open for 7% of the time, Pallas kernels for 0%

profile of v4, /device:TPU:8, one launch (start us, length us, event | category | flops | bytes accessed | tf_op | source)
XLA Modules:
  0.0 349.3 jit_solution(15835245280664226745)
XLA Ops:
  0.7 1.5 fusion.53
  2.7 1.3 fusion.51
  4.0 1.2 pad_maximum_fusion.2
  5.1 16.7 %all-to-all-start.2 = ((bf16[32,3,48,128]{3,2,1,0:T(8,128)(2,1)}), bf16[32,3,48,128]{3,2,1,0:T(8,128)(2,1)S(1)}, u32[]{:S(2)}, u32[]{:S(2)}) async-start(bf16[32,3,48,128]{3,2,1,0:T(8,128)(2,1)} %pad_maximum_fusion.2), calls=%async_computation.2 | async-start | bytes 2359296 | tf_op jit(solution)/shard_map/all_to_all | solution.py:158
  21.8 2.1 pad_maximum_fusion.1
  24.0 56.9 %all-to-all-done.2 = bf16[32,3,48,128]{3,2,1,0:T(8,128)(2,1)S(1)} async-done(((bf16[32,3,48,128]{3,2,1,0:T(8,128)(2,1)}), bf16[32,3,48,128]{3,2,1,0:T(8,128)(2,1)S(1)}, u32[]{:S(2)}, u32[]{:S(2)}) %all-to-all-start.2) | async-done | bytes 1179680 | tf_op jit(solution)/shard_map/all_to_all | solution.py:158
  80.8 1.0 copy-done.3
  81.9 5.5 %all-to-all-start.1 = ((bf16[32,3,48,128]{3,2,1,0:T(8,128)(2,1)}), bf16[32,3,48,128]{3,2,1,0:T(8,128)(2,1)S(1)}, u32[]{:S(2)}, u32[]{:S(2)}) async-start(bf16[32,3,48,128]{3,2,1,0:T(8,128)(2,1)} %pad_maximum_fusion.1), calls=%async_computation.1 | async-start | bytes 2359296 | tf_op jit(solution)/shard_map/all_to_all | solution.py:158
  87.5 2.2 pad_maximum_fusion
  89.9 56.3 %all-to-all-done.1 = bf16[32,3,48,128]{3,2,1,0:T(8,128)(2,1)S(1)} async-done(((bf16[32,3,48,128]{3,2,1,0:T(8,128)(2,1)}), bf16[32,3,48,128]{3,2,1,0:T(8,128)(2,1)S(1)}, u32[]{:S(2)}, u32[]{:S(2)}) %all-to-all-start.1) | async-done | bytes 1179680 | tf_op jit(solution)/shard_map/all_to_all | solution.py:158
  146.2 6.0 %all-to-all-start = ((bf16[32,3,48,128]{3,2,1,0:T(8,128)(2,1)}), bf16[32,3,48,128]{3,2,1,0:T(8,128)(2,1)}, u32[]{:S(2)}, u32[]{:S(2)}) async-start(bf16[32,3,48,128]{3,2,1,0:T(8,128)(2,1)} %pad_maximum_fusion), calls=%async_computation | async-start | bytes 2359296 | tf_op jit(solution)/shard_map/all_to_all | solution.py:158
  152.3 6.1 %while.32 = (s32[]{:T(128)}, bf16[3,512,128]{2,1,0:T(8,128)(2,1)S(1)}, bf16[3,512,128]{2,1,0:T(8,128)(2,1)S(1)}, bf16[1536,128]{1,0:T(8,128)(2,1)S(1)}, bf16[1536,128]{1,0:T(8,128)(2,1)S(1)}, /*index=5*/s32[]{:T(128)}) while((s32[]{:T(128)}, bf16[3,512,128]{2,1,0:T(8,128)(2,1)S(1)}, bf16[3,512,128]{2,1,0:T(8,128)(2,1)S(1)}, ...), condition=%wide.region_11.12_spmd, body=%wide.region_8.11_spmd.sunk | while | flops 408222720 | bytes 10496085 | solution.py:91
  152.3 0.7 fusion.95
  153.5 0.8 fusion.97
  154.3 0.7 fusion.95
  155.5 0.8 fusion.97
  156.3 0.7 fusion.95
  157.5 0.8 fusion.97
  158.6 6.1 %while.31 = (s32[]{:T(128)}, bf16[3,512,128]{2,1,0:T(8,128)(2,1)S(1)}, bf16[3,512,128]{2,1,0:T(8,128)(2,1)S(1)}, bf16[1536,128]{1,0:T(8,128)(2,1)S(1)}, bf16[1536,128]{1,0:T(8,128)(2,1)S(1)}, /*index=5*/s32[]{:T(128)}) while((s32[]{:T(128)}, bf16[3,512,128]{2,1,0:T(8,128)(2,1)S(1)}, bf16[3,512,128]{2,1,0:T(8,128)(2,1)S(1)}, ...), condition=%wide.region_7.8_spmd, body=%wide.region_4.7_spmd.sunk | while | flops 408222720 | bytes 10496085 | solution.py:91
  158.6 0.7 fusion.90
  159.8 0.8 fusion.92
  160.6 0.7 fusion.90
  161.8 0.8 fusion.92
  162.6 0.7 fusion.90
  163.8 0.8 fusion.92
  164.6 46.3 %all-to-all-done = bf16[32,3,48,128]{3,2,1,0:T(8,128)(2,1)} async-done(((bf16[32,3,48,128]{3,2,1,0:T(8,128)(2,1)}), bf16[32,3,48,128]{3,2,1,0:T(8,128)(2,1)}, u32[]{:S(2)}, u32[]{:S(2)}) %all-to-all-start) | async-done | bytes 1179680 | tf_op jit(solution)/shard_map/all_to_all | solution.py:158
  211.0 1.3 copy.125
  212.5 6.1 %while.30 = (s32[]{:T(128)}, bf16[3,512,128]{2,1,0:T(8,128)(2,1)S(1)}, bf16[3,512,128]{2,1,0:T(8,128)(2,1)S(1)}, bf16[1536,128]{1,0:T(8,128)(2,1)S(1)}, bf16[1536,128]{1,0:T(8,128)(2,1)S(1)}, /*index=5*/s32[]{:T(128)}) while((s32[]{:T(128)}, bf16[3,512,128]{2,1,0:T(8,128)(2,1)S(1)}, bf16[3,512,128]{2,1,0:T(8,128)(2,1)S(1)}, ...), condition=%wide.region_3.4_spmd, body=%wide.region_0.3_spmd.sunk | while | flops 408222720 | bytes 10496085 | solution.py:91
  212.5 0.7 fusion.85
  213.7 0.8 fusion.87
  214.5 0.7 fusion.85
  215.7 0.8 fusion.87
  216.5 0.7 fusion.85
  217.7 0.8 fusion.87
  218.8 0.7 multiply_reduce_fusion
  219.5 1.3 convert_bitcast_fusion
  220.9 2.0 copy.128
  222.9 2.0 bitcast_subtract_fusion
  224.9 1.6 fusion.35
  226.9 1.8 all_to_all.67
  228.7 15.5 %all-to-all-start.3 = ((f32[32,1,3168]{2,1,0:T(1,128)}), f32[32,1,3168]{2,1,0:T(1,128)S(1)}, u32[]{:S(2)}, u32[]{:S(2)}) async-start(f32[32,1,3168]{2,1,0:T(1,128)} %all_to_all.67), calls=%async_computation.3 | async-start | bytes 819200 | tf_op jit(solution)/shard_map/all_to_all | solution.py:180
  245.2 26.5 %all-to-all-done.3 = f32[32,1,3168]{2,1,0:T(1,128)S(1)} async-done(((f32[32,1,3168]{2,1,0:T(1,128)}), f32[32,1,3168]{2,1,0:T(1,128)S(1)}, u32[]{:S(2)}, u32[]{:S(2)}) %all-to-all-start.3) | async-done | bytes 405536 | tf_op jit(solution)/shard_map/all_to_all | solution.py:180
  271.7 1.0 reduce.14
  273.3 0.8 slice_reduce_fusion.4
  275.6 0.7 fusion.47
  276.3 0.9 broadcast_in_dim.36
  277.3 6.1 %all-to-all-start.4 = ((bf16[16,4,3,2,512]{4,3,2,1,0:T(2,128)(2,1)}), bf16[16,4,3,2,512]{4,3,2,1,0:T(2,128)(2,1)S(1)}, u32[]{:S(2)}, u32[]{:S(2)}) async-start(bf16[16,4,3,2,512]{4,3,2,1,0:T(2,128)(2,1)} %broadcast_in_dim.36), calls=%async_computation.4 | async-start | bytes 786432 | tf_op jit(solution)/shard_map/all_to_all | solution.py:44
  283.6 10.8 %all-to-all-done.4 = bf16[16,4,3,2,512]{4,3,2,1,0:T(2,128)(2,1)S(1)} async-done(((bf16[16,4,3,2,512]{4,3,2,1,0:T(2,128)(2,1)}), bf16[16,4,3,2,512]{4,3,2,1,0:T(2,128)(2,1)S(1)}, u32[]{:S(2)}, u32[]{:S(2)}) %all-to-all-start.4) | async-done | bytes 393248 | tf_op jit(solution)/shard_map/all_to_all | solution.py:44
  295.1 2.5 collective-permute-start
  297.7 3.3 collective-permute-start.1
  301.1 3.2 collective-permute-done.1
  306.7 0.7 copy.151
  308.7 2.6 broadcast_add_fusion
  311.3 1.5 copy.142
  314.6 1.5 copy.144
  316.7 0.8 reshape.194
  317.4 7.3 %all-to-all-start.5 = ((f32[32,1,256]{2,1,0:T(1,128)}), f32[32,1,256]{2,1,0:T(1,128)S(1)}, u32[]{:S(2)}, u32[]{:S(2)}) async-start(f32[32,1,256]{2,1,0:T(1,128)} %reshape.194), calls=%async_computation.5 | async-start | bytes 65536 | tf_op jit(solution)/shard_map/all_to_all | solution.py:44
  324.8 1.5 copy.140
  327.2 2.5 reshape.164
  329.7 7.6 %all-to-all-done.5 = f32[32,1,256]{2,1,0:T(1,128)S(1)} async-done(((f32[32,1,256]{2,1,0:T(1,128)}), f32[32,1,256]{2,1,0:T(1,128)S(1)}, u32[]{:S(2)}, u32[]{:S(2)}) %all-to-all-start.5) | async-done | bytes 32800 | tf_op jit(solution)/shard_map/all_to_all | solution.py:44
  337.8 0.7 reduce.18
  339.1 2.5 mul.125
  342.0 2.5 sub.112
  344.5 4.6 %fusion.26 = bf16[4,3,2,16384]{3,2,1,0:T(2,128)(2,1)} fusion(f32[4,3,2,16384]{3,2,1,0:T(2,128)} %mul.125, f32[4,3,2,16384]{3,2,1,0:T(2,128)} %sub.112, f32[4,3,2,16384]{3,2,1,0:T(2,128)} %reshape.164, f32[16384]{0:T(1024)S(1)} %bitcast.176, f32[16384]{0:T(1024)S(1)} %bitcast.177, f32[16384]{0:T(1024)S(1)} %bitcast.178), kind=kLoop, calls=%fused_computation.46 | loop fusion | flops 3932160 | bytes 5701632 | tf_op jit(solution)/shard_map/convert_element_type | solution.py:237
  (126 shorter events, 19.1 us)
Async XLA Ops:
  0.6 308.0 %copy-start = (bf16[3,3,3,16,512]{4,3,2,1,0:T(8,128)(2,1)S(1)}, bf16[3,3,3,16,512]{4,3,2,1,0:T(8,128)(2,1)}, u32[]{:S(2)}) copy-start(bf16[3,3,3,16,512]{4,3,2,1,0:T(8,128)(2,1)} %param.30) | copy-start | bytes 1327108
  0.6 1.7 copy-start.7
  0.7 2.0 copy-start.8
  5.1 75.7 %all-to-all-start.2 = ((bf16[32,3,48,128]{3,2,1,0:T(8,128)(2,1)}), bf16[32,3,48,128]{3,2,1,0:T(8,128)(2,1)S(1)}, u32[]{:S(2)}, u32[]{:S(2)}) async-start(bf16[32,3,48,128]{3,2,1,0:T(8,128)(2,1)} %pad_maximum_fusion.2), calls=%async_computation.2 | async-start | bytes 2359296 | tf_op jit(solution)/shard_map/all_to_all | solution.py:158
  24.0 63.4 %copy-start.9 = (f32[4,3072]{1,0:T(4,128)S(1)}, f32[4,3072]{1,0:T(4,128)}, u32[]{:S(2)}) copy-start(f32[4,3072]{1,0:T(4,128)} %param.24) | copy-start | bytes 147460
  80.8 1.0 copy-start.3
  81.9 64.4 %all-to-all-start.1 = ((bf16[32,3,48,128]{3,2,1,0:T(8,128)(2,1)}), bf16[32,3,48,128]{3,2,1,0:T(8,128)(2,1)S(1)}, u32[]{:S(2)}, u32[]{:S(2)}) async-start(bf16[32,3,48,128]{3,2,1,0:T(8,128)(2,1)} %pad_maximum_fusion.1), calls=%async_computation.1 | async-start | bytes 2359296 | tf_op jit(solution)/shard_map/all_to_all | solution.py:158
  87.4 2.4 copy-start.4
  146.2 64.7 %all-to-all-start = ((bf16[32,3,48,128]{3,2,1,0:T(8,128)(2,1)}), bf16[32,3,48,128]{3,2,1,0:T(8,128)(2,1)}, u32[]{:S(2)}, u32[]{:S(2)}) async-start(bf16[32,3,48,128]{3,2,1,0:T(8,128)(2,1)} %pad_maximum_fusion), calls=%async_computation | async-start | bytes 2359296 | tf_op jit(solution)/shard_map/all_to_all | solution.py:158
  164.6 54.2 %copy-start.1 = (bf16[3,512,128]{2,1,0:T(8,128)(2,1)}, bf16[3,512,128]{2,1,0:T(8,128)(2,1)S(1)}, u32[]{:S(2)}) copy-start(bf16[3,512,128]{2,1,0:T(8,128)(2,1)S(1)} %get-tuple-element.84) | copy-start | bytes 1179652
  218.5 1.0 copy-start.2
  222.9 2.0 copy-start.6
  226.6 17.6 %copy-start.17 = (s32[4]{0:T(128)S(1)}, s32[4]{0:T(128)}, u32[]{:S(2)}) copy-start(s32[4]{0:T(128)} %param.28) | copy-start | bytes 52
  226.6 17.7 %copy-start.12 = (f32[512]{0:T(512)S(1)}, f32[512]{0:T(512)}, u32[]{:S(2)}) copy-start(f32[512]{0:T(512)} %param.33) | copy-start | bytes 6148
  226.6 17.7 %copy-start.10 = (f32[4,3072]{1,0:T(4,128)S(1)}, f32[4,3072]{1,0:T(4,128)}, u32[]{:S(2)}) copy-start(f32[4,3072]{1,0:T(4,128)} %param.23) | copy-start | bytes 147460
  228.7 43.0 %all-to-all-start.3 = ((f32[32,1,3168]{2,1,0:T(1,128)}), f32[32,1,3168]{2,1,0:T(1,128)S(1)}, u32[]{:S(2)}, u32[]{:S(2)}) async-start(f32[32,1,3168]{2,1,0:T(1,128)} %all_to_all.67), calls=%async_computation.3 | async-start | bytes 819200 | tf_op jit(solution)/shard_map/all_to_all | solution.py:180
  272.6 1.5 copy-start.15
  273.3 2.3 copy-start.11
  274.5 8.9 %copy-start.16 = (s32[64]{0:T(128)S(1)}, s32[64]{0:T(128)}, u32[]{:S(2)}) copy-start(s32[64]{0:T(128)} %param.29) | copy-start | bytes 772
  274.5 9.0 %copy-start.13 = (f32[512]{0:T(512)S(1)}, f32[512]{0:T(512)}, u32[]{:S(2)}) copy-start(f32[512]{0:T(512)} %param.32) | copy-start | bytes 6148
  274.6 26.4 %copy-start.14 = (f32[512]{0:T(512)S(1)}, f32[512]{0:T(512)}, u32[]{:S(2)}) copy-start(f32[512]{0:T(512)} %param.31) | copy-start | bytes 6148
  277.3 17.1 %all-to-all-start.4 = ((bf16[16,4,3,2,512]{4,3,2,1,0:T(2,128)(2,1)}), bf16[16,4,3,2,512]{4,3,2,1,0:T(2,128)(2,1)S(1)}, u32[]{:S(2)}, u32[]{:S(2)}) async-start(bf16[16,4,3,2,512]{4,3,2,1,0:T(2,128)(2,1)} %broadcast_in_dim.36), calls=%async_computation.4 | async-start | bytes 786432 | tf_op jit(solution)/shard_map/all_to_all | solution.py:44
  295.1 6.0 %collective-permute-start = (bf16[4,3,1,512]{3,2,1,0:T(2,128)(2,1)S(1)}, bf16[4,3,1,512]{3,2,1,0:T(2,128)(2,1)S(1)}, u32[]{:S(2)}, u32[]{:S(2)}) collective-permute-start(bf16[4,3,1,512]{3,2,1,0:T(2,128)(2,1)S(1)} %get-tuple-element.153), channel_id=1, source_target_pairs={{0,8},{8,16},{16,24},{24,32},{32,40},{40,48},{48,56},{56,64},{64,7... | collective-permute-start | bytes 36872 | tf_op jit(solution)/shard_map/ppermute | solution.py:32
  297.7 6.6 %collective-permute-start.1 = (bf16[4,3,1,512]{3,2,1,0:T(2,128)(2,1)S(1)}, bf16[4,3,1,512]{3,2,1,0:T(2,128)(2,1)S(1)}, u32[]{:S(2)}, u32[]{:S(2)}) collective-permute-start(bf16[4,3,1,512]{3,2,1,0:T(2,128)(2,1)S(1)} %get-tuple-element.154), channel_id=1, source_target_pairs={{8,0},{16,8},{24,16},{32,24},{40,32},{48,40},{56,48},{64,56},{72,6... | collective-permute-start | bytes 36872 | tf_op jit(solution)/shard_map/ppermute | solution.py:34
  307.9 0.7 copy-start.18
  316.1 8.6 %copy-start.5 = (f32[3,2,32,5,512]{4,2,3,1,0:T(8,128)S(1)}, f32[3,2,32,5,512]{4,2,3,1,0:T(8,128)}, u32[]{:S(2)}) copy-start(f32[3,2,32,5,512]{4,2,3,1,0:T(8,128)} %get-tuple-element.158) | copy-start | bytes 5898244
  317.4 19.8 %all-to-all-start.5 = ((f32[32,1,256]{2,1,0:T(1,128)}), f32[32,1,256]{2,1,0:T(1,128)S(1)}, u32[]{:S(2)}, u32[]{:S(2)}) async-start(f32[32,1,256]{2,1,0:T(1,128)} %reshape.194), calls=%async_computation.5 | async-start | bytes 65536 | tf_op jit(solution)/shard_map/all_to_all | solution.py:44

commit v5 on v3

--- a/solution.py
+++ b/solution.py
@@ -221,19 +221,23 @@
         preferred_element_type=jnp.float32,
     )
     conv_out = conv_out.reshape(clips, -1, VAE_CH) + conv_bias
-    conv_out = conv_out.reshape(clips, -1, GROUPS, VAE_CH // GROUPS)
-    count = conv_out.shape[1] * (VAE_CH // GROUPS)
-    local_mean = jnp.sum(conv_out, axis=(1, 3)) / count
-    centered_local = conv_out - local_mean[:, None, :, None]
-    local_m2 = jnp.sum(jnp.square(centered_local), axis=(1, 3))
+    group = VAE_CH // GROUPS
+    count = conv_out.shape[1] * group
+    chan_sum = jnp.sum(conv_out, axis=1)
+    local_mean = jnp.sum(chan_sum.reshape(clips, GROUPS, group), axis=2) / count
+    local_mean_c = jnp.repeat(local_mean, group, axis=1)
+    chan_m2 = jnp.sum(jnp.square(conv_out - local_mean_c[:, None, :]), axis=1)
+    local_m2 = jnp.sum(chan_m2.reshape(clips, GROUPS, group), axis=2)
     moments = gather_all(jnp.stack([local_mean, local_m2]), "seq")
     means, m2s = moments[:, 0], moments[:, 1]
     mean = jnp.mean(means, axis=0)
     m2 = jnp.sum(m2s, axis=0) + count * jnp.sum(jnp.square(means - mean), axis=0)
-    centered = conv_out - mean[:, None, :, None]
     spread = m2 / (count * n_seq)
-    normed = (centered * lax.rsqrt(spread + eps_norm)[:, None, :, None]).reshape(clips, -1, VAE_CH)
-    features = jax.nn.silu(normed * group_gain + group_shift).astype(jnp.bfloat16)
+    mean_c = jnp.repeat(mean, group, axis=1)
+    factor_c = jnp.repeat(lax.rsqrt(spread + eps_norm), group, axis=1) * group_gain
+    features = jax.nn.silu(
+        (conv_out - mean_c[:, None, :]) * factor_c[:, None, :] + group_shift
+    ).astype(jnp.bfloat16)
     features = features.reshape(clips, FRAMES, rows_dev, LAT_W * VAE_CH)
     return (denoised, features)
 

time: 327 us -> 327 us (level)
  no operation moved by 1% of the time
where the time goes in v5:
time: 327 us
  waiting for transfers between devices  208 us (64%)
  starting transfers between devices  39.7 us (12%)
  local copies, waits for them, and re-layouts  36.8 us (11%)
  other arithmetic  21.5 us (7%)
  matrix products  18.3 us (6%)
    all_to_all x1, waiting for transfers between devices, shards(): lax.all_to_all(stacked, 'seq', split_axis=0, concat_axis=3, tiled=True)  161 us
    all_to_all x1, waiting for transfers between devices, shards(): lax.all_to_all(packed, 'seq', split_axis=0, concat_axis=0, tiled=True)  26.2 us
    all_to_all x2, waiting for transfers between devices, gather_all(): return lax.all_to_all(copies, axis, 0, 0, tiled=True)  18.4 us
    all_to_all x1, starting transfers between devices, shards(): lax.all_to_all(stacked, 'seq', split_axis=0, concat_axis=3, tiled=True)  16.8 us
    all_to_all x2, starting transfers between devices, gather_all(): return lax.all_to_all(copies, axis, 0, 0, tiled=True)  13.4 us
    dot_general x9, matrix products, one_block(): jnp.dot(weights, value_rows, preferred_element_type=jnp.float32)  6.97 us
  transfers between devices with their start and end apart: 6, of which 5 were waited for; matrix products, arithmetic and copies ran while one was open for 2% of the time, Pallas kernels for 0%

profile of v5, /device:TPU:8, one launch (start us, length us, event | category | flops | bytes accessed | tf_op | source)
XLA Modules:
  0.0 326.5 jit_solution(1763658307007625055)
XLA Ops:
  0.6 3.5 %pad_maximum_fusion = bf16[32,3,3,48,128]{4,3,2,1,0:T(8,128)(2,1)} fusion(bf16[32,1,3,48,128]{4,3,2,1,0:T(8,128)(2,1)} %bitcast.112, bf16[32,1,3,48,128]{4,3,2,1,0:T(8,128)(2,1)} %bitcast.113, bf16[32,1,3,48,128]{4,3,2,1,0:T(8,128)(2,1)} %bitcast.114), kind=kLoop, calls=%fused_computation.16 | loop fusion | flops 3538944 | bytes 7077888 | tf_op jit(solution)/shard_map/stack | solution.py:150
  4.1 16.8 %all-to-all-start = ((bf16[32,3,3,48,128]{4,3,2,1,0:T(8,128)(2,1)}), bf16[32,3,3,48,128]{4,3,2,1,0:T(8,128)(2,1)}, u32[]{:S(2)}, u32[]{:S(2)}) async-start(bf16[32,3,3,48,128]{4,3,2,1,0:T(8,128)(2,1)} %pad_maximum_fusion), calls=%async_computation | async-start | bytes 7077888 | tf_op jit(solution)/shard_map/all_to_all | solution.py:158
  20.9 1.4 add_reduce_fusion
  22.3 160.8 %all-to-all-done = bf16[32,3,3,48,128]{4,3,2,1,0:T(8,128)(2,1)} async-done(((bf16[32,3,3,48,128]{4,3,2,1,0:T(8,128)(2,1)}), bf16[32,3,3,48,128]{4,3,2,1,0:T(8,128)(2,1)}, u32[]{:S(2)}, u32[]{:S(2)}) %all-to-all-start) | async-done | bytes 3538976 | tf_op jit(solution)/shard_map/all_to_all | solution.py:158
  183.1 2.7 copy.101
  185.8 1.8 slice_bitcast_fusion.1
  187.6 25.6 %while.21 = (s32[]{:T(128)}, bf16[3,1536,128]{1,2,0:T(8,128)(2,1)S(1)}, bf16[3,1536,128]{2,1,0:T(8,128)(2,1)}, bf16[3,1536,128]{2,1,0:T(8,128)(2,1)}, bf16[3,153...) while((s32[]{:T(128)}, bf16[3,1536,128]{1,2,0:T(8,128)(2,1)S(1)}, ...), condition=%wide.region_5.6_spmd, body=%wide.region_0.5_spmd.sunk | while | flops 408222720 | bytes 14428406 | solution.py:159
  187.6 1.0 constant_dynamic-slice_fusion.2
  188.7 1.2 dynamic-slice_bitcast_fusion.3
  189.8 6.1 %while.22 = (s32[]{:T(128)}, bf16[3,512,128]{2,1,0:T(8,128)(2,1)S(1)}, bf16[3,512,128]{2,1,0:T(8,128)(2,1)S(1)}, bf16[1536,128]{1,0:T(8,128)(2,1)S(1)}, bf16[1536,128]{1,0:T(8,128)(2,1)S(1)}, /*index=5*/s32[]{:T(128)}) while((s32[]{:T(128)}, bf16[3,512,128]{2,1,0:T(8,128)(2,1)S(1)}, bf16[3,512,128]{2,1,0:T(8,128)(2,1)S(1)}, ...), condition=%wide.region_4.4_spmd, body=%wide.region_1.3_spmd.sunk | while | flops 408222720 | bytes 10496085 | solution.py:91
  189.8 0.7 fusion.52
  191.1 0.8 fusion.54
  191.9 0.7 fusion.52
  193.1 0.8 fusion.54
  193.9 0.7 fusion.52
  195.1 0.8 fusion.54
  196.1 1.0 constant_dynamic-slice_fusion.2
  197.2 1.2 dynamic-slice_bitcast_fusion.3
  198.4 6.1 %while.22 = (s32[]{:T(128)}, bf16[3,512,128]{2,1,0:T(8,128)(2,1)S(1)}, bf16[3,512,128]{2,1,0:T(8,128)(2,1)S(1)}, bf16[1536,128]{1,0:T(8,128)(2,1)S(1)}, bf16[1536,128]{1,0:T(8,128)(2,1)S(1)}, /*index=5*/s32[]{:T(128)}) while((s32[]{:T(128)}, bf16[3,512,128]{2,1,0:T(8,128)(2,1)S(1)}, bf16[3,512,128]{2,1,0:T(8,128)(2,1)S(1)}, ...), condition=%wide.region_4.4_spmd, body=%wide.region_1.3_spmd.sunk | while | flops 408222720 | bytes 10496085 | solution.py:91
  198.4 0.7 fusion.52
  199.6 0.8 fusion.54
  200.4 0.7 fusion.52
  201.6 0.8 fusion.54
  202.4 0.7 fusion.52
  203.6 0.8 fusion.54
  204.7 1.0 constant_dynamic-slice_fusion.2
  205.7 1.2 dynamic-slice_bitcast_fusion.3
  206.9 6.1 %while.22 = (s32[]{:T(128)}, bf16[3,512,128]{2,1,0:T(8,128)(2,1)S(1)}, bf16[3,512,128]{2,1,0:T(8,128)(2,1)S(1)}, bf16[1536,128]{1,0:T(8,128)(2,1)S(1)}, bf16[1536,128]{1,0:T(8,128)(2,1)S(1)}, /*index=5*/s32[]{:T(128)}) while((s32[]{:T(128)}, bf16[3,512,128]{2,1,0:T(8,128)(2,1)S(1)}, bf16[3,512,128]{2,1,0:T(8,128)(2,1)S(1)}, ...), condition=%wide.region_4.4_spmd, body=%wide.region_1.3_spmd.sunk | while | flops 408222720 | bytes 10496085 | solution.py:91
  206.9 0.7 fusion.52
  208.1 0.8 fusion.54
  208.9 0.7 fusion.52
  210.1 0.8 fusion.54
  210.9 0.7 fusion.52
  212.2 0.8 fusion.54
  214.1 0.7 copy-done.2
  214.7 1.6 fusion.21
  216.7 1.8 all_to_all.33
  218.5 3.7 %all-to-all-start.1 = ((f32[32,1,3168]{2,1,0:T(1,128)}), f32[32,1,3168]{2,1,0:T(1,128)S(1)}, u32[]{:S(2)}, u32[]{:S(2)}) async-start(f32[32,1,3168]{2,1,0:T(1,128)} %all_to_all.33), calls=%async_computation.1 | async-start | bytes 819200 | tf_op jit(solution)/shard_map/all_to_all | solution.py:179
  223.2 26.2 %all-to-all-done.1 = f32[32,1,3168]{2,1,0:T(1,128)S(1)} async-done(((f32[32,1,3168]{2,1,0:T(1,128)}), f32[32,1,3168]{2,1,0:T(1,128)S(1)}, u32[]{:S(2)}, u32[]{:S(2)}) %all-to-all-start.1) | async-done | bytes 405536 | tf_op jit(solution)/shard_map/all_to_all | solution.py:179
  249.4 1.0 reduce.12
  251.0 0.8 slice_reduce_fusion.4
  253.3 0.7 fusion.33
  254.0 0.9 broadcast_in_dim.64
  255.0 6.1 %all-to-all-start.2 = ((bf16[16,4,3,2,512]{4,3,2,1,0:T(2,128)(2,1)}), bf16[16,4,3,2,512]{4,3,2,1,0:T(2,128)(2,1)S(1)}, u32[]{:S(2)}, u32[]{:S(2)}) async-start(bf16[16,4,3,2,512]{4,3,2,1,0:T(2,128)(2,1)} %broadcast_in_dim.64), calls=%async_computation.2 | async-start | bytes 786432 | tf_op jit(solution)/shard_map/all_to_all | solution.py:44
  261.3 10.8 %all-to-all-done.2 = bf16[16,4,3,2,512]{4,3,2,1,0:T(2,128)(2,1)S(1)} async-done(((bf16[16,4,3,2,512]{4,3,2,1,0:T(2,128)(2,1)}), bf16[16,4,3,2,512]{4,3,2,1,0:T(2,128)(2,1)S(1)}, u32[]{:S(2)}, u32[]{:S(2)}) %all-to-all-start.2) | async-done | bytes 393248 | tf_op jit(solution)/shard_map/all_to_all | solution.py:44
  272.1 0.6 gather_fusion
  272.8 2.4 collective-permute-start
  275.3 3.4 %collective-permute-start.1 = (bf16[4,3,1,512]{3,2,1,0:T(2,128)(2,1)S(1)}, bf16[4,3,1,512]{3,2,1,0:T(2,128)(2,1)S(1)}, u32[]{:S(2)}, u32[]{:S(2)}) collective-permute-start(bf16[4,3,1,512]{3,2,1,0:T(2,128)(2,1)S(1)} %get-tuple-element.98), channel_id=1, source_target_pairs={{8,0},{16,8},{24,16},{32,24},{40,32},{48,40},{56,48},{64,56},{72,6... | collective-permute-start | bytes 36872 | tf_op jit(solution)/shard_map/ppermute | solution.py:34
  278.8 3.1 collective-permute-done.1
  284.3 0.7 copy.129
  285.6 0.6 fusion.13
  286.2 2.6 broadcast_add_fusion
  288.9 1.5 copy.116
  292.2 1.5 copy.118
  294.3 0.8 reshape.179
  295.0 7.3 %all-to-all-start.3 = ((f32[32,1,256]{2,1,0:T(1,128)}), f32[32,1,256]{2,1,0:T(1,128)S(1)}, u32[]{:S(2)}, u32[]{:S(2)}) async-start(f32[32,1,256]{2,1,0:T(1,128)} %reshape.179), calls=%async_computation.3 | async-start | bytes 65536 | tf_op jit(solution)/shard_map/all_to_all | solution.py:44
  302.3 1.5 copy.114
  303.8 0.6 slice_bitcast_fusion
  304.8 2.5 reshape.146
  307.2 7.6 %all-to-all-done.3 = f32[32,1,256]{2,1,0:T(1,128)S(1)} async-done(((f32[32,1,256]{2,1,0:T(1,128)}), f32[32,1,256]{2,1,0:T(1,128)S(1)}, u32[]{:S(2)}, u32[]{:S(2)}) %all-to-all-start.3) | async-done | bytes 32800 | tf_op jit(solution)/shard_map/all_to_all | solution.py:44
  315.3 0.7 reduce.16
  316.7 2.5 mul.109
  319.6 2.5 sub.89
  322.0 4.5 %fusion.12 = bf16[4,3,2,16384]{3,2,1,0:T(2,128)(2,1)} fusion(f32[4,3,2,16384]{3,2,1,0:T(2,128)} %mul.109, f32[4,3,2,16384]{3,2,1,0:T(2,128)} %sub.89, f32[4,3,2,16384]{3,2,1,0:T(2,128)} %reshape.146, f32[16384]{0:T(1024)S(1)} %bitcast.116, f32[16384]{0:T(1024)S(1)} %bitcast.117), kind=kLoop, calls=%fused_computation.29 | loop fusion | flops 3538944 | bytes 5636096 | tf_op jit(solution)/shard_map/convert_element_type | solution.py:240
  (115 shorter events, 17.2 us)
Async XLA Ops:
  0.6 285.6 %copy-start = (bf16[3,3,3,16,512]{4,3,2,1,0:T(8,128)(2,1)S(1)}, bf16[3,3,3,16,512]{4,3,2,1,0:T(8,128)(2,1)}, u32[]{:S(2)}) copy-start(bf16[3,3,3,16,512]{4,3,2,1,0:T(8,128)(2,1)} %param.28) | copy-start | bytes 1327108
  4.1 178.9 %all-to-all-start = ((bf16[32,3,3,48,128]{4,3,2,1,0:T(8,128)(2,1)}), bf16[32,3,3,48,128]{4,3,2,1,0:T(8,128)(2,1)}, u32[]{:S(2)}, u32[]{:S(2)}) async-start(bf16[32,3,3,48,128]{4,3,2,1,0:T(8,128)(2,1)} %pad_maximum_fusion), calls=%async_computation | async-start | bytes 7077888 | tf_op jit(solution)/shard_map/all_to_all | solution.py:158
  213.7 1.0 copy-start.2
  213.7 1.0 copy-start.6
  216.4 5.8 %copy-start.12 = (s32[4]{0:T(128)S(1)}, s32[4]{0:T(128)}, u32[]{:S(2)}) copy-start(s32[4]{0:T(128)} %param.26) | copy-start | bytes 52
  216.4 5.8 %copy-start.4 = (f32[4,3072]{1,0:T(4,128)S(1)}, f32[4,3072]{1,0:T(4,128)}, u32[]{:S(2)}) copy-start(f32[4,3072]{1,0:T(4,128)} %param.21) | copy-start | bytes 147460
  216.4 6.2 %copy-start.3 = (f32[4,3072]{1,0:T(4,128)S(1)}, f32[4,3072]{1,0:T(4,128)}, u32[]{:S(2)}) copy-start(f32[4,3072]{1,0:T(4,128)} %param.22) | copy-start | bytes 147460
  218.5 30.9 %all-to-all-start.1 = ((f32[32,1,3168]{2,1,0:T(1,128)}), f32[32,1,3168]{2,1,0:T(1,128)S(1)}, u32[]{:S(2)}, u32[]{:S(2)}) async-start(f32[32,1,3168]{2,1,0:T(1,128)} %all_to_all.33), calls=%async_computation.1 | async-start | bytes 819200 | tf_op jit(solution)/shard_map/all_to_all | solution.py:179
  250.3 1.5 copy-start.10
  251.0 2.3 copy-start.5
  252.2 8.9 %copy-start.11 = (s32[64]{0:T(128)S(1)}, s32[64]{0:T(128)}, u32[]{:S(2)}) copy-start(s32[64]{0:T(128)} %param.27) | copy-start | bytes 772
  252.2 9.0 %copy-start.7 = (f32[512]{0:T(512)S(1)}, f32[512]{0:T(512)}, u32[]{:S(2)}) copy-start(f32[512]{0:T(512)} %param.31) | copy-start | bytes 6148
  252.3 26.4 %copy-start.8 = (f32[512]{0:T(512)S(1)}, f32[512]{0:T(512)}, u32[]{:S(2)}) copy-start(f32[512]{0:T(512)} %param.29) | copy-start | bytes 6148
  255.0 17.1 %all-to-all-start.2 = ((bf16[16,4,3,2,512]{4,3,2,1,0:T(2,128)(2,1)}), bf16[16,4,3,2,512]{4,3,2,1,0:T(2,128)(2,1)S(1)}, u32[]{:S(2)}, u32[]{:S(2)}) async-start(bf16[16,4,3,2,512]{4,3,2,1,0:T(2,128)(2,1)} %broadcast_in_dim.64), calls=%async_computation.2 | async-start | bytes 786432 | tf_op jit(solution)/shard_map/all_to_all | solution.py:44
  272.8 5.9 %collective-permute-start = (bf16[4,3,1,512]{3,2,1,0:T(2,128)(2,1)S(1)}, bf16[4,3,1,512]{3,2,1,0:T(2,128)(2,1)S(1)}, u32[]{:S(2)}, u32[]{:S(2)}) collective-permute-start(bf16[4,3,1,512]{3,2,1,0:T(2,128)(2,1)S(1)} %get-tuple-element.97), channel_id=1, source_target_pairs={{0,8},{8,16},{16,24},{24,32},{32,40},{40,48},{48,56},{56,64},{64,7... | collective-permute-start | bytes 36872 | tf_op jit(solution)/shard_map/ppermute | solution.py:32
  275.3 6.6 %collective-permute-start.1 = (bf16[4,3,1,512]{3,2,1,0:T(2,128)(2,1)S(1)}, bf16[4,3,1,512]{3,2,1,0:T(2,128)(2,1)S(1)}, u32[]{:S(2)}, u32[]{:S(2)}) collective-permute-start(bf16[4,3,1,512]{3,2,1,0:T(2,128)(2,1)S(1)} %get-tuple-element.98), channel_id=1, source_target_pairs={{8,0},{16,8},{24,16},{32,24},{40,32},{48,40},{56,48},{64,56},{72,6... | collective-permute-start | bytes 36872 | tf_op jit(solution)/shard_map/ppermute | solution.py:34
  285.5 0.7 copy-start.13
  293.7 8.6 %copy-start.1 = (f32[3,2,32,5,512]{4,2,3,1,0:T(8,128)S(1)}, f32[3,2,32,5,512]{4,2,3,1,0:T(8,128)}, u32[]{:S(2)}) copy-start(f32[3,2,32,5,512]{4,2,3,1,0:T(8,128)} %get-tuple-element.102) | copy-start | bytes 5898244
  295.0 19.8 %all-to-all-start.3 = ((f32[32,1,256]{2,1,0:T(1,128)}), f32[32,1,256]{2,1,0:T(1,128)S(1)}, u32[]{:S(2)}, u32[]{:S(2)}) async-start(f32[32,1,256]{2,1,0:T(1,128)} %reshape.179), calls=%async_computation.3 | async-start | bytes 65536 | tf_op jit(solution)/shard_map/all_to_all | solution.py:44
  304.8 11.7 %copy-start.9 = (f32[512]{0:T(512)S(1)}, f32[512]{0:T(512)}, u32[]{:S(2)}) copy-start(f32[512]{0:T(512)} %param.30) | copy-start | bytes 6148

commit v6 on v5

--- a/solution.py
+++ b/solution.py
@@ -235,10 +235,11 @@
     spread = m2 / (count * n_seq)
     mean_c = jnp.repeat(mean, group, axis=1)
     factor_c = jnp.repeat(lax.rsqrt(spread + eps_norm), group, axis=1) * group_gain
-    features = jax.nn.silu(
-        (conv_out - mean_c[:, None, :]) * factor_c[:, None, :] + group_shift
-    ).astype(jnp.bfloat16)
-    features = features.reshape(clips, FRAMES, rows_dev, LAT_W * VAE_CH)
+    laid = conv_out.reshape(clips, FRAMES, rows_dev, LAT_W * VAE_CH)
+    mean_t = jnp.tile(mean_c, (1, LAT_W))[:, None, None, :]
+    factor_t = jnp.tile(factor_c, (1, LAT_W))[:, None, None, :]
+    shift_t = jnp.tile(group_shift, LAT_W)
+    features = jax.nn.silu((laid - mean_t) * factor_t + shift_t).astype(jnp.bfloat16)
     return (denoised, features)
 
 

time: 327 us -> 322 us (0.985)
  no operation moved by 1% of the time
where the time goes in v6:
time: 322 us; the launch traced here: 321 us
  waiting for transfers between devices  209 us (65%)
  starting transfers between devices  39.7 us (12%)
  local copies, waits for them, and re-layouts  34.4 us (11%)
  other arithmetic  19.9 us (6%)
  matrix products  17.1 us (5%)
    all_to_all x1, waiting for transfers between devices, shards(): lax.all_to_all(stacked, 'seq', split_axis=0, concat_axis=3, tiled=True)  161 us
    all_to_all x1, waiting for transfers between devices, shards(): lax.all_to_all(packed, 'seq', split_axis=0, concat_axis=0, tiled=True)  26.2 us
    all_to_all x2, waiting for transfers between devices, gather_all(): return lax.all_to_all(copies, axis, 0, 0, tiled=True)  18.7 us
    all_to_all x1, starting transfers between devices, shards(): lax.all_to_all(stacked, 'seq', split_axis=0, concat_axis=3, tiled=True)  16.8 us
    all_to_all x2, starting transfers between devices, gather_all(): return lax.all_to_all(copies, axis, 0, 0, tiled=True)  13.4 us
    dot_general x9, matrix products, one_block(): jnp.dot(weights, value_rows, preferred_element_type=jnp.float32)  6.97 us
  transfers between devices with their start and end apart: 6, of which 5 were waited for; matrix products, arithmetic and copies ran while one was open for 2% of the time, Pallas kernels for 0%

profile of v6, /device:TPU:8, one launch (start us, length us, event | category | flops | bytes accessed | tf_op | source)
XLA Modules:
  0.0 321.5 jit_solution(16868892820671824214)
XLA Ops:
  0.6 3.5 %pad_maximum_fusion = bf16[32,3,3,48,128]{4,3,2,1,0:T(8,128)(2,1)} fusion(bf16[32,1,3,48,128]{4,3,2,1,0:T(8,128)(2,1)} %bitcast.118, bf16[32,1,3,48,128]{4,3,2,1,0:T(8,128)(2,1)} %bitcast.119, bf16[32,1,3,48,128]{4,3,2,1,0:T(8,128)(2,1)} %bitcast.120), kind=kLoop, calls=%fused_computation.16 | loop fusion | flops 3538944 | bytes 7077888 | tf_op jit(solution)/shard_map/stack | solution.py:150
  4.1 16.8 %all-to-all-start = ((bf16[32,3,3,48,128]{4,3,2,1,0:T(8,128)(2,1)}), bf16[32,3,3,48,128]{4,3,2,1,0:T(8,128)(2,1)}, u32[]{:S(2)}, u32[]{:S(2)}) async-start(bf16[32,3,3,48,128]{4,3,2,1,0:T(8,128)(2,1)} %pad_maximum_fusion), calls=%async_computation | async-start | bytes 7077888 | tf_op jit(solution)/shard_map/all_to_all | solution.py:158
  20.9 1.4 add_reduce_fusion
  22.3 160.8 %all-to-all-done = bf16[32,3,3,48,128]{4,3,2,1,0:T(8,128)(2,1)} async-done(((bf16[32,3,3,48,128]{4,3,2,1,0:T(8,128)(2,1)}), bf16[32,3,3,48,128]{4,3,2,1,0:T(8,128)(2,1)}, u32[]{:S(2)}, u32[]{:S(2)}) %all-to-all-start) | async-done | bytes 3538976 | tf_op jit(solution)/shard_map/all_to_all | solution.py:158
  183.1 2.7 copy.101
  185.8 1.8 slice_bitcast_fusion.1
  187.6 25.6 %while.21 = (s32[]{:T(128)}, bf16[3,1536,128]{1,2,0:T(8,128)(2,1)S(1)}, bf16[3,1536,128]{2,1,0:T(8,128)(2,1)}, bf16[3,1536,128]{2,1,0:T(8,128)(2,1)}, bf16[3,153...) while((s32[]{:T(128)}, bf16[3,1536,128]{1,2,0:T(8,128)(2,1)S(1)}, ...), condition=%wide.region_5.6_spmd, body=%wide.region_0.5_spmd.sunk | while | flops 408222720 | bytes 14428406 | solution.py:159
  187.6 1.0 constant_dynamic-slice_fusion.2
  188.7 1.2 dynamic-slice_bitcast_fusion.3
  189.8 6.1 %while.22 = (s32[]{:T(128)}, bf16[3,512,128]{2,1,0:T(8,128)(2,1)S(1)}, bf16[3,512,128]{2,1,0:T(8,128)(2,1)S(1)}, bf16[1536,128]{1,0:T(8,128)(2,1)S(1)}, bf16[1536,128]{1,0:T(8,128)(2,1)S(1)}, /*index=5*/s32[]{:T(128)}) while((s32[]{:T(128)}, bf16[3,512,128]{2,1,0:T(8,128)(2,1)S(1)}, bf16[3,512,128]{2,1,0:T(8,128)(2,1)S(1)}, ...), condition=%wide.region_4.4_spmd, body=%wide.region_1.3_spmd.sunk | while | flops 408222720 | bytes 10496085 | solution.py:91
  189.8 0.7 fusion.52
  190.5 0.6 fusion.53
  191.1 0.8 fusion.54
  191.9 0.7 fusion.52
  193.1 0.8 fusion.54
  193.9 0.7 fusion.52
  195.1 0.8 fusion.54
  196.1 1.0 constant_dynamic-slice_fusion.2
  197.2 1.2 dynamic-slice_bitcast_fusion.3
  198.4 6.1 %while.22 = (s32[]{:T(128)}, bf16[3,512,128]{2,1,0:T(8,128)(2,1)S(1)}, bf16[3,512,128]{2,1,0:T(8,128)(2,1)S(1)}, bf16[1536,128]{1,0:T(8,128)(2,1)S(1)}, bf16[1536,128]{1,0:T(8,128)(2,1)S(1)}, /*index=5*/s32[]{:T(128)}) while((s32[]{:T(128)}, bf16[3,512,128]{2,1,0:T(8,128)(2,1)S(1)}, bf16[3,512,128]{2,1,0:T(8,128)(2,1)S(1)}, ...), condition=%wide.region_4.4_spmd, body=%wide.region_1.3_spmd.sunk | while | flops 408222720 | bytes 10496085 | solution.py:91
  198.4 0.7 fusion.52
  199.6 0.8 fusion.54
  200.4 0.7 fusion.52
  201.6 0.8 fusion.54
  202.4 0.7 fusion.52
  203.6 0.8 fusion.54
  204.7 1.0 constant_dynamic-slice_fusion.2
  205.7 1.2 dynamic-slice_bitcast_fusion.3
  206.9 6.1 %while.22 = (s32[]{:T(128)}, bf16[3,512,128]{2,1,0:T(8,128)(2,1)S(1)}, bf16[3,512,128]{2,1,0:T(8,128)(2,1)S(1)}, bf16[1536,128]{1,0:T(8,128)(2,1)S(1)}, bf16[1536,128]{1,0:T(8,128)(2,1)S(1)}, /*index=5*/s32[]{:T(128)}) while((s32[]{:T(128)}, bf16[3,512,128]{2,1,0:T(8,128)(2,1)S(1)}, bf16[3,512,128]{2,1,0:T(8,128)(2,1)S(1)}, ...), condition=%wide.region_4.4_spmd, body=%wide.region_1.3_spmd.sunk | while | flops 408222720 | bytes 10496085 | solution.py:91
  206.9 0.7 fusion.52
  208.1 0.8 fusion.54
  208.9 0.7 fusion.52
  210.1 0.8 fusion.54
  210.9 0.7 fusion.52
  212.2 0.8 fusion.54
  214.1 0.7 copy-done.2
  214.7 1.6 fusion.21
  216.7 1.8 all_to_all.33
  218.5 3.7 %all-to-all-start.1 = ((f32[32,1,3168]{2,1,0:T(1,128)}), f32[32,1,3168]{2,1,0:T(1,128)S(1)}, u32[]{:S(2)}, u32[]{:S(2)}) async-start(f32[32,1,3168]{2,1,0:T(1,128)} %all_to_all.33), calls=%async_computation.1 | async-start | bytes 819200 | tf_op jit(solution)/shard_map/all_to_all | solution.py:179
  223.2 26.2 %all-to-all-done.1 = f32[32,1,3168]{2,1,0:T(1,128)S(1)} async-done(((f32[32,1,3168]{2,1,0:T(1,128)}), f32[32,1,3168]{2,1,0:T(1,128)S(1)}, u32[]{:S(2)}, u32[]{:S(2)}) %all-to-all-start.1) | async-done | bytes 405536 | tf_op jit(solution)/shard_map/all_to_all | solution.py:179
  249.4 1.0 reduce.12
  250.3 0.6 reshape.149
  251.0 0.8 slice_reduce_fusion.4
  253.3 0.7 fusion.33
  254.0 0.9 broadcast_in_dim.62
  255.0 6.1 %all-to-all-start.2 = ((bf16[16,4,3,2,512]{4,3,2,1,0:T(2,128)(2,1)}), bf16[16,4,3,2,512]{4,3,2,1,0:T(2,128)(2,1)S(1)}, u32[]{:S(2)}, u32[]{:S(2)}) async-start(bf16[16,4,3,2,512]{4,3,2,1,0:T(2,128)(2,1)} %broadcast_in_dim.62), calls=%async_computation.2 | async-start | bytes 786432 | tf_op jit(solution)/shard_map/all_to_all | solution.py:44
  261.3 10.8 %all-to-all-done.2 = bf16[16,4,3,2,512]{4,3,2,1,0:T(2,128)(2,1)S(1)} async-done(((bf16[16,4,3,2,512]{4,3,2,1,0:T(2,128)(2,1)}), bf16[16,4,3,2,512]{4,3,2,1,0:T(2,128)(2,1)S(1)}, u32[]{:S(2)}, u32[]{:S(2)}) %all-to-all-start.2) | async-done | bytes 393248 | tf_op jit(solution)/shard_map/all_to_all | solution.py:44
  272.1 0.6 gather_fusion
  272.8 2.4 collective-permute-start
  275.3 3.4 %collective-permute-start.1 = (bf16[4,3,1,512]{3,2,1,0:T(2,128)(2,1)S(1)}, bf16[4,3,1,512]{3,2,1,0:T(2,128)(2,1)S(1)}, u32[]{:S(2)}, u32[]{:S(2)}) collective-permute-start(bf16[4,3,1,512]{3,2,1,0:T(2,128)(2,1)S(1)} %get-tuple-element.98), channel_id=1, source_target_pairs={{8,0},{16,8},{24,16},{32,24},{40,32},{48,40},{56,48},{64,56},{72,6... | collective-permute-start | bytes 36872 | tf_op jit(solution)/shard_map/ppermute | solution.py:34
  278.8 3.1 collective-permute-done.1
  284.3 0.7 copy.129
  285.6 0.6 fusion.13
  286.2 1.3 broadcast_add_fusion
  287.6 2.8 copy.114
  290.4 1.5 copy.116
  293.7 1.5 copy.118
  295.8 0.8 reshape.189
  296.5 7.3 %all-to-all-start.3 = ((f32[32,1,256]{2,1,0:T(1,128)}), f32[32,1,256]{2,1,0:T(1,128)S(1)}, u32[]{:S(2)}, u32[]{:S(2)}) async-start(f32[32,1,256]{2,1,0:T(1,128)} %reshape.189), calls=%async_computation.3 | async-start | bytes 65536 | tf_op jit(solution)/shard_map/all_to_all | solution.py:44
  304.4 1.4 copy.115
  305.8 2.6 reshape.156
  308.5 7.8 %all-to-all-done.3 = f32[32,1,256]{2,1,0:T(1,128)S(1)} async-done(((f32[32,1,256]{2,1,0:T(1,128)}), f32[32,1,256]{2,1,0:T(1,128)S(1)}, u32[]{:S(2)}, u32[]{:S(2)}) %all-to-all-start.3) | async-done | bytes 32800 | tf_op jit(solution)/shard_map/all_to_all | solution.py:44
  316.8 0.7 reduce.16
  318.6 2.8 fusion.12
  (115 shorter events, 16.3 us)
Async XLA Ops:
  0.6 285.6 %copy-start = (bf16[3,3,3,16,512]{4,3,2,1,0:T(8,128)(2,1)S(1)}, bf16[3,3,3,16,512]{4,3,2,1,0:T(8,128)(2,1)}, u32[]{:S(2)}) copy-start(bf16[3,3,3,16,512]{4,3,2,1,0:T(8,128)(2,1)} %param.28) | copy-start | bytes 1327108
  4.1 178.9 %all-to-all-start = ((bf16[32,3,3,48,128]{4,3,2,1,0:T(8,128)(2,1)}), bf16[32,3,3,48,128]{4,3,2,1,0:T(8,128)(2,1)}, u32[]{:S(2)}, u32[]{:S(2)}) async-start(bf16[32,3,3,48,128]{4,3,2,1,0:T(8,128)(2,1)} %pad_maximum_fusion), calls=%async_computation | async-start | bytes 7077888 | tf_op jit(solution)/shard_map/all_to_all | solution.py:158
  213.7 1.0 copy-start.2
  213.7 1.0 copy-start.6
  216.3 5.8 %copy-start.12 = (s32[4]{0:T(128)S(1)}, s32[4]{0:T(128)}, u32[]{:S(2)}) copy-start(s32[4]{0:T(128)} %param.26) | copy-start | bytes 52
  216.4 5.8 %copy-start.4 = (f32[4,3072]{1,0:T(4,128)S(1)}, f32[4,3072]{1,0:T(4,128)}, u32[]{:S(2)}) copy-start(f32[4,3072]{1,0:T(4,128)} %param.21) | copy-start | bytes 147460
  216.4 6.2 %copy-start.3 = (f32[4,3072]{1,0:T(4,128)S(1)}, f32[4,3072]{1,0:T(4,128)}, u32[]{:S(2)}) copy-start(f32[4,3072]{1,0:T(4,128)} %param.22) | copy-start | bytes 147460
  218.5 30.9 %all-to-all-start.1 = ((f32[32,1,3168]{2,1,0:T(1,128)}), f32[32,1,3168]{2,1,0:T(1,128)S(1)}, u32[]{:S(2)}, u32[]{:S(2)}) async-start(f32[32,1,3168]{2,1,0:T(1,128)} %all_to_all.33), calls=%async_computation.1 | async-start | bytes 819200 | tf_op jit(solution)/shard_map/all_to_all | solution.py:179
  250.3 1.6 copy-start.10
  251.0 2.3 copy-start.5
  251.8 9.3 %copy-start.11 = (s32[64]{0:T(128)S(1)}, s32[64]{0:T(128)}, u32[]{:S(2)}) copy-start(s32[64]{0:T(128)} %param.27) | copy-start | bytes 772
  251.8 9.4 %copy-start.7 = (f32[512]{0:T(512)S(1)}, f32[512]{0:T(512)}, u32[]{:S(2)}) copy-start(f32[512]{0:T(512)} %param.31) | copy-start | bytes 6148
  251.8 26.9 %copy-start.8 = (f32[512]{0:T(512)S(1)}, f32[512]{0:T(512)}, u32[]{:S(2)}) copy-start(f32[512]{0:T(512)} %param.29) | copy-start | bytes 6148
  255.0 17.1 %all-to-all-start.2 = ((bf16[16,4,3,2,512]{4,3,2,1,0:T(2,128)(2,1)}), bf16[16,4,3,2,512]{4,3,2,1,0:T(2,128)(2,1)S(1)}, u32[]{:S(2)}, u32[]{:S(2)}) async-start(bf16[16,4,3,2,512]{4,3,2,1,0:T(2,128)(2,1)} %broadcast_in_dim.62), calls=%async_computation.2 | async-start | bytes 786432 | tf_op jit(solution)/shard_map/all_to_all | solution.py:44
  272.8 5.9 %collective-permute-start = (bf16[4,3,1,512]{3,2,1,0:T(2,128)(2,1)S(1)}, bf16[4,3,1,512]{3,2,1,0:T(2,128)(2,1)S(1)}, u32[]{:S(2)}, u32[]{:S(2)}) collective-permute-start(bf16[4,3,1,512]{3,2,1,0:T(2,128)(2,1)S(1)} %get-tuple-element.97), channel_id=1, source_target_pairs={{0,8},{8,16},{16,24},{24,32},{32,40},{40,48},{48,56},{56,64},{64,7... | collective-permute-start | bytes 36872 | tf_op jit(solution)/shard_map/ppermute | solution.py:32
  275.3 6.6 %collective-permute-start.1 = (bf16[4,3,1,512]{3,2,1,0:T(2,128)(2,1)S(1)}, bf16[4,3,1,512]{3,2,1,0:T(2,128)(2,1)S(1)}, u32[]{:S(2)}, u32[]{:S(2)}) collective-permute-start(bf16[4,3,1,512]{3,2,1,0:T(2,128)(2,1)S(1)} %get-tuple-element.98), channel_id=1, source_target_pairs={{8,0},{16,8},{24,16},{32,24},{40,32},{48,40},{56,48},{64,56},{72,6... | collective-permute-start | bytes 36872 | tf_op jit(solution)/shard_map/ppermute | solution.py:34
  285.1 1.1 copy-start.13
  295.2 8.6 %copy-start.1 = (f32[3,2,32,5,512]{4,1,3,2,0:T(2,128)S(1)}, f32[3,2,32,5,512]{4,1,3,2,0:T(2,128)}, u32[]{:S(2)}) copy-start(f32[3,2,32,5,512]{4,1,3,2,0:T(2,128)} %copy.114) | copy-start | bytes 5898244
  296.5 19.8 %all-to-all-start.3 = ((f32[32,1,256]{2,1,0:T(1,128)}), f32[32,1,256]{2,1,0:T(1,128)S(1)}, u32[]{:S(2)}, u32[]{:S(2)}) async-start(f32[32,1,256]{2,1,0:T(1,128)} %reshape.189), calls=%async_computation.3 | async-start | bytes 65536 | tf_op jit(solution)/shard_map/all_to_all | solution.py:44
  305.8 12.2 %copy-start.9 = (f32[512]{0:T(512)S(1)}, f32[512]{0:T(512)}, u32[]{:S(2)}) copy-start(f32[512]{0:T(512)} %param.30) | copy-start | bytes 6148

commit v7 on v6

--- a/solution.py
+++ b/solution.py
@@ -3,6 +3,7 @@
 import jax
 import jax.numpy as jnp
 from jax import lax
+from jax.experimental import pallas as pl
 from jax.sharding import PartitionSpec as P
 
 HEADS = 24
@@ -72,6 +73,39 @@
         mean = (mean + other_mean) * 0.5
         step *= 2
     return mean, m2
+
+
+QUERY_BLOCK = 512
+
+def attend_kernel(scale, q_ref, k_ref, v_ref, o_ref):
+    scores = lax.dot_general(
+        q_ref[0], k_ref[0], (((1,), (1,)), ((), ())), preferred_element_type=jnp.float32
+    ) * scale
+    top = jnp.max(scores, axis=1, keepdims=True)
+    expd = jnp.exp(scores - top)
+    weights = (expd / jnp.sum(expd, axis=1, keepdims=True)).astype(jnp.bfloat16)
+    o_ref[0] = jnp.dot(weights, v_ref[0], preferred_element_type=jnp.float32).astype(o_ref.dtype)
+
+def attend_units(query, keys, values):
+    units, length, depth = query.shape
+    block = math.gcd(length, QUERY_BLOCK)
+    scale = 1.0 / math.sqrt(depth)
+    return pl.pallas_call(
+        lambda *refs: attend_kernel(scale, *refs),
+        grid=(units, length // block),
+        in_specs=[
+            pl.BlockSpec((1, block, depth), lambda u, b: (u, b, 0)),
+            pl.BlockSpec((1, length, depth), lambda u, b: (u, 0, 0)),
+            pl.BlockSpec((1, length, depth), lambda u, b: (u, 0, 0)),
+        ],
+        out_specs=pl.BlockSpec((1, block, depth), lambda u, b: (u, b, 0)),
+        out_shape=jax.ShapeDtypeStruct((units, length, depth), jnp.bfloat16),
+        cost_estimate=pl.CostEstimate(
+            flops=4 * units * length * length * depth,
+            transcendentals=units * length * length,
+            bytes_accessed=4 * units * length * depth * 2,
+        ),
+    )(query, keys, values)
 
 
 def attend_unit(operands):
@@ -156,7 +190,7 @@
         axis=1,
     )
     parts = lax.all_to_all(stacked, "seq", split_axis=0, concat_axis=3, tiled=True)
-    outputs = lax.map(attend_unit, (parts[0, 0], parts[0, 1], parts[0, 2]))
+    outputs = attend_units(parts[0, 0], parts[0, 1], parts[0, 2])
     seq_len = outputs.shape[1]
     chunks = HEADS // units_local
     width = units_local * HEAD_DIM

time: 322 us -> 326 us (1.012)
  Pallas kernels: 0 us -> 24.2 us
  matrix products: 17.1 us -> 4.2 us
  local copies, waits for them, and re-layouts: 34.4 us -> 28.5 us
    pallas_call x0 -> x1, Pallas kernels: none -> 24.2 us  [attend_units(): pl.pallas_call(lambda *refs: attend_kernel(scale, *refs), grid=(units, le...]
    dot_general x18 -> x0, matrix products: 12.9 us -> none  [the longest x9 6.97 us: one_block(): jnp.dot(weights, value_rows, preferred_element_type=jnp.float32)]
    reduce_sum x9 -> x0, other arithmetic: 5.16 us -> none  [one_block(): weights = (expd / jnp.sum(expd, axis=1, keepdims=True)).astype(jnp.bfloat16)]
    squeeze x4 -> x1, local copies, waits for them, and re-layouts: 5.37 us -> 1.85 us  [shards(): outputs = attend_units(parts[0, 0], parts[0, 1], parts[0, 2])]
where the time goes in v7:
time: 326 us; the launch traced here: 325 us
  waiting for transfers between devices  210 us (64%)
  starting transfers between devices  40 us (12%)
  local copies, waits for them, and re-layouts  28.5 us (9%)
  Pallas kernels  24.2 us (7%)
  other arithmetic  17.1 us (5%)
  matrix products  4.2 us (1%)
    all_to_all x1, waiting for transfers between devices, shards(): lax.all_to_all(stacked, 'seq', split_axis=0, concat_axis=3, tiled=True)  162 us
    all_to_all x1, waiting for transfers between devices, shards(): lax.all_to_all(packed, 'seq', split_axis=0, concat_axis=0, tiled=True)  26 us
    pallas_call x1, Pallas kernels, attend_units(): pl.pallas_call(lambda *refs: attend_kernel(scale, *refs), grid=(units, le...  24.2 us
    all_to_all x2, waiting for transfers between devices, gather_all(): return lax.all_to_all(copies, axis, 0, 0, tiled=True)  18.7 us
    all_to_all x1, starting transfers between devices, shards(): lax.all_to_all(stacked, 'seq', split_axis=0, concat_axis=3, tiled=True)  16.9 us
    all_to_all x2, starting transfers between devices, gather_all(): return lax.all_to_all(copies, axis, 0, 0, tiled=True)  13.5 us
  transfers between devices with their start and end apart: 6, of which 5 were waited for; matrix products, arithmetic and copies ran while one was open for 2% of the time, Pallas kernels for 0%

profile of v7, /device:TPU:8, one launch (start us, length us, event | category | flops | bytes accessed | tf_op | source)
XLA Modules:
  0.0 325.4 jit_solution(13633471349010723813)
XLA Ops:
  0.6 3.5 %pad_maximum_fusion = bf16[32,3,3,48,128]{4,3,2,1,0:T(8,128)(2,1)} fusion(bf16[32,1,3,48,128]{4,3,2,1,0:T(8,128)(2,1)} %bitcast.81, bf16[32,1,3,48,128]{4,3,2,1,0:T(8,128)(2,1)} %bitcast.82, bf16[32,1,3,48,128]{4,3,2,1,0:T(8,128)(2,1)} %bitcast.83), kind=kLoop, calls=%fused_computation.1 | loop fusion | flops 3538944 | bytes 7077888 | tf_op jit(solution)/shard_map/stack | solution.py:184
  4.1 16.9 %all-to-all-start = ((bf16[32,3,3,48,128]{4,3,2,1,0:T(8,128)(2,1)}), bf16[32,3,3,48,128]{4,3,2,1,0:T(8,128)(2,1)}, u32[]{:S(2)}, u32[]{:S(2)}) async-start(bf16[32,3,3,48,128]{4,3,2,1,0:T(8,128)(2,1)} %pad_maximum_fusion), calls=%async_computation | async-start | bytes 7077888 | tf_op jit(solution)/shard_map/all_to_all | solution.py:192
  21.2 162.0 %all-to-all-done = bf16[32,3,3,48,128]{4,3,2,1,0:T(8,128)(2,1)} async-done(((bf16[32,3,3,48,128]{4,3,2,1,0:T(8,128)(2,1)}), bf16[32,3,3,48,128]{4,3,2,1,0:T(8,128)(2,1)}, u32[]{:S(2)}, u32[]{:S(2)}) %all-to-all-start) | async-done | bytes 3538976 | tf_op jit(solution)/shard_map/all_to_all | solution.py:192
  183.2 2.7 copy.84
  185.9 1.8 slice_bitcast_fusion.1
  187.8 24.2 %shard_map.149 = bf16[3,1536,128]{2,1,0:T(8,128)(2,1)} custom-call(bf16[3,1536,128]{2,1,0:T(8,128)(2,1)} %get-tuple-element.13.refs_0_, bf16[3,1536,128]{2,1,0:T(8,128)(2,1)} %get-tuple-element.12.refs_1_, bf16[3,1536,128]{2,1,0:T(8,128)(2,1)} %get-tuple-element.11.refs_2_), custom_call_target="tpu_custom_call" | custom-call | flops 3623878656 | bytes 4718592 | tf_op jit(solution)/shard_map/pallas_call | solution.py:93
  212.0 1.6 convert_reduce_fusion
  213.7 0.7 multiply_reduce_fusion
  214.4 0.2 convert_bitcast_fusion
  214.6 2.0 copy.85
  216.6 2.0 bitcast_subtract_fusion
  218.6 1.6 fusion.11
  220.3 0.3 copy.86
  220.6 1.8 all_to_all.33
  222.3 3.8 %all-to-all-start.1 = ((f32[32,1,3168]{2,1,0:T(1,128)}), f32[32,1,3168]{2,1,0:T(1,128)S(1)}, u32[]{:S(2)}, u32[]{:S(2)}) async-start(f32[32,1,3168]{2,1,0:T(1,128)} %all_to_all.33), calls=%async_computation.1 | async-start | bytes 819200 | tf_op jit(solution)/shard_map/all_to_all | solution.py:213
  226.2 0.4 fusion.26
  226.7 0.5 convolution_bitcast_fusion
  227.2 26.0 %all-to-all-done.1 = f32[32,1,3168]{2,1,0:T(1,128)S(1)} async-done(((f32[32,1,3168]{2,1,0:T(1,128)}), f32[32,1,3168]{2,1,0:T(1,128)S(1)}, u32[]{:S(2)}, u32[]{:S(2)}) %all-to-all-start.1) | async-done | bytes 405536 | tf_op jit(solution)/shard_map/all_to_all | solution.py:213
  253.2 1.0 reduce.12
  254.2 0.6 reshape.141
  254.9 0.8 slice_reduce_fusion.4
  255.7 0.4 fusion.8
  256.1 0.3 reshape.144
  256.5 0.2 copy.91
  256.6 0.5 reshape.145
  257.2 0.7 fusion.23
  257.9 0.9 broadcast_in_dim.26
  258.8 6.1 %all-to-all-start.2 = ((bf16[16,4,3,2,512]{4,3,2,1,0:T(2,128)(2,1)}), bf16[16,4,3,2,512]{4,3,2,1,0:T(2,128)(2,1)S(1)}, u32[]{:S(2)}, u32[]{:S(2)}) async-start(bf16[16,4,3,2,512]{4,3,2,1,0:T(2,128)(2,1)} %broadcast_in_dim.26), calls=%async_computation.2 | async-start | bytes 786432 | tf_op jit(solution)/shard_map/all_to_all | solution.py:45
  265.1 10.8 %all-to-all-done.2 = bf16[16,4,3,2,512]{4,3,2,1,0:T(2,128)(2,1)S(1)} async-done(((bf16[16,4,3,2,512]{4,3,2,1,0:T(2,128)(2,1)}), bf16[16,4,3,2,512]{4,3,2,1,0:T(2,128)(2,1)S(1)}, u32[]{:S(2)}, u32[]{:S(2)}) %all-to-all-start.2) | async-done | bytes 393248 | tf_op jit(solution)/shard_map/all_to_all | solution.py:45
  275.9 0.6 gather_fusion
  276.7 2.5 collective-permute-start
  279.2 3.3 %collective-permute-start.1 = (bf16[4,3,1,512]{3,2,1,0:T(2,128)(2,1)S(1)}, bf16[4,3,1,512]{3,2,1,0:T(2,128)(2,1)S(1)}, u32[]{:S(2)}, u32[]{:S(2)}) collective-permute-start(bf16[4,3,1,512]{3,2,1,0:T(2,128)(2,1)S(1)} %get-tuple-element.19), channel_id=1, source_target_pairs={{8,0},{16,8},{24,16},{32,24},{40,32},{48,40},{56,48},{64,56},{72,6... | collective-permute-start | bytes 36872 | tf_op jit(solution)/shard_map/ppermute | solution.py:35
  282.6 3.2 collective-permute-done.1
  286.0 0.3 reshape.147
  286.3 0.1 pad_maximum_fusion.1
  286.5 0.3 copy.93
  286.8 0.6 copy.94
  287.4 0.6 copy.92
  287.9 0.3 maximum_bitcast_fusion
  288.3 0.7 copy.108
  289.0 0.4 pad.clone
  289.5 0.6 fusion.3
  290.2 1.3 broadcast_add_fusion
  291.5 2.8 copy.97
  294.3 1.5 copy.99
  295.8 0.3 slice_reduce_fusion.1
  296.4 0.1 sub.71
  296.5 0.6 broadcast.137
  297.1 0.5 fusion.1
  297.6 1.5 copy.101
  299.2 0.3 slice_reduce_fusion
  299.7 0.8 reshape.181
  300.5 7.3 %all-to-all-start.3 = ((f32[32,1,256]{2,1,0:T(1,128)}), f32[32,1,256]{2,1,0:T(1,128)S(1)}, u32[]{:S(2)}, u32[]{:S(2)}) async-start(f32[32,1,256]{2,1,0:T(1,128)} %reshape.181), calls=%async_computation.3 | async-start | bytes 65536 | tf_op jit(solution)/shard_map/all_to_all | solution.py:45
  307.8 0.5 slice_bitcast_fusion
  308.4 1.4 copy.98
  309.8 2.6 reshape.148
  312.5 7.8 %all-to-all-done.3 = f32[32,1,256]{2,1,0:T(1,128)S(1)} async-done(((f32[32,1,256]{2,1,0:T(1,128)}), f32[32,1,256]{2,1,0:T(1,128)S(1)}, u32[]{:S(2)}, u32[]{:S(2)}) %all-to-all-start.3) | async-done | bytes 32800 | tf_op jit(solution)/shard_map/all_to_all | solution.py:45
  320.3 0.5 broadcast.161
  320.8 0.7 reduce.16
  321.6 0.1 reshape.182
  321.9 0.1 reshape.151
  322.0 0.2 copy.112
  322.4 0.2 copy.111
  322.6 2.8 fusion.2
  (71 shorter events, 1.8 us)
Async XLA Ops:
  0.6 289.5 %copy-start = (bf16[3,3,3,16,512]{4,3,2,1,0:T(8,128)(2,1)S(1)}, bf16[3,3,3,16,512]{4,3,2,1,0:T(8,128)(2,1)}, u32[]{:S(2)}) copy-start(bf16[3,3,3,16,512]{4,3,2,1,0:T(8,128)(2,1)} %param.24) | copy-start | bytes 1327108
  4.1 16.9 %copy-start.4 = (f32[4,3072]{1,0:T(4,128)S(1)}, f32[4,3072]{1,0:T(4,128)}, u32[]{:S(2)}) copy-start(f32[4,3072]{1,0:T(4,128)} %param.18) | copy-start | bytes 147460
  4.1 179.1 %all-to-all-start = ((bf16[32,3,3,48,128]{4,3,2,1,0:T(8,128)(2,1)}), bf16[32,3,3,48,128]{4,3,2,1,0:T(8,128)(2,1)}, u32[]{:S(2)}, u32[]{:S(2)}) async-start(bf16[32,3,3,48,128]{4,3,2,1,0:T(8,128)(2,1)} %pad_maximum_fusion), calls=%async_computation | async-start | bytes 7077888 | tf_op jit(solution)/shard_map/all_to_all | solution.py:192
  212.0 1.7 copy-start.1
  216.6 2.0 copy-start.3
  220.2 6.0 %copy-start.12 = (s32[4]{0:T(128)S(1)}, s32[4]{0:T(128)}, u32[]{:S(2)}) copy-start(s32[4]{0:T(128)} %param.22) | copy-start | bytes 52
  220.2 6.0 %copy-start.5 = (f32[4,3072]{1,0:T(4,128)S(1)}, f32[4,3072]{1,0:T(4,128)}, u32[]{:S(2)}) copy-start(f32[4,3072]{1,0:T(4,128)} %param.17) | copy-start | bytes 147460
  222.3 30.9 %all-to-all-start.1 = ((f32[32,1,3168]{2,1,0:T(1,128)}), f32[32,1,3168]{2,1,0:T(1,128)S(1)}, u32[]{:S(2)}, u32[]{:S(2)}) async-start(f32[32,1,3168]{2,1,0:T(1,128)} %all_to_all.33), calls=%async_computation.1 | async-start | bytes 819200 | tf_op jit(solution)/shard_map/all_to_all | solution.py:213
  254.2 1.6 copy-start.10
  254.8 2.3 copy-start.6
  255.7 9.3 %copy-start.11 = (s32[64]{0:T(128)S(1)}, s32[64]{0:T(128)}, u32[]{:S(2)}) copy-start(s32[64]{0:T(128)} %param.23) | copy-start | bytes 772
  255.7 9.4 %copy-start.7 = (f32[512]{0:T(512)S(1)}, f32[512]{0:T(512)}, u32[]{:S(2)}) copy-start(f32[512]{0:T(512)} %param.27) | copy-start | bytes 6148
  255.7 26.9 %copy-start.8 = (f32[512]{0:T(512)S(1)}, f32[512]{0:T(512)}, u32[]{:S(2)}) copy-start(f32[512]{0:T(512)} %param.25) | copy-start | bytes 6148
  258.8 17.1 %all-to-all-start.2 = ((bf16[16,4,3,2,512]{4,3,2,1,0:T(2,128)(2,1)}), bf16[16,4,3,2,512]{4,3,2,1,0:T(2,128)(2,1)S(1)}, u32[]{:S(2)}, u32[]{:S(2)}) async-start(bf16[16,4,3,2,512]{4,3,2,1,0:T(2,128)(2,1)} %broadcast_in_dim.26), calls=%async_computation.2 | async-start | bytes 786432 | tf_op jit(solution)/shard_map/all_to_all | solution.py:45
  276.7 5.9 %collective-permute-start = (bf16[4,3,1,512]{3,2,1,0:T(2,128)(2,1)S(1)}, bf16[4,3,1,512]{3,2,1,0:T(2,128)(2,1)S(1)}, u32[]{:S(2)}, u32[]{:S(2)}) collective-permute-start(bf16[4,3,1,512]{3,2,1,0:T(2,128)(2,1)S(1)} %get-tuple-element.18), channel_id=1, source_target_pairs={{0,8},{8,16},{16,24},{24,32},{32,40},{40,48},{48,56},{56,64},{64,7... | collective-permute-start | bytes 36872 | tf_op jit(solution)/shard_map/ppermute | solution.py:33
  279.2 6.6 %collective-permute-start.1 = (bf16[4,3,1,512]{3,2,1,0:T(2,128)(2,1)S(1)}, bf16[4,3,1,512]{3,2,1,0:T(2,128)(2,1)S(1)}, u32[]{:S(2)}, u32[]{:S(2)}) collective-permute-start(bf16[4,3,1,512]{3,2,1,0:T(2,128)(2,1)S(1)} %get-tuple-element.19), channel_id=1, source_target_pairs={{8,0},{16,8},{24,16},{32,24},{40,32},{48,40},{56,48},{64,56},{72,6... | collective-permute-start | bytes 36872 | tf_op jit(solution)/shard_map/ppermute | solution.py:35
  289.0 1.1 copy-start.13
  299.2 8.7 %copy-start.2 = (f32[3,2,32,5,512]{4,1,3,2,0:T(2,128)S(1)}, f32[3,2,32,5,512]{4,1,3,2,0:T(2,128)}, u32[]{:S(2)}) copy-start(f32[3,2,32,5,512]{4,1,3,2,0:T(2,128)} %copy.97) | copy-start | bytes 5898244
  300.5 19.8 %all-to-all-start.3 = ((f32[32,1,256]{2,1,0:T(1,128)}), f32[32,1,256]{2,1,0:T(1,128)S(1)}, u32[]{:S(2)}, u32[]{:S(2)}) async-start(f32[32,1,256]{2,1,0:T(1,128)} %reshape.181), calls=%async_computation.3 | async-start | bytes 65536 | tf_op jit(solution)/shard_map/all_to_all | solution.py:45
  309.8 12.2 %copy-start.9 = (f32[512]{0:T(512)S(1)}, f32[512]{0:T(512)}, u32[]{:S(2)}) copy-start(f32[512]{0:T(512)} %param.26) | copy-start | bytes 6148

commit v8 on v6

--- a/solution.py
+++ b/solution.py
@@ -77,7 +77,7 @@
 def attend_unit(operands):
     query_rows, key_rows, value_rows = operands
     length = query_rows.shape[0]
-    block = math.gcd(length, 512)
+    block = length
     scale = 1.0 / math.sqrt(query_rows.shape[1])
     blocks = query_rows.reshape(length // block, block, query_rows.shape[1])
 

time: 322 us -> 317 us (0.984)
  local copies, waits for them, and re-layouts: 34.4 us -> 27.8 us
    squeeze x4 -> x1, local copies, waits for them, and re-layouts: 5.37 us -> 1.85 us  [shards(): outputs = lax.map(attend_unit, (parts[0, 0], parts[0, 1], parts[0, 2]))]
    dot_general x9 -> x3, matrix products: 5.9 us -> 7.54 us  [one_block(): jnp.dot(rows, key_rows.T, preferred_element_type=jnp.float32) * scale]
    dot_general x9 -> x3, matrix products: 6.97 us -> 8.12 us  [one_block(): jnp.dot(weights, value_rows, preferred_element_type=jnp.float32)]
where the time goes in v8:
time: 317 us
  waiting for transfers between devices  210 us (66%)
  starting transfers between devices  40 us (13%)
  local copies, waits for them, and re-layouts  27.8 us (9%)
  matrix products  19.9 us (6%)
  other arithmetic  17.4 us (5%)
    all_to_all x1, waiting for transfers between devices, shards(): lax.all_to_all(stacked, 'seq', split_axis=0, concat_axis=3, tiled=True)  162 us
    all_to_all x1, waiting for transfers between devices, shards(): lax.all_to_all(packed, 'seq', split_axis=0, concat_axis=0, tiled=True)  26 us
    all_to_all x2, waiting for transfers between devices, gather_all(): return lax.all_to_all(copies, axis, 0, 0, tiled=True)  18.7 us
    all_to_all x1, starting transfers between devices, shards(): lax.all_to_all(stacked, 'seq', split_axis=0, concat_axis=3, tiled=True)  16.9 us
    all_to_all x2, starting transfers between devices, gather_all(): return lax.all_to_all(copies, axis, 0, 0, tiled=True)  13.5 us
    dot_general x3, matrix products, one_block(): jnp.dot(weights, value_rows, preferred_element_type=jnp.float32)  8.12 us
    dot_general x3, matrix products, one_block(): jnp.dot(rows, key_rows.T, preferred_element_type=jnp.float32) * scale  7.54 us
  transfers between devices with their start and end apart: 6, of which 5 were waited for; matrix products, arithmetic and copies ran while one was open for 2% of the time, Pallas kernels for 0%

profile of v8, /device:TPU:8, one launch (start us, length us, event | category | flops | bytes accessed | tf_op | source)
XLA Modules:
  0.0 316.5 jit_solution(7971791671741189769)
XLA Ops:
  0.6 3.5 %pad_maximum_fusion = bf16[32,3,3,48,128]{4,3,2,1,0:T(8,128)(2,1)} fusion(bf16[32,1,3,48,128]{4,3,2,1,0:T(8,128)(2,1)} %bitcast.108, bf16[32,1,3,48,128]{4,3,2,1,0:T(8,128)(2,1)} %bitcast.109, bf16[32,1,3,48,128]{4,3,2,1,0:T(8,128)(2,1)} %bitcast.110), kind=kLoop, calls=%fused_computation.17 | loop fusion | flops 3538944 | bytes 7077888 | tf_op jit(solution)/shard_map/stack | solution.py:150
  4.1 16.9 %all-to-all-start = ((bf16[32,3,3,48,128]{4,3,2,1,0:T(8,128)(2,1)}), bf16[32,3,3,48,128]{4,3,2,1,0:T(8,128)(2,1)}, u32[]{:S(2)}, u32[]{:S(2)}) async-start(bf16[32,3,3,48,128]{4,3,2,1,0:T(8,128)(2,1)} %pad_maximum_fusion), calls=%async_computation | async-start | bytes 7077888 | tf_op jit(solution)/shard_map/all_to_all | solution.py:158
  21.2 162.0 %all-to-all-done = bf16[32,3,3,48,128]{4,3,2,1,0:T(8,128)(2,1)} async-done(((bf16[32,3,3,48,128]{4,3,2,1,0:T(8,128)(2,1)}), bf16[32,3,3,48,128]{4,3,2,1,0:T(8,128)(2,1)}, u32[]{:S(2)}, u32[]{:S(2)}) %all-to-all-start) | async-done | bytes 3538976 | tf_op jit(solution)/shard_map/all_to_all | solution.py:158
  183.2 2.7 copy.101
  185.9 1.8 slice_bitcast_fusion.1
  187.8 20.4 %while.10 = (s32[]{:T(128)}, bf16[3,1536,128]{1,2,0:T(8,128)(2,1)S(1)}, bf16[3,1536,128]{2,1,0:T(8,128)(2,1)}, bf16[3,1536,128]{2,1,0:T(8,128)(2,1)}, bf16[3,1536,128]{2,1,0:T(8,128)(2,1)}, /*index=5*/s32[]{:T(128)}) while((s32[]{:T(128)}, bf16[3,1536,128]{1,2,0:T(8,128)(2,1)S(1)}, bf16[3,1536,128]{2,1,0:T(8,128)(2,1)}, ...), condition=%wide.region_3.0_spmd, body=%wide.region_0.3_spmd.sunk | while | flops 1224668160 | bytes 31489108 | solution.py:159
  187.8 2.5 fusion.52
  190.3 1.3 fusion.53
  191.6 2.7 fusion.54
  194.6 2.5 fusion.52
  197.1 1.3 fusion.53
  198.4 2.7 fusion.54
  201.4 2.5 fusion.52
  203.9 1.3 fusion.53
  205.2 2.7 fusion.54
  208.4 0.3 fusion.13
  208.7 0.3 bitcast_subtract_fusion
  209.0 0.7 copy-done.2
  209.7 1.6 fusion.25
  211.4 0.3 copy.103
  211.7 1.8 all_to_all.33
  213.4 3.8 %all-to-all-start.1 = ((f32[32,1,3168]{2,1,0:T(1,128)}), f32[32,1,3168]{2,1,0:T(1,128)S(1)}, u32[]{:S(2)}, u32[]{:S(2)}) async-start(f32[32,1,3168]{2,1,0:T(1,128)} %all_to_all.33), calls=%async_computation.1 | async-start | bytes 819200 | tf_op jit(solution)/shard_map/all_to_all | solution.py:179
  217.3 0.4 fusion.41
  217.8 0.5 convolution_bitcast_fusion
  218.3 26.0 %all-to-all-done.1 = f32[32,1,3168]{2,1,0:T(1,128)S(1)} async-done(((f32[32,1,3168]{2,1,0:T(1,128)}), f32[32,1,3168]{2,1,0:T(1,128)S(1)}, u32[]{:S(2)}, u32[]{:S(2)}) %all-to-all-start.1) | async-done | bytes 405536 | tf_op jit(solution)/shard_map/all_to_all | solution.py:179
  244.3 1.0 reduce.12
  245.3 0.6 reshape.145
  246.0 0.8 slice_reduce_fusion.4
  246.9 0.4 fusion.22
  247.2 0.3 reshape.148
  247.8 0.5 reshape.149
  248.3 0.7 fusion.37
  249.0 0.9 broadcast_in_dim.63
  249.9 6.1 %all-to-all-start.2 = ((bf16[16,4,3,2,512]{4,3,2,1,0:T(2,128)(2,1)}), bf16[16,4,3,2,512]{4,3,2,1,0:T(2,128)(2,1)S(1)}, u32[]{:S(2)}, u32[]{:S(2)}) async-start(bf16[16,4,3,2,512]{4,3,2,1,0:T(2,128)(2,1)} %broadcast_in_dim.63), calls=%async_computation.2 | async-start | bytes 786432 | tf_op jit(solution)/shard_map/all_to_all | solution.py:44
  256.2 10.8 %all-to-all-done.2 = bf16[16,4,3,2,512]{4,3,2,1,0:T(2,128)(2,1)S(1)} async-done(((bf16[16,4,3,2,512]{4,3,2,1,0:T(2,128)(2,1)}), bf16[16,4,3,2,512]{4,3,2,1,0:T(2,128)(2,1)S(1)}, u32[]{:S(2)}, u32[]{:S(2)}) %all-to-all-start.2) | async-done | bytes 393248 | tf_op jit(solution)/shard_map/all_to_all | solution.py:44
  267.0 0.6 gather_fusion
  267.8 2.5 collective-permute-start
  270.3 3.3 %collective-permute-start.1 = (bf16[4,3,1,512]{3,2,1,0:T(2,128)(2,1)S(1)}, bf16[4,3,1,512]{3,2,1,0:T(2,128)(2,1)S(1)}, u32[]{:S(2)}, u32[]{:S(2)}) collective-permute-start(bf16[4,3,1,512]{3,2,1,0:T(2,128)(2,1)S(1)} %get-tuple-element.74), channel_id=1, source_target_pairs={{8,0},{16,8},{24,16},{32,24},{40,32},{48,40},{56,48},{64,56},{72,6... | collective-permute-start | bytes 36872 | tf_op jit(solution)/shard_map/ppermute | solution.py:34
  273.7 3.2 %collective-permute-done.1 = bf16[4,3,1,512]{3,2,1,0:T(2,128)(2,1)S(1)} collective-permute-done((bf16[4,3,1,512]{3,2,1,0:T(2,128)(2,1)S(1)}, bf16[4,3,1,512]{3,2,1,0:T(2,128)(2,1)S(1)}, u32[]{:S(2)}, u32[]{:S(2)}) %collective-permute-start.1) | collective-permute-done | bytes 12320 | tf_op jit(solution)/shard_map/ppermute | solution.py:34
  277.1 0.3 reshape.151
  277.6 0.3 copy.110
  277.9 0.6 copy.111
  278.5 0.6 copy.109
  279.1 0.3 maximum_bitcast_fusion
  279.4 0.7 copy.129
  280.1 0.4 pad.clone
  280.7 0.6 fusion.17
  281.3 1.3 broadcast_add_fusion
  282.6 2.8 copy.114
  285.4 1.5 copy.116
  286.9 0.3 slice_reduce_fusion.1
  287.6 0.6 broadcast.144
  288.2 0.5 fusion.15
  288.7 1.5 copy.118
  290.3 0.3 slice_reduce_fusion
  290.8 0.8 reshape.185
  291.6 7.3 %all-to-all-start.3 = ((f32[32,1,256]{2,1,0:T(1,128)}), f32[32,1,256]{2,1,0:T(1,128)S(1)}, u32[]{:S(2)}, u32[]{:S(2)}) async-start(f32[32,1,256]{2,1,0:T(1,128)} %reshape.185), calls=%async_computation.3 | async-start | bytes 65536 | tf_op jit(solution)/shard_map/all_to_all | solution.py:44
  298.9 0.5 slice_bitcast_fusion
  299.5 1.4 copy.115
  300.9 2.6 reshape.152
  303.6 7.8 %all-to-all-done.3 = f32[32,1,256]{2,1,0:T(1,128)S(1)} async-done(((f32[32,1,256]{2,1,0:T(1,128)}), f32[32,1,256]{2,1,0:T(1,128)S(1)}, u32[]{:S(2)}, u32[]{:S(2)}) %all-to-all-start.3) | async-done | bytes 32800 | tf_op jit(solution)/shard_map/all_to_all | solution.py:44
  311.4 0.5 broadcast.169
  311.9 0.7 reduce.16
  313.7 2.8 fusion.16
  (83 shorter events, 3.7 us)
Async XLA Ops:
  0.6 280.6 %copy-start = (bf16[3,3,3,16,512]{4,3,2,1,0:T(8,128)(2,1)S(1)}, bf16[3,3,3,16,512]{4,3,2,1,0:T(8,128)(2,1)}, u32[]{:S(2)}) copy-start(bf16[3,3,3,16,512]{4,3,2,1,0:T(8,128)(2,1)} %param.26) | copy-start | bytes 1327108
  4.1 16.9 %copy-start.3 = (f32[4,3072]{1,0:T(4,128)S(1)}, f32[4,3072]{1,0:T(4,128)}, u32[]{:S(2)}) copy-start(f32[4,3072]{1,0:T(4,128)} %param.20) | copy-start | bytes 147460
  4.1 179.1 %all-to-all-start = ((bf16[32,3,3,48,128]{4,3,2,1,0:T(8,128)(2,1)}), bf16[32,3,3,48,128]{4,3,2,1,0:T(8,128)(2,1)}, u32[]{:S(2)}, u32[]{:S(2)}) async-start(bf16[32,3,3,48,128]{4,3,2,1,0:T(8,128)(2,1)} %pad_maximum_fusion), calls=%async_computation | async-start | bytes 7077888 | tf_op jit(solution)/shard_map/all_to_all | solution.py:158
  208.7 1.0 copy-start.2
  211.3 6.0 %copy-start.11 = (s32[4]{0:T(128)S(1)}, s32[4]{0:T(128)}, u32[]{:S(2)}) copy-start(s32[4]{0:T(128)} %param.24) | copy-start | bytes 52
  211.3 6.0 %copy-start.4 = (f32[4,3072]{1,0:T(4,128)S(1)}, f32[4,3072]{1,0:T(4,128)}, u32[]{:S(2)}) copy-start(f32[4,3072]{1,0:T(4,128)} %param.19) | copy-start | bytes 147460
  213.4 30.9 %all-to-all-start.1 = ((f32[32,1,3168]{2,1,0:T(1,128)}), f32[32,1,3168]{2,1,0:T(1,128)S(1)}, u32[]{:S(2)}, u32[]{:S(2)}) async-start(f32[32,1,3168]{2,1,0:T(1,128)} %all_to_all.33), calls=%async_computation.1 | async-start | bytes 819200 | tf_op jit(solution)/shard_map/all_to_all | solution.py:179
  245.3 1.6 copy-start.9
  246.0 2.3 copy-start.5
  246.8 9.3 %copy-start.10 = (s32[64]{0:T(128)S(1)}, s32[64]{0:T(128)}, u32[]{:S(2)}) copy-start(s32[64]{0:T(128)} %param.25) | copy-start | bytes 772
  246.8 9.4 %copy-start.6 = (f32[512]{0:T(512)S(1)}, f32[512]{0:T(512)}, u32[]{:S(2)}) copy-start(f32[512]{0:T(512)} %param.29) | copy-start | bytes 6148
  246.8 26.9 %copy-start.7 = (f32[512]{0:T(512)S(1)}, f32[512]{0:T(512)}, u32[]{:S(2)}) copy-start(f32[512]{0:T(512)} %param.27) | copy-start | bytes 6148
  249.9 17.1 %all-to-all-start.2 = ((bf16[16,4,3,2,512]{4,3,2,1,0:T(2,128)(2,1)}), bf16[16,4,3,2,512]{4,3,2,1,0:T(2,128)(2,1)S(1)}, u32[]{:S(2)}, u32[]{:S(2)}) async-start(bf16[16,4,3,2,512]{4,3,2,1,0:T(2,128)(2,1)} %broadcast_in_dim.63), calls=%async_computation.2 | async-start | bytes 786432 | tf_op jit(solution)/shard_map/all_to_all | solution.py:44
  267.8 5.9 %collective-permute-start = (bf16[4,3,1,512]{3,2,1,0:T(2,128)(2,1)S(1)}, bf16[4,3,1,512]{3,2,1,0:T(2,128)(2,1)S(1)}, u32[]{:S(2)}, u32[]{:S(2)}) collective-permute-start(bf16[4,3,1,512]{3,2,1,0:T(2,128)(2,1)S(1)} %get-tuple-element.73), channel_id=1, source_target_pairs={{0,8},{8,16},{16,24},{24,32},{32,40},{40,48},{48,56},{56,64},{64,7... | collective-permute-start | bytes 36872 | tf_op jit(solution)/shard_map/ppermute | solution.py:32
  270.3 6.6 %collective-permute-start.1 = (bf16[4,3,1,512]{3,2,1,0:T(2,128)(2,1)S(1)}, bf16[4,3,1,512]{3,2,1,0:T(2,128)(2,1)S(1)}, u32[]{:S(2)}, u32[]{:S(2)}) collective-permute-start(bf16[4,3,1,512]{3,2,1,0:T(2,128)(2,1)S(1)} %get-tuple-element.74), channel_id=1, source_target_pairs={{8,0},{16,8},{24,16},{32,24},{40,32},{48,40},{56,48},{64,56},{72,6... | collective-permute-start | bytes 36872 | tf_op jit(solution)/shard_map/ppermute | solution.py:34
  280.1 1.1 copy-start.12
  290.3 8.7 %copy-start.1 = (f32[3,2,32,5,512]{4,1,3,2,0:T(2,128)S(1)}, f32[3,2,32,5,512]{4,1,3,2,0:T(2,128)}, u32[]{:S(2)}) copy-start(f32[3,2,32,5,512]{4,1,3,2,0:T(2,128)} %copy.114) | copy-start | bytes 5898244
  291.6 19.8 %all-to-all-start.3 = ((f32[32,1,256]{2,1,0:T(1,128)}), f32[32,1,256]{2,1,0:T(1,128)S(1)}, u32[]{:S(2)}, u32[]{:S(2)}) async-start(f32[32,1,256]{2,1,0:T(1,128)} %reshape.185), calls=%async_computation.3 | async-start | bytes 65536 | tf_op jit(solution)/shard_map/all_to_all | solution.py:44
  300.9 12.2 %copy-start.8 = (f32[512]{0:T(512)S(1)}, f32[512]{0:T(512)}, u32[]{:S(2)}) copy-start(f32[512]{0:T(512)} %param.28) | copy-start | bytes 6148
